TPU v7x, 256 devices: a whole 4x4x8 slice. The times are simulated.
256 devices in a mesh: req: 64 (over z, y, core), tp: 4 (over x).
Axes of the slice: x: 4, y: 4, z: 8, core: 2. Of those that a mesh axis runs over, the one named last changes fastest.
Arguments:
- hidden_in: bfloat16 [8192, 2048], P('req'), may hold values from -6 to 6
- attn_gain: float32 [2048], replicated, may hold values from 0.1 to 1.9
- w_query: bfloat16 [2048, 3072], P(None, 'tp'), may hold values from -0.125 to 0.125
- w_latent: bfloat16 [2048, 576], P(None, 'tp'), may hold values from -0.125 to 0.125
- kv_gain: float32 [512], replicated, may hold values from 0.1 to 1.9
- w_key_up: bfloat16 [512, 2048], P(None, 'tp'), may hold values from -0.25 to 0.25
- w_value_up: bfloat16 [512, 2048], P(None, 'tp'), may hold values from -0.25 to 0.25
- w_out: bfloat16 [2048, 2048], P('tp'), may hold values from -0.125 to 0.125
- moe_gain: float32 [2048], replicated, may hold values from 0.1 to 1.9
- w_gate: bfloat16 [64, 2048, 1408], P('req', None, 'tp'), may hold values from -0.125 to 0.125
- w_up: bfloat16 [64, 2048, 1408], P('req', None, 'tp'), may hold values from -0.125 to 0.125
- w_down: bfloat16 [64, 1408, 2048], P('req', 'tp'), may hold values from -0.15625 to 0.15625
- latent_cache: bfloat16 [2048, 64, 576], P('req'), may hold values from -3000 to 3000
- page_table: int32 [256, 8], P('req'), may hold values from 0 to 7, as said below
- cache_len: int32 [256], P('req'), may hold values from 1 to 512, 65536 in all
- parents: int32 [256, 3, 8], P('req'), may hold values from 0 to 7
- routes: int32 [8192, 6], P('req'), may hold values from 0 to 63, all different within a row; in each aligned block of 128 rows (0 to 127, 128 to 255, ...) at most 24 rows name the same one
- route_weights: float32 [8192, 6], P('req'), may hold values from 0.1 to 1
Outputs:
- layer_out: bfloat16 [8192, 2048], P('req', 'tp')
Inputs may be any that keep to these rules, and one draw needn't show every extreme that they name: `page_table`: each request's row lists the 8 pages of that request's block of the pool, each once. `routes`: each row names 6 different experts; in the rows of one index of req no expert is named more than 24 times, a bound that some block reaches.
All inputs are finite; a program needn't handle non-finite values. No bound on the sum of `cache_len` on one device may be relied on, other than what follows from the above.
Results may differ from a plain program's by a relative error of at most 0.015.
The roundings to bfloat16 on the way count: a program that leaves them out, or rounds other values in their place, can miss the bound.
Values may be sent and summed in bfloat16 or wider, within the bound.
No kernel may reach another device: no remote copies, remote signals or barrier semaphores. Data moves between devices by JAX's collectives and lax.ppermute only.
A program may use at most 128 MiB of HBM per device.

v0:
```python
import jax
import jax.numpy as jnp
from jax import lax
from jax.sharding import PartitionSpec as P

D = 2048
NOPE = 128
ROPE = 64
VDIM = 128
LATENT = 512
TOPK = 6
EXP_DEV = 1
BEAMS = 8
STEPS = 4
PAGE = 64
PAGES = 8


eps = 1e-06
rope_base = 50000.0


def rms_scale(values):
    return lax.rsqrt(jnp.mean(values * values, axis=-1, keepdims=True) + eps)


def rotate(values, cos_val, sin_val):
    half_rope = values.shape[-1] // 2
    first = values[..., :half_rope]
    second = values[..., half_rope:]
    return jnp.concatenate(
        [first * cos_val - second * sin_val, second * cos_val + first * sin_val], axis=-1
    )


def expert_math(arrived, gate_w, up_w, down_w):
    gate_val = jnp.einsum("nesd,edf->nesf", arrived, gate_w, preferred_element_type=jnp.float32)
    up_val = jnp.einsum("nesd,edf->nesf", arrived, up_w, preferred_element_type=jnp.float32)
    active = (jax.nn.silu(gate_val) * up_val).astype(jnp.bfloat16)
    return jnp.einsum("nesf,efd->nesd", active, down_w, preferred_element_type=jnp.float32)


def send_home(shares):
    return lax.all_to_all(shares, "req", split_axis=0, concat_axis=0, tiled=True)


def local(
    hidden_in,
    attn_gain,
    w_query,
    w_latent,
    kv_gain,
    w_key_up,
    w_value_up,
    w_out,
    moe_gain,
    w_gate,
    w_up,
    w_down,
    latent_cache,
    page_table,
    cache_len,
    parents,
    routes,
    route_weights,
):
    highest = lax.Precision.HIGHEST
    row_count = hidden_in.shape[0]
    req_local = cache_len.shape[0]
    heads_local = w_value_up.shape[1] // VDIM
    tp_count = lax.axis_size("tp")
    req_count = lax.axis_size("req")
    col_share = D // tp_count
    max_len = PAGES * PAGE
    hidden_f = hidden_in.astype(jnp.float32)
    normed = (hidden_f * rms_scale(hidden_f) * attn_gain).astype(jnp.bfloat16)
    positions = (
        cache_len.astype(jnp.float32)[:, None, None]
        + jnp.arange(STEPS, dtype=jnp.float32)[None, :, None]
        + jnp.zeros((1, 1, BEAMS), jnp.float32)
    ).reshape(row_count)
    frequency = rope_base ** (-2.0 * jnp.arange(ROPE // 2, dtype=jnp.float32) / ROPE)
    angles = positions[:, None] * frequency[None, :]
    cos_val = jnp.cos(angles)
    sin_val = jnp.sin(angles)
    queries = jnp.dot(normed, w_query, preferred_element_type=jnp.float32).reshape(
        row_count, heads_local, NOPE + ROPE
    )
    q_nope = queries[:, :, :NOPE].astype(jnp.bfloat16)
    q_rope = rotate(queries[:, :, NOPE:], cos_val[:, None, :], sin_val[:, None, :]).astype(
        jnp.bfloat16
    )
    kv_part = jnp.dot(normed, w_latent, preferred_element_type=jnp.float32)
    kv_all = lax.all_gather(kv_part, "tp", axis=1, tiled=True)
    new_lat = kv_all[:, :LATENT] * rms_scale(kv_all[:, :LATENT]) * kv_gain
    new_rope = rotate(kv_all[:, LATENT:], cos_val, sin_val)
    new_keys = jnp.concatenate([new_lat, new_rope], axis=1).astype(jnp.bfloat16)
    key_up = w_key_up.reshape(LATENT, heads_local, NOPE)
    q_lat = jnp.einsum("nhc,lhc->nhl", q_nope, key_up, preferred_element_type=jnp.float32).astype(
        jnp.bfloat16
    )
    query_key = jnp.concatenate([q_lat, q_rope], axis=2)
    pool_index = (jnp.arange(req_local, dtype=jnp.int32) * PAGES)[:, None] + page_table
    cache_keys = jnp.take(latent_cache, pool_index.reshape(-1), axis=0).reshape(
        req_local, max_len, LATENT + ROPE
    )
    live_mask = jnp.arange(max_len, dtype=jnp.int32)[None, :] < cache_len[:, None]
    score_scale = (NOPE + ROPE) ** (-0.5)
    grouped = query_key.reshape(req_local, STEPS * BEAMS * heads_local, LATENT + ROPE)
    s_cache = (
        jnp.einsum("rqd,rld->rql", grouped, cache_keys, preferred_element_type=jnp.float32)
        * score_scale
    )
    s_cache = jnp.where(live_mask[:, None, :], s_cache, -jnp.inf).reshape(
        req_local, STEPS, BEAMS, heads_local, max_len
    )
    fresh = new_keys.reshape(req_local, STEPS, BEAMS, LATENT + ROPE).astype(jnp.float32)
    parent_hot = (parents[..., None] == jnp.arange(BEAMS, dtype=jnp.int32)).astype(jnp.float32)
    identity = jnp.broadcast_to(jnp.eye(BEAMS, dtype=jnp.float32), (req_local, BEAMS, BEAMS))
    tail_rows = []
    for step_index in range(STEPS):
        lineage = identity
        pieces = [None] * STEPS
        for earlier in range(step_index, -1, -1):
            pieces[earlier] = jnp.einsum(
                "rba,rad->rbd", lineage, fresh[:, earlier], precision=highest
            )
            if earlier > 0:
                lineage = jnp.einsum(
                    "rba,rac->rbc", lineage, parent_hot[:, earlier - 1], precision=highest
                )
        for later in range(step_index + 1, STEPS):
            pieces[later] = jnp.zeros_like(pieces[0])
        tail_rows.append(jnp.stack(pieces, axis=2))
    tail_keys = jnp.stack(tail_rows, axis=1).astype(jnp.bfloat16)
    queries_tail = query_key.reshape(req_local, STEPS, BEAMS, heads_local, LATENT + ROPE)
    s_tail = (
        jnp.einsum(
            "rsbhd,rsbjd->rsbhj", queries_tail, tail_keys, preferred_element_type=jnp.float32
        )
        * score_scale
    )
    causal = jnp.arange(STEPS)[None, :] <= jnp.arange(STEPS)[:, None]
    s_tail = jnp.where(causal[None, :, None, None, :], s_tail, -jnp.inf)
    top_score = jnp.maximum(jnp.max(s_cache, axis=-1), jnp.max(s_tail, axis=-1))
    e_cache = jnp.exp(s_cache - top_score[..., None])
    e_tail = jnp.exp(s_tail - top_score[..., None])
    total = jnp.sum(e_cache, axis=-1) + jnp.sum(e_tail, axis=-1)
    p_cache = (e_cache / total[..., None]).astype(jnp.bfloat16)
    p_tail = (e_tail / total[..., None]).astype(jnp.bfloat16)
    context = jnp.einsum(
        "rsbhl,rld->rsbhd", p_cache, cache_keys[..., :LATENT], preferred_element_type=jnp.float32
    )
    context = context + jnp.einsum(
        "rsbhj,rsbjd->rsbhd", p_tail, tail_keys[..., :LATENT], preferred_element_type=jnp.float32
    )
    context = context.astype(jnp.bfloat16).reshape(row_count, heads_local, LATENT)
    value_up = w_value_up.reshape(LATENT, heads_local, VDIM)
    head_out = (
        jnp.einsum("nhl,lhv->nhv", context, value_up, preferred_element_type=jnp.float32)
        .astype(jnp.bfloat16)
        .reshape(row_count, heads_local * VDIM)
    )
    attn_part = jnp.dot(head_out, w_out, preferred_element_type=jnp.float32)
    expert_count = EXP_DEV * req_count
    capacity = min(row_count, 2 * row_count * TOPK // expert_count)
    slot_count = expert_count * capacity
    picks = routes.reshape(-1)
    pick_hot = (picks[:, None] == jnp.arange(expert_count, dtype=jnp.int32)[None, :]).astype(
        jnp.int32
    )
    before = jnp.cumsum(pick_hot, axis=0) - pick_hot
    ranks = jnp.sum(before * pick_hot, axis=1)
    slot_of = picks * capacity + ranks
    slot_hot = (slot_of[:, None] == jnp.arange(slot_count, dtype=jnp.int32)[None, :]).reshape(
        row_count, TOPK, slot_count
    )
    gather_rows = jnp.sum(slot_hot.astype(jnp.int32), axis=1).astype(jnp.bfloat16)
    weight_rows = jnp.sum(jnp.where(slot_hot, route_weights[:, :, None], 0.0), axis=1)
    tp_index = lax.axis_index("tp")
    col_start = tp_index * col_share
    attn_full = lax.psum(attn_part, "tp")
    resid_full = hidden_f + attn_full
    moe_in = (resid_full * rms_scale(resid_full) * moe_gain).astype(jnp.bfloat16)
    placed = jnp.dot(gather_rows.T, moe_in, preferred_element_type=jnp.float32).astype(jnp.bfloat16)
    partial_out = expert_math(
        lax.all_to_all(
            placed.reshape(req_count, EXP_DEV, capacity, moe_in.shape[1]),
            "req",
            split_axis=0,
            concat_axis=0,
            tiled=True,
        ),
        w_gate,
        w_up,
        w_down,
    )
    shares = lax.psum_scatter(partial_out, "tp", scatter_dimension=3, tiled=True)
    returned = send_home(shares.astype(jnp.bfloat16))
    resid_cols = lax.dynamic_slice_in_dim(resid_full, col_start, col_share, 1)
    combined = jnp.dot(
        weight_rows, returned.reshape(slot_count, col_share).astype(jnp.float32), precision=highest
    )
    return (resid_cols + combined).astype(jnp.bfloat16)


def solution(mesh):
    in_specs = (
        P("req", None),
        P(),
        P(None, "tp"),
        P(None, "tp"),
        P(),
        P(None, "tp"),
        P(None, "tp"),
        P("tp", None),
        P(),
        P("req", None, "tp"),
        P("req", None, "tp"),
        P("req", "tp", None),
        P("req", None, None),
        P("req", None),
        P("req"),
        P("req", None, None),
        P("req", None),
        P("req", None),
    )
    out_specs = P("req", "tp")
    return jax.shard_map(local, mesh=mesh, in_specs=in_specs, out_specs=out_specs, check_vma=False)
```

profile of v0, /device:TPU:1, one launch (start us, length us, event | category | flops | bytes accessed | tf_op | source)
XLA Modules:
  0.0 477.5 jit_solution(17207747423116017685)
XLA Ops:
  6.5 0.6 multiply_power_fusion
  7.1 0.8 iota_compare_fusion.3
  8.2 1.2 fusion.40
  9.5 1.6 fusion.63
  11.1 11.2 %all_gather.3 = f32[128,576]{0,1:T(8,128)S(1)} all-gather(f32[128,144]{0,1:T(8,128)S(1)} %fusion.63), channel_id=1, replica_groups=mesh['req'=64,'tp'=4] {'tp'}, dimensions={1}, use_global_device_ids=true | all-gather | bytes 368640 | tf_op jit(solution)/shard_map/all_gather | solution.py:94
  22.4 0.8 multiply_convert_fusion.2
  23.2 1.6 copy.150
  25.1 0.8 multiply_cosine_fusion
  26.1 0.1 fusion.70
  26.3 0.1 fusion.72
  26.4 1.0 pad_maximum_fusion.2
  27.4 0.8 fusion.37
  28.3 0.8 fusion.34
  29.1 0.8 fusion.38
  30.1 0.8 fusion.30
  30.9 0.8 fusion.32
  31.6 0.8 fusion.35
  32.4 0.8 fusion.39
  33.2 0.5 iota_compare_fusion.6
  33.7 0.5 iota_multiply_fusion
  34.2 0.7 iota_compare_fusion.4
  35.0 0.8 fusion.36
  35.8 0.8 fusion.33
  36.6 0.8 fusion.31
  37.3 0.7 copy.144
  38.0 0.7 copy.146
  38.8 2.4 fusion.65
  41.5 1.4 fusion.22
  42.9 0.9 subtract_convert_fusion
  44.0 0.5 copy.147
  44.5 1.2 reshape.300
  46.0 4.1 gather_fusion
  50.1 2.1 bitcast_select_fusion
  52.3 2.0 fusion.86
  54.5 0.9 maximum_bitcast_fusion
  55.6 3.1 fusion.87
  58.9 0.2 copy.158
  59.0 1.2 fusion.58
  60.2 2.6 reshape.302
  62.8 1.5 exponential_reduce_fusion
  64.5 0.2 copy.160
  64.6 1.7 fusion.51
  66.3 0.9 fusion.21
  67.3 1.4 copy.179
  68.7 0.3 convolution_convert_fusion.2
  69.1 1.5 fusion.88
  70.6 0.2 reduce-scatter.2.cloned.1.call-start
  71.2 1.8 reduce-window.6
  73.0 0.3 slice_reduce_fusion
  73.3 0.1 fusion.61
  73.7 0.7 convert_reduce_fusion
  74.4 50.8 %all-reduce.2.cloned.1.call-done = f32[128,2048]{1,0:T(8,128)} async-done(((f32[128,2048]{1,0:T(8,128)}), f32[128,2048]{1,0:T(8,128)}) %all-reduce.2.cloned.1.call-update) | async-done | bytes 1048592 | tf_op jit(solution)/shard_map/psum | solution.py:182
  125.1 1.4 multiply_reduce_fusion
  126.6 1.9 convolution_convert_fusion
  128.5 151.6 %all_to_all.10 = bf16[64,1,24,2048]{3,2,1,0:T(8,128)(2,1)S(1)} all-to-all(bf16[64,1,24,2048]{3,2,1,0:T(8,128)(2,1)S(1)} %bitcast.216), channel_id=1, replica_groups=mesh['req'=64,'tp'=4] {'req'}, dimensions={0} | all-to-all | bytes 12582912 | tf_op jit(solution)/shard_map/all_to_all | solution.py:187
  280.1 2.6 copy-done.2
  282.6 5.0 %fusion.2 = f32[64,24,352]{2,1,0:T(8,128)} fusion(bf16[64,1,24,2048]{3,2,1,0:T(8,128)(2,1)S(1)} %all_to_all.10, bf16[1,2048,352]{1,2,0:T(8,128)(2,1)S(1)} %copy-done.25), kind=kOutput, calls=%fused_computation.4 | convolution fusion | flops 2214592512 | bytes 9895936 | tf_op jit(solution)/shard_map/nesd,edf->nesf/dot_general | solution.py:37
  287.7 12.3 %convolution_bitcast_fusion = f32[64,1,24,2048]{3,2,0,1:T(8,128)} fusion(bf16[1,352,2048]{2,1,0:T(8,128)(2,1)S(1)} %copy-done.26, bf16[1,2048,352]{1,2,0:T(8,128)(2,1)} %param.28, bf16[64,1,24,2048]{3,2,1,0:T(8,128)(2,1)} %copy-done.2, f32[64,24,352]{2,1,0:T(8,128)} %fusion.2), kind=kOutput, calls=%fused_computation.6 | convolution fusion | flops 4432429056 | bytes 23920640 | tf_op jit(solution)/shard_map/nesf,efd->nesd/dot_general | solution.py:40
  300.0 114.4 %reduce-scatter.2.cloned.1.call-done = f32[64,1,24,512]{3,2,0,1:T(8,128)} async-done(((f32[64,1,24,2048]{3,2,0,1:T(8,128)}), f32[64,1,24,512]{3,2,0,1:T(8,128)}) %reduce-scatter.2.cloned.1.call-update) | async-done | bytes 3145744 | tf_op jit(solution)/shard_map/reduce_scatter | solution.py:198
  414.4 3.2 convert_bitcast_fusion
  417.7 10.9 %all-to-all-start.1 = ((bf16[64,1,24,512]{3,2,1,0:T(8,128)(2,1)}), bf16[64,1,24,512]{3,2,1,0:T(8,128)(2,1)}, u32[]{:S(2)}, u32[]{:S(2)}) async-start(bf16[64,1,24,512]{3,2,1,0:T(8,128)(2,1)} %convert_bitcast_fusion), calls=%async_computation.2 | async-start | bytes 3145728 | tf_op jit(solution)/shard_map/all_to_all | solution.py:44
  428.6 1.5 select_reduce_fusion
  430.2 37.4 %all-to-all-done.1 = bf16[64,1,24,512]{3,2,1,0:T(8,128)(2,1)} async-done(((bf16[64,1,24,512]{3,2,1,0:T(8,128)(2,1)}), bf16[64,1,24,512]{3,2,1,0:T(8,128)(2,1)}, u32[]{:S(2)}, u32[]{:S(2)}) %all-to-all-start.1) | async-done | bytes 1572896 | tf_op jit(solution)/shard_map/all_to_all | solution.py:44
  467.6 3.1 fusion.29
  (104 shorter events, 3.2 us)
Async XLA Ops:
  6.5 32.2 %copy-start = (bf16[2048,768]{1,0:T(8,128)(2,1)S(1)}, bf16[2048,768]{1,0:T(8,128)(2,1)}, u32[]{:S(2)}) copy-start(bf16[2048,768]{1,0:T(8,128)(2,1)} %param.20) | copy-start | bytes 9437188
  6.5 15.8 %copy-start.21 = (f32[512]{0:T(512)S(1)}, f32[512]{0:T(512)}, u32[]{:S(2)}) copy-start(f32[512]{0:T(512)} %param.22) | copy-start | bytes 6148
  6.5 18.3 %copy-start.23 = (s32[4]{0:T(128)S(1)}, s32[4]{0:T(128)}, u32[]{:S(2)}) copy-start(s32[4]{0:T(128)} %param.32) | copy-start | bytes 52
  6.5 118.6 %all-reduce.2.cloned.1.call-start = ((), (), s32[]{:S(2)}) async-start(), calls=%async_computation.3 | async-start | bytes 2097152 | tf_op jit(solution)/shard_map/psum | solution.py:182
  9.5 29.3 %copy-start.18 = (f32[2048]{0:T(1024)S(1)}, f32[2048]{0:T(1024)}, u32[]{:S(2)}) copy-start(f32[2048]{0:T(1024)} %param.19) | copy-start | bytes 24580
  42.9 2.8 copy-start.22
  42.9 2.8 copy-start.24
  44.0 6.1 %copy-start.6 = (bf16[128,4,576]{2,0,1:T(8,128)(2,1)}, bf16[128,4,576]{2,0,1:T(8,128)(2,1)S(1)}, u32[]{:S(2)}) copy-start(bf16[128,4,576]{2,0,1:T(8,128)(2,1)S(1)} %pad_maximum_fusion) | copy-start | bytes 1769476
  50.1 2.1 copy-start.5
  52.2 2.3 copy-start.10
  52.2 2.3 copy-start.11
  52.2 2.3 copy-start.12
  52.2 2.3 copy-start.13
  52.2 2.3 copy-start.14
  52.2 2.3 copy-start.15
  52.3 2.3 copy-start.16
  54.3 1.4 copy-start.27
  55.6 3.1 copy-start.7
  58.7 5.9 %slice-start = ((bf16[4,4,8,4,576]{4,2,0,3,1:T(8,128)(2,1)}), bf16[4,4,8,4,512]{4,2,0,3,1:T(8,128)(2,1)S(1)}, s32[]{:S(2)}) async-start(bf16[4,4,8,4,576]{4,2,0,3,1:T(8,128)(2,1)} %copy-done.7), calls=%async_computation.5 | async-start | bytes 1048576 | tf_op jit(solution)/shard_map/slice | solution.py:155
  64.6 1.7 copy-start.9
  67.3 1.8 copy-start.8
  69.0 1.8 copy-start.17
  70.5 54.6 %copy-start.4 = (bf16[128,2048]{1,0:T(8,128)(2,1)S(1)}, bf16[128,2048]{1,0:T(8,128)(2,1)}, u32[]{:S(2)}) copy-start(bf16[128,2048]{1,0:T(8,128)(2,1)} %param.18) | copy-start | bytes 1572868
  70.6 343.9 %reduce-scatter.2.cloned.1.call-start = ((), (), s32[]{:S(2)}) async-start(), calls=%async_computation.4 | async-start | bytes 15728640 | tf_op jit(solution)/shard_map/reduce_scatter | solution.py:198
  70.9 55.7 %copy-start.19 = (f32[2048]{0:T(1024)S(1)}, f32[2048]{0:T(1024)}, u32[]{:S(2)}) copy-start(f32[2048]{0:T(1024)} %param.26) | copy-start | bytes 24580
  126.6 1.9 copy-start.3
  128.5 154.2 %copy-start.25 = (bf16[1,2048,352]{1,2,0:T(8,128)(2,1)S(1)}, bf16[1,2048,352]{1,2,0:T(8,128)(2,1)}, u32[]{:S(2)}) copy-start(bf16[1,2048,352]{1,2,0:T(8,128)(2,1)} %param.27) | copy-start | bytes 4325380
  280.1 2.6 copy-start.2
  282.6 5.0 %copy-start.26 = (bf16[1,352,2048]{2,1,0:T(8,128)(2,1)S(1)}, bf16[1,352,2048]{2,1,0:T(8,128)(2,1)}, u32[]{:S(2)}) copy-start(bf16[1,352,2048]{2,1,0:T(8,128)(2,1)} %param.29) | copy-start | bytes 4325380
  417.7 11.0 %copy-start.20 = (f32[128,6]{0,1:T(8,128)S(1)}, f32[128,6]{0,1:T(8,128)}, u32[]{:S(2)}) copy-start(f32[128,6]{0,1:T(8,128)} %param.35) | copy-start | bytes 9220
  417.7 49.9 %all-to-all-start.1 = ((bf16[64,1,24,512]{3,2,1,0:T(8,128)(2,1)}), bf16[64,1,24,512]{3,2,1,0:T(8,128)(2,1)}, u32[]{:S(2)}, u32[]{:S(2)}) async-start(bf16[64,1,24,512]{3,2,1,0:T(8,128)(2,1)} %convert_bitcast_fusion), calls=%async_computation.2 | async-start | bytes 3145728 | tf_op jit(solution)/shard_map/all_to_all | solution.py:44
  428.6 42.1 %copy-start.1 = (bf16[2048,768]{1,0:T(8,128)(2,1)S(1)}, bf16[2048,768]{1,0:T(8,128)(2,1)}, u32[]{:S(2)}) copy-start(bf16[2048,768]{1,0:T(8,128)(2,1)} %param.20) | copy-start | bytes 9437188
Sparse Core Ops, SparseCore 0:
  70.7 54.3 all-reduce.1
  300.1 114.2 reduce-scatter.1
where the time goes:
time: 478 us
  waiting for transfers between devices  203 us (42%)
  blocking collectives  163 us (34%)
  matrix products  45.9 us (10%)
  other arithmetic  23 us (5%)
  local copies, waits for them, and re-layouts  18.1 us (4%)
  between operations  14 us (3%)
  starting transfers between devices  11.2 us (2%)
    all_to_all x1, blocking collectives, local(): lax.all_to_all(placed.reshape(req_count, EXP_DEV, capacity, moe_in.shape[...  152 us
    reduce_scatter x1, waiting for transfers between devices, local(): lax.psum_scatter(partial_out, 'tp', scatter_dimension=3, tiled=True)  114 us
    psum x1, waiting for transfers between devices, local(): attn_full = lax.psum(attn_part, 'tp')  50.8 us
    all_to_all x1, waiting for transfers between devices, send_home(): lax.all_to_all(shares, 'req', split_axis=0, concat_axis=0, tiled=True)  37.4 us
    dot_general x1, matrix products, expert_math(): jnp.einsum('nesf,efd->nesd', active, down_w, preferred_element_type=jnp.f...  12.3 us
    all_gather x1, blocking collectives, local(): kv_all = lax.all_gather(kv_part, 'tp', axis=1, tiled=True)  11.2 us
    all_to_all x1, starting transfers between devices, send_home(): lax.all_to_all(shares, 'req', split_axis=0, concat_axis=0, tiled=True)  10.9 us
  transfers between devices with their start and end apart: 3, of which 3 were waited for; matrix products, arithmetic and copies ran while one was open for 1% of the time, Pallas kernels for 0%

commit v1 on v0

--- a/solution.py
+++ b/solution.py
@@ -179,25 +179,27 @@
     weight_rows = jnp.sum(jnp.where(slot_hot, route_weights[:, :, None], 0.0), axis=1)
     tp_index = lax.axis_index("tp")
     col_start = tp_index * col_share
-    attn_full = lax.psum(attn_part, "tp")
-    resid_full = hidden_f + attn_full
-    moe_in = (resid_full * rms_scale(resid_full) * moe_gain).astype(jnp.bfloat16)
-    placed = jnp.dot(gather_rows.T, moe_in, preferred_element_type=jnp.float32).astype(jnp.bfloat16)
-    partial_out = expert_math(
-        lax.all_to_all(
-            placed.reshape(req_count, EXP_DEV, capacity, moe_in.shape[1]),
-            "req",
-            split_axis=0,
-            concat_axis=0,
-            tiled=True,
-        ),
-        w_gate,
-        w_up,
-        w_down,
-    )
+    attn_cols = lax.psum_scatter(attn_part, "tp", scatter_dimension=1, tiled=True)
+    hidden_cols = lax.dynamic_slice_in_dim(hidden_f, col_start, col_share, 1)
+    resid_cols = hidden_cols + attn_cols
+    square_sum = lax.psum(jnp.sum(resid_cols * resid_cols, axis=-1, keepdims=True), "tp")
+    moe_scale = lax.rsqrt(square_sum / D + eps)
+    gain_cols = lax.dynamic_slice_in_dim(moe_gain, col_start, col_share, 0)
+    moe_in_cols = (resid_cols * moe_scale * gain_cols).astype(jnp.bfloat16)
+    placed = jnp.dot(gather_rows.T, moe_in_cols, preferred_element_type=jnp.float32).astype(
+        jnp.bfloat16
+    )
+    arrived_cols = lax.all_to_all(
+        placed.reshape(req_count, EXP_DEV, capacity, col_share),
+        "req",
+        split_axis=0,
+        concat_axis=0,
+        tiled=True,
+    )
+    arrived = lax.all_gather(arrived_cols, "tp", axis=3, tiled=True)
+    partial_out = expert_math(arrived, w_gate, w_up, w_down)
     shares = lax.psum_scatter(partial_out, "tp", scatter_dimension=3, tiled=True)
     returned = send_home(shares.astype(jnp.bfloat16))
-    resid_cols = lax.dynamic_slice_in_dim(resid_full, col_start, col_share, 1)
     combined = jnp.dot(
         weight_rows, returned.reshape(slot_count, col_share).astype(jnp.float32), precision=highest
     )

time: 478 us -> 427 us (0.89)
  blocking collectives: 163 us -> 70.8 us
  waiting for transfers between devices: 203 us -> 244 us
    all_to_all x1, blocking collectives: 152 us -> 53.2 us  [local(): lax.all_to_all(placed.reshape(req_count, EXP_DEV, capacity, col_share), '...]
    all_gather x0 -> x1, waiting for transfers between devices: none -> 63.6 us  [local(): arrived = lax.all_gather(arrived_cols, 'tp', axis=3, tiled=True)]
    psum x1 -> x0, waiting for transfers between devices: 50.8 us -> none  [local(): attn_full = lax.psum(attn_part, 'tp')]
    reduce_scatter x0 -> x1, waiting for transfers between devices: none -> 25 us  [local(): lax.psum_scatter(attn_part, 'tp', scatter_dimension=1, tiled=True)]
    psum x0 -> x1, blocking collectives: none -> 6.39 us  [local(): lax.psum(jnp.sum(resid_cols * resid_cols, axis=-1, keepdims=True), 'tp')]
  transfers between devices with their start and end apart: 3 -> 4, of which waited for: 3 -> 4; matrix products, arithmetic and copies ran while one was open for 1% -> 1% of each run, Pallas kernels for 0% -> 0%
where the time goes in v1:
time: 427 us; the launch traced here: 426 us
  waiting for transfers between devices  244 us (57%)
  blocking collectives  70.8 us (17%)
  matrix products  47.3 us (11%)
  other arithmetic  22.7 us (5%)
  local copies, waits for them, and re-layouts  16.3 us (4%)
  between operations  13.7 us (3%)
  starting transfers between devices  11.2 us (3%)
    reduce_scatter x1, waiting for transfers between devices, local(): lax.psum_scatter(partial_out, 'tp', scatter_dimension=3, tiled=True)  118 us
    all_gather x1, waiting for transfers between devices, local(): arrived = lax.all_gather(arrived_cols, 'tp', axis=3, tiled=True)  63.6 us
    all_to_all x1, blocking collectives, local(): lax.all_to_all(placed.reshape(req_count, EXP_DEV, capacity, col_share), '...  53.2 us
    all_to_all x1, waiting for transfers between devices, send_home(): lax.all_to_all(shares, 'req', split_axis=0, concat_axis=0, tiled=True)  37.4 us
    reduce_scatter x1, waiting for transfers between devices, local(): lax.psum_scatter(attn_part, 'tp', scatter_dimension=1, tiled=True)  25 us
    dot_general x1, matrix products, expert_math(): jnp.einsum('nesf,efd->nesd', active, down_w, preferred_element_type=jnp.f...  12.3 us
    all_gather x1, blocking collectives, local(): kv_all = lax.all_gather(kv_part, 'tp', axis=1, tiled=True)  11.2 us
    all_to_all x1, starting transfers between devices, send_home(): lax.all_to_all(shares, 'req', split_axis=0, concat_axis=0, tiled=True)  10.9 us
  transfers between devices with their start and end apart: 4, of which 4 were waited for; matrix products, arithmetic and copies ran while one was open for 1% of the time, Pallas kernels for 0%

profile of v1, /device:TPU:1, one launch (start us, length us, event | category | flops | bytes accessed | tf_op | source)
XLA Modules:
  0.0 425.9 jit_solution(5263665199859982133)
XLA Ops:
  6.5 0.5 multiply_power_fusion
  7.1 0.8 iota_compare_fusion.3
  8.1 1.2 multiply_reduce_fusion
  9.4 1.6 fusion.58
  11.0 11.2 %all_gather.6 = f32[128,576]{0,1:T(8,128)S(1)} all-gather(f32[128,144]{0,1:T(8,128)S(1)} %fusion.58), channel_id=1, replica_groups=mesh['req'=64,'tp'=4] {'tp'}, dimensions={1}, use_global_device_ids=true | all-gather | bytes 368640 | tf_op jit(solution)/shard_map/all_gather | solution.py:94
  22.3 0.8 multiply_convert_fusion.2
  23.1 1.6 copy.152
  25.0 0.7 multiply_cosine_fusion
  26.1 0.1 fusion.67
  26.3 1.0 pad_maximum_fusion.2
  27.3 0.8 fusion.37
  28.2 0.8 fusion.34
  29.0 0.8 fusion.38
  29.9 0.8 fusion.30
  30.7 0.8 fusion.32
  31.5 0.8 fusion.35
  32.3 0.8 fusion.39
  33.1 0.6 iota_compare_fusion.6
  33.6 0.5 iota_multiply_fusion
  34.2 0.7 iota_compare_fusion.4
  34.9 0.8 fusion.36
  35.7 0.8 fusion.33
  36.5 0.8 fusion.31
  37.3 0.7 copy.146
  38.0 0.7 copy.148
  38.7 2.4 fusion.59
  41.4 1.4 fusion.22
  42.9 0.9 subtract_convert_fusion
  43.9 0.5 copy.149
  44.5 1.2 reshape.292
  46.0 4.1 gather_fusion
  50.1 2.1 bitcast_select_fusion
  52.2 2.0 fusion.81
  54.5 0.9 maximum_bitcast_fusion
  55.6 3.1 fusion.82
  58.8 0.2 copy.160
  59.0 1.2 fusion.53
  60.2 2.6 reshape.294
  62.7 1.5 exponential_reduce_fusion
  64.4 0.2 copy.162
  64.6 1.7 fusion.48
  66.3 0.9 fusion.21
  67.3 1.4 copy.182
  68.7 0.3 convolution_convert_fusion.2
  69.0 1.5 fusion.83
  70.5 0.2 all-gather.2.cloned.1.call-start
  71.3 1.8 reduce-window.6
  73.1 0.3 slice_reduce_fusion
  73.7 0.8 dynamic_slice.7
  74.5 0.6 convert_reduce_fusion
  75.2 25.0 %reduce-scatter.3.cloned.1.call-done = f32[128,512]{1,0:T(8,128)} async-done(((f32[128,2048]{1,0:T(8,128)}), f32[128,512]{1,0:T(8,128)}) %reduce-scatter.3.cloned.1.call-update) | async-done | bytes 262160 | tf_op jit(solution)/shard_map/reduce_scatter | solution.py:182
  100.2 1.1 multiply_reduce_fusion.1
  101.3 6.4 %psum.7 = f32[128,1]{0,1:T(1,128)S(1)} all-reduce(f32[128,1]{0,1:T(1,128)S(1)} %bitcast.233), channel_id=1, replica_groups=mesh['req'=64,'tp'=4] {'tp'}, use_global_device_ids=true, to_apply=%region_13.14 | all-reduce | flops 128 | bytes 1024 | tf_op jit(solution)/shard_map/psum | solution.py:185
  107.7 0.6 convolution_convert_fusion
  108.3 53.2 %all_to_all.10 = bf16[64,1,24,512]{3,2,1,0:T(8,128)(2,1)} all-to-all(bf16[64,1,24,512]{3,2,1,0:T(8,128)(2,1)S(1)} %bitcast.222), channel_id=1, replica_groups=mesh['req'=64,'tp'=4] {'req'}, dimensions={0} | all-to-all | bytes 3145728 | tf_op jit(solution)/shard_map/all_to_all | solution.py:192
  161.6 63.6 %all-gather.2.cloned.1.call-done = bf16[64,1,24,2048]{3,2,0,1:T(8,128)(2,1)} async-done(((bf16[64,1,24,512]{3,2,0,1:T(8,128)(2,1)}), bf16[64,1,24,2048]{3,2,0,1:T(8,128)(2,1)}) %all-gather.2.cloned.1.call-update) | async-done | bytes 6291472 | tf_op jit(solution)/shard_map/all_gather | solution.py:199
  225.2 7.6 %fusion.2 = f32[64,24,352]{2,1,0:T(8,128)} fusion(bf16[64,1,24,2048]{3,2,0,1:T(8,128)(2,1)} %all-gather.2.cloned.1.call-done, bf16[1,2048,352]{1,2,0:T(8,128)(2,1)S(1)} %copy-done.22), kind=kOutput, calls=%fused_computation.3 | convolution fusion | flops 2214592512 | bytes 9895936 | tf_op jit(solution)/shard_map/nesd,edf->nesf/dot_general | solution.py:37
  232.9 12.3 %convolution_bitcast_fusion = f32[64,1,24,2048]{3,2,0,1:T(8,128)} fusion(bf16[1,352,2048]{2,1,0:T(8,128)(2,1)S(1)} %copy-done.23, bf16[1,2048,352]{1,2,0:T(8,128)(2,1)} %param.28, bf16[64,1,24,2048]{3,2,0,1:T(8,128)(2,1)} %all-gather.2.cloned.1.call-done, f32[64,24,352]{2,1,0:T(8,128)} %fusion.2), kind=kOutput, calls=%fused_computation.5 | convolution fusion | flops 4432429056 | bytes 23920640 | tf_op jit(solution)/shard_map/nesf,efd->nesd/dot_general | solution.py:40
  245.2 118.0 %reduce-scatter.5.cloned.1.call-done = f32[64,1,24,512]{3,2,0,1:T(8,128)} async-done(((f32[64,1,24,2048]{3,2,0,1:T(8,128)}), f32[64,1,24,512]{3,2,0,1:T(8,128)}) %reduce-scatter.5.cloned.1.call-update) | async-done | bytes 3145744 | tf_op jit(solution)/shard_map/reduce_scatter | solution.py:201
  363.1 3.2 convert_bitcast_fusion
  366.4 10.9 %all-to-all-start.1 = ((bf16[64,1,24,512]{3,2,1,0:T(8,128)(2,1)}), bf16[64,1,24,512]{3,2,1,0:T(8,128)(2,1)}, u32[]{:S(2)}, u32[]{:S(2)}) async-start(bf16[64,1,24,512]{3,2,1,0:T(8,128)(2,1)} %convert_bitcast_fusion), calls=%async_computation.3 | async-start | bytes 3145728 | tf_op jit(solution)/shard_map/all_to_all | solution.py:44
  377.3 1.5 select_reduce_fusion
  378.9 37.4 %all-to-all-done.1 = bf16[64,1,24,512]{3,2,1,0:T(8,128)(2,1)} async-done(((bf16[64,1,24,512]{3,2,1,0:T(8,128)(2,1)}), bf16[64,1,24,512]{3,2,1,0:T(8,128)(2,1)}, u32[]{:S(2)}, u32[]{:S(2)}) %all-to-all-start.1) | async-done | bytes 1572896 | tf_op jit(solution)/shard_map/all_to_all | solution.py:44
  416.2 3.1 fusion.29
  (104 shorter events, 3.7 us)
Async XLA Ops:
  6.5 32.2 %copy-start = (bf16[2048,768]{1,0:T(8,128)(2,1)S(1)}, bf16[2048,768]{1,0:T(8,128)(2,1)}, u32[]{:S(2)}) copy-start(bf16[2048,768]{1,0:T(8,128)(2,1)} %param.20) | copy-start | bytes 9437188
  6.5 15.8 %copy-start.18 = (f32[512]{0:T(512)S(1)}, f32[512]{0:T(512)}, u32[]{:S(2)}) copy-start(f32[512]{0:T(512)} %param.22) | copy-start | bytes 6148
  6.5 18.2 %copy-start.20 = (s32[4]{0:T(128)S(1)}, s32[4]{0:T(128)}, u32[]{:S(2)}) copy-start(s32[4]{0:T(128)} %param.32) | copy-start | bytes 52
  6.5 93.7 %reduce-scatter.3.cloned.1.call-start = ((), (), s32[]{:S(2)}) async-start(), calls=%async_computation.4 | async-start | bytes 1310720 | tf_op jit(solution)/shard_map/reduce_scatter | solution.py:182
  9.4 29.4 %copy-start.16 = (f32[2048]{0:T(1024)S(1)}, f32[2048]{0:T(1024)}, u32[]{:S(2)}) copy-start(f32[2048]{0:T(1024)} %param.19) | copy-start | bytes 24580
  42.8 2.8 copy-start.19
  42.9 2.8 copy-start.21
  43.9 6.1 %copy-start.4 = (bf16[128,4,576]{2,0,1:T(8,128)(2,1)}, bf16[128,4,576]{2,0,1:T(8,128)(2,1)S(1)}, u32[]{:S(2)}) copy-start(bf16[128,4,576]{2,0,1:T(8,128)(2,1)S(1)} %pad_maximum_fusion) | copy-start | bytes 1769476
  50.1 2.1 copy-start.3
  52.2 2.3 copy-start.8
  52.2 2.3 copy-start.9
  52.2 2.3 copy-start.10
  52.2 2.3 copy-start.11
  52.2 2.3 copy-start.12
  52.2 2.3 copy-start.13
  52.2 2.3 copy-start.14
  54.2 1.4 copy-start.24
  55.6 3.1 copy-start.5
  58.7 5.9 %slice-start = ((bf16[4,4,8,4,576]{4,2,0,3,1:T(8,128)(2,1)}), bf16[4,4,8,4,512]{4,2,0,3,1:T(8,128)(2,1)S(1)}, s32[]{:S(2)}) async-start(bf16[4,4,8,4,576]{4,2,0,3,1:T(8,128)(2,1)} %copy-done.5), calls=%async_computation.7 | async-start | bytes 1048576 | tf_op jit(solution)/shard_map/slice | solution.py:155
  64.6 1.7 copy-start.7
  67.2 1.8 copy-start.6
  69.0 1.8 copy-start.2
  69.0 1.9 copy-start.15
  70.5 154.7 %all-gather.2.cloned.1.call-start = ((), (), s32[]{:S(2)}) async-start(), calls=%async_computation.5 | async-start | bytes 7864320 | tf_op jit(solution)/shard_map/all_gather | solution.py:199
  108.3 116.9 %copy-start.22 = (bf16[1,2048,352]{1,2,0:T(8,128)(2,1)S(1)}, bf16[1,2048,352]{1,2,0:T(8,128)(2,1)}, u32[]{:S(2)}) copy-start(bf16[1,2048,352]{1,2,0:T(8,128)(2,1)} %param.27) | copy-start | bytes 4325380
  161.5 71.3 %copy-start.23 = (bf16[1,352,2048]{2,1,0:T(8,128)(2,1)S(1)}, bf16[1,352,2048]{2,1,0:T(8,128)(2,1)}, u32[]{:S(2)}) copy-start(bf16[1,352,2048]{2,1,0:T(8,128)(2,1)} %param.29) | copy-start | bytes 4325380
  161.6 201.6 %reduce-scatter.5.cloned.1.call-start = ((), (), s32[]{:S(2)}) async-start(), calls=%async_computation.6 | async-start | bytes 15728640 | tf_op jit(solution)/shard_map/reduce_scatter | solution.py:201
  366.4 10.9 %copy-start.17 = (f32[128,6]{0,1:T(8,128)S(1)}, f32[128,6]{0,1:T(8,128)}, u32[]{:S(2)}) copy-start(f32[128,6]{0,1:T(8,128)} %param.35) | copy-start | bytes 9220
  366.4 49.9 %all-to-all-start.1 = ((bf16[64,1,24,512]{3,2,1,0:T(8,128)(2,1)}), bf16[64,1,24,512]{3,2,1,0:T(8,128)(2,1)}, u32[]{:S(2)}, u32[]{:S(2)}) async-start(bf16[64,1,24,512]{3,2,1,0:T(8,128)(2,1)} %convert_bitcast_fusion), calls=%async_computation.3 | async-start | bytes 3145728 | tf_op jit(solution)/shard_map/all_to_all | solution.py:44
  377.3 42.0 %copy-start.1 = (bf16[2048,768]{1,0:T(8,128)(2,1)S(1)}, bf16[2048,768]{1,0:T(8,128)(2,1)}, u32[]{:S(2)}) copy-start(bf16[2048,768]{1,0:T(8,128)(2,1)} %param.20) | copy-start | bytes 9437188
Sparse Core Ops, SparseCore 0:
  70.6 29.5 reduce-scatter.2
  161.7 63.4 all-gather.1
  245.3 117.8 reduce-scatter.4

commit v2 on v1

--- a/solution.py
+++ b/solution.py
@@ -198,8 +198,10 @@
     )
     arrived = lax.all_gather(arrived_cols, "tp", axis=3, tiled=True)
     partial_out = expert_math(arrived, w_gate, w_up, w_down)
-    shares = lax.psum_scatter(partial_out, "tp", scatter_dimension=3, tiled=True)
-    returned = send_home(shares.astype(jnp.bfloat16))
+    shares = lax.psum_scatter(
+        partial_out.astype(jnp.bfloat16), "tp", scatter_dimension=3, tiled=True
+    )
+    returned = send_home(shares)
     combined = jnp.dot(
         weight_rows, returned.reshape(slot_count, col_share).astype(jnp.float32), precision=highest
     )

time: 427 us -> 387 us (0.906)
  waiting for transfers between devices: 244 us -> 190 us
  local copies, waits for them, and re-layouts: 16.3 us -> 26.5 us
    reduce_scatter x1, waiting for transfers between devices: 118 us -> 67.4 us  [local(): lax.psum_scatter(partial_out.astype(jnp.bfloat16), 'tp', scatter_dimensio...]
    unnamed x53 -> x45, local copies, waits for them, and re-layouts: 0.49 us -> 5.89 us
  transfers between devices with their start and end apart: 4 -> 4, of which waited for: 4 -> 4; matrix products, arithmetic and copies ran while one was open for 1% -> 2% of each run, Pallas kernels for 0% -> 0%
where the time goes in v2:
time: 387 us; the launch traced here: 386 us
  waiting for transfers between devices  190 us (49%)
  blocking collectives  70.6 us (18%)
  matrix products  51.1 us (13%)
  local copies, waits for them, and re-layouts  26.5 us (7%)
  other arithmetic  22.7 us (6%)
  between operations  13.5 us (3%)
  starting transfers between devices  11.1 us (3%)
    reduce_scatter x1, waiting for transfers between devices, local(): lax.psum_scatter(partial_out.astype(jnp.bfloat16), 'tp', scatter_dimensio...  67.4 us
    all_gather x1, waiting for transfers between devices, local(): arrived = lax.all_gather(arrived_cols, 'tp', axis=3, tiled=True)  63.6 us
    all_to_all x1, blocking collectives, local(): lax.all_to_all(placed.reshape(req_count, EXP_DEV, capacity, col_share), '...  53.1 us
    all_to_all x1, waiting for transfers between devices, send_home(): lax.all_to_all(shares, 'req', split_axis=0, concat_axis=0, tiled=True)  37.4 us
    reduce_scatter x1, waiting for transfers between devices, local(): lax.psum_scatter(attn_part, 'tp', scatter_dimension=1, tiled=True)  22 us
    dot_general x1, matrix products, expert_math(): jnp.einsum('nesf,efd->nesd', active, down_w, preferred_element_type=jnp.f...  11.7 us
    all_gather x1, blocking collectives, local(): kv_all = lax.all_gather(kv_part, 'tp', axis=1, tiled=True)  11.2 us
    all_to_all x1, starting transfers between devices, send_home(): lax.all_to_all(shares, 'req', split_axis=0, concat_axis=0, tiled=True)  10.8 us
  transfers between devices with their start and end apart: 4, of which 4 were waited for; matrix products, arithmetic and copies ran while one was open for 2% of the time, Pallas kernels for 0%

profile of v2, /device:TPU:1, one launch (start us, length us, event | category | flops | bytes accessed | tf_op | source)
XLA Modules:
  0.0 385.9 jit_solution(17170568226605119130)
XLA Ops:
  7.1 0.8 iota_compare_fusion.3
  8.1 1.2 multiply_reduce_fusion
  9.4 1.6 fusion.58
  11.0 11.2 %all_gather.6 = f32[128,576]{0,1:T(8,128)S(1)} all-gather(f32[128,144]{0,1:T(8,128)S(1)} %fusion.58), channel_id=1, replica_groups=mesh['req'=64,'tp'=4] {'tp'}, dimensions={1}, use_global_device_ids=true | all-gather | bytes 368640 | tf_op jit(solution)/shard_map/all_gather | solution.py:94
  22.3 0.8 multiply_convert_fusion.2
  23.1 1.6 copy.152
  25.0 0.7 multiply_cosine_fusion
  26.3 1.0 pad_maximum_fusion.2
  27.3 0.8 fusion.37
  28.2 0.8 fusion.34
  29.0 0.8 fusion.38
  29.9 0.8 fusion.30
  30.7 0.8 fusion.32
  31.5 0.8 fusion.35
  32.3 0.8 fusion.39
  33.1 0.5 iota_compare_fusion.6
  34.1 0.7 iota_compare_fusion.4
  34.8 0.8 fusion.36
  35.6 0.8 fusion.33
  36.4 0.8 fusion.31
  37.2 0.7 copy.146
  37.9 0.7 copy.148
  38.7 2.4 fusion.59
  41.1 0.6 fusion.80
  41.7 1.7 copy.183
  43.4 1.7 copy.184
  45.1 1.4 fusion.22
  46.5 1.1 subtract_convert_fusion
  47.7 0.8 copy-done.4
  48.5 1.3 copy.149
  49.9 2.2 reshape.293
  52.5 4.1 %gather_fusion = bf16[32,64,576]{2,1,0:T(8,128)(2,1)} fusion(bf16[32,64,576]{2,1,0:T(8,128)(2,1)} %param.30, s32[1024]{0:T(1024)S(1)} %pad_clamp_fusion), kind=kCustom, calls=%fused_computation | custom fusion | bytes 4718720 | tf_op jit(solution)/shard_map/jit(_take)/gather | solution.py:104
  56.6 2.1 bitcast_select_fusion
  58.6 1.5 copy-done.1
  60.2 2.0 fusion.81
  62.4 1.0 maximum_bitcast_fusion
  63.6 0.9 slice.101
  64.5 1.7 fusion.82
  66.5 1.2 fusion.53
  67.7 2.5 reshape.295
  70.1 1.5 exponential_reduce_fusion
  72.0 1.9 fusion.48
  74.0 2.1 fusion.21
  76.1 0.8 copy.166
  77.0 2.1 copy.182
  79.0 1.5 convolution_convert_fusion.2
  80.5 3.1 fusion.83
  83.9 2.2 convert_element_type.90
  86.5 1.8 reduce-window.6
  88.9 0.8 dynamic_slice.7
  89.7 1.6 convert_reduce_fusion
  91.2 22.0 %reduce-scatter.3.cloned.1.call-done = f32[128,512]{1,0:T(8,128)} async-done(((f32[128,2048]{1,0:T(8,128)}), f32[128,512]{1,0:T(8,128)}) %reduce-scatter.3.cloned.1.call-update) | async-done | bytes 262160 | tf_op jit(solution)/shard_map/reduce_scatter | solution.py:182
  113.3 1.1 multiply_reduce_fusion.1
  114.4 6.4 %psum.7 = f32[128,1]{0,1:T(1,128)S(1)} all-reduce(f32[128,1]{0,1:T(1,128)S(1)} %bitcast.233), channel_id=1, replica_groups=mesh['req'=64,'tp'=4] {'tp'}, use_global_device_ids=true, to_apply=%region_13.14 | all-reduce | flops 128 | bytes 1024 | tf_op jit(solution)/shard_map/psum | solution.py:185
  120.8 1.8 convolution_convert_fusion
  122.6 53.1 %all_to_all.10 = bf16[64,1,24,512]{3,2,1,0:T(8,128)(2,1)} all-to-all(bf16[64,1,24,512]{3,2,1,0:T(8,128)(2,1)S(1)} %bitcast.221), channel_id=1, replica_groups=mesh['req'=64,'tp'=4] {'req'}, dimensions={0} | all-to-all | bytes 3145728 | tf_op jit(solution)/shard_map/all_to_all | solution.py:192
  175.8 63.6 %all-gather.2.cloned.1.call-done = bf16[64,1,24,2048]{3,2,0,1:T(8,128)(2,1)} async-done(((bf16[64,1,24,512]{3,2,0,1:T(8,128)(2,1)}), bf16[64,1,24,2048]{3,2,0,1:T(8,128)(2,1)}) %all-gather.2.cloned.1.call-update) | async-done | bytes 6291472 | tf_op jit(solution)/shard_map/all_gather | solution.py:199
  239.4 8.1 %fusion.2 = f32[64,24,352]{2,1,0:T(8,128)} fusion(bf16[64,1,24,2048]{3,2,0,1:T(8,128)(2,1)} %all-gather.2.cloned.1.call-done, bf16[1,2048,352]{1,2,0:T(8,128)(2,1)} %param.27), kind=kOutput, calls=%fused_computation.3 | convolution fusion | flops 2214592512 | bytes 9895936 | tf_op jit(solution)/shard_map/nesd,edf->nesf/dot_general | solution.py:37
  247.4 11.7 %convert_bitcast_fusion = bf16[64,1,24,2048]{3,2,0,1:T(8,128)(2,1)} fusion(bf16[1,352,2048]{2,1,0:T(8,128)(2,1)} %param.29, bf16[1,2048,352]{1,2,0:T(8,128)(2,1)} %param.28, bf16[64,1,24,2048]{3,2,0,1:T(8,128)(2,1)} %all-gather.2.cloned.1.call-done, f32[64,24,352]{2,1,0:T(8,128)} %fusion.2), kind=kOutput, calls=%fused_computation.5 | convolution fusion | flops 4435574784 | bytes 17629184 | tf_op jit(solution)/shard_map/nesf,efd->nesd/dot_general | solution.py:40
  259.2 67.4 %reduce-scatter.5.cloned.1.call-done = bf16[64,1,24,512]{3,2,0,1:T(8,128)(2,1)} async-done(((bf16[64,1,24,2048]{3,2,0,1:T(8,128)(2,1)}), bf16[64,1,24,512]{3,2,0,1:T(8,128)(2,1)}) %reduce-scatter.5.cloned.1.call-update) | async-done | bytes 1572880 | tf_op jit(solution)/shard_map/reduce_scatter | solution.py:201
  326.6 10.8 %all-to-all-start.1 = ((bf16[64,1,24,512]{3,2,1,0:T(8,128)(2,1)}), bf16[64,1,24,512]{3,2,1,0:T(8,128)(2,1)}, u32[]{:S(2)}, u32[]{:S(2)}) async-start(bf16[64,1,24,512]{3,2,1,0:T(8,128)(2,1)} %bitcast.227), calls=%async_computation.3 | async-start | bytes 3145728 | tf_op jit(solution)/shard_map/all_to_all | solution.py:44
  337.4 1.5 select_reduce_fusion
  338.9 37.4 %all-to-all-done.1 = bf16[64,1,24,512]{3,2,1,0:T(8,128)(2,1)} async-done(((bf16[64,1,24,512]{3,2,1,0:T(8,128)(2,1)}), bf16[64,1,24,512]{3,2,1,0:T(8,128)(2,1)}, u32[]{:S(2)}, u32[]{:S(2)}) %all-to-all-start.1) | async-done | bytes 1572896 | tf_op jit(solution)/shard_map/all_to_all | solution.py:44
  376.3 3.1 fusion.29
  (94 shorter events, 5.2 us)
Async XLA Ops:
  6.5 32.1 %copy-start = (bf16[2048,768]{1,0:T(8,128)(2,1)S(1)}, bf16[2048,768]{1,0:T(8,128)(2,1)}, u32[]{:S(2)}) copy-start(bf16[2048,768]{1,0:T(8,128)(2,1)} %param.20) | copy-start | bytes 9437188
  6.5 15.8 %copy-start.16 = (f32[512]{0:T(512)S(1)}, f32[512]{0:T(512)}, u32[]{:S(2)}) copy-start(f32[512]{0:T(512)} %param.22) | copy-start | bytes 6148
  6.5 18.2 %copy-start.18 = (s32[4]{0:T(128)S(1)}, s32[4]{0:T(128)}, u32[]{:S(2)}) copy-start(s32[4]{0:T(128)} %param.32) | copy-start | bytes 52
  6.5 106.7 %reduce-scatter.3.cloned.1.call-start = ((), (), s32[]{:S(2)}) async-start(), calls=%async_computation.4 | async-start | bytes 1310720 | tf_op jit(solution)/shard_map/reduce_scatter | solution.py:182
  9.4 29.3 %copy-start.14 = (f32[2048]{0:T(1024)S(1)}, f32[2048]{0:T(1024)}, u32[]{:S(2)}) copy-start(f32[2048]{0:T(1024)} %param.19) | copy-start | bytes 24580
  46.5 5.7 %copy-start.17 = (s32[4,8]{1,0:T(4,128)S(1)}, s32[4,8]{1,0:T(4,128)}, u32[]{:S(2)}) copy-start(s32[4,8]{1,0:T(4,128)} %param.31) | copy-start | bytes 388
  46.5 5.6 %copy-start.19 = (s32[4]{0:T(128)S(1)}, s32[4]{0:T(128)}, u32[]{:S(2)}) copy-start(s32[4]{0:T(128)} %iota_multiply_fusion) | copy-start | bytes 52
  47.7 0.8 copy-start.4
  56.6 3.6 copy-start.3
  58.6 1.5 copy-start.1
  60.1 2.3 copy-start.6
  60.1 2.3 copy-start.7
  60.1 2.3 copy-start.8
  60.1 2.3 copy-start.9
  60.1 2.3 copy-start.10
  60.2 2.3 copy-start.11
  60.2 2.3 copy-start.12
  62.2 2.3 copy-start.20
  62.3 2.2 copy-start.5
  72.0 2.0 copy-start.2
  80.5 5.5 %copy-start.13 = (s32[128,6]{0,1:T(8,128)S(1)}, s32[128,6]{0,1:T(8,128)}, u32[]{:S(2)}) copy-start(s32[128,6]{0,1:T(8,128)} %param.34) | copy-start | bytes 9220
  83.6 155.8 %all-gather.2.cloned.1.call-start = ((), (), s32[]{:S(2)}) async-start(), calls=%async_computation.5 | async-start | bytes 7864320 | tf_op jit(solution)/shard_map/all_gather | solution.py:199
  175.7 150.8 %reduce-scatter.5.cloned.1.call-start = ((), (), s32[]{:S(2)}) async-start(), calls=%async_computation.6 | async-start | bytes 7864320 | tf_op jit(solution)/shard_map/reduce_scatter | solution.py:201
  259.1 78.2 %copy-start.15 = (f32[128,6]{0,1:T(8,128)S(1)}, f32[128,6]{0,1:T(8,128)}, u32[]{:S(2)}) copy-start(f32[128,6]{0,1:T(8,128)} %param.35) | copy-start | bytes 9220
  326.6 49.7 %all-to-all-start.1 = ((bf16[64,1,24,512]{3,2,1,0:T(8,128)(2,1)}), bf16[64,1,24,512]{3,2,1,0:T(8,128)(2,1)}, u32[]{:S(2)}, u32[]{:S(2)}) async-start(bf16[64,1,24,512]{3,2,1,0:T(8,128)(2,1)} %bitcast.227), calls=%async_computation.3 | async-start | bytes 3145728 | tf_op jit(solution)/shard_map/all_to_all | solution.py:44
Sparse Core Ops, SparseCore 0:
  83.7 29.4 reduce-scatter.2
  175.8 63.4 all-gather.1
  259.3 67.2 reduce-scatter.4

commit v3 on v1

--- a/solution.py
+++ b/solution.py
@@ -14,6 +14,7 @@
 STEPS = 4
 PAGE = 64
 PAGES = 8
+MOE_CHUNKS = 4
 
 
 eps = 1e-06
@@ -189,17 +190,24 @@
     placed = jnp.dot(gather_rows.T, moe_in_cols, preferred_element_type=jnp.float32).astype(
         jnp.bfloat16
     )
-    arrived_cols = lax.all_to_all(
-        placed.reshape(req_count, EXP_DEV, capacity, col_share),
-        "req",
-        split_axis=0,
-        concat_axis=0,
-        tiled=True,
-    )
-    arrived = lax.all_gather(arrived_cols, "tp", axis=3, tiled=True)
-    partial_out = expert_math(arrived, w_gate, w_up, w_down)
-    shares = lax.psum_scatter(partial_out, "tp", scatter_dimension=3, tiled=True)
-    returned = send_home(shares.astype(jnp.bfloat16))
+    placed = placed.reshape(req_count, EXP_DEV, capacity, col_share)
+    chunk = capacity // MOE_CHUNKS
+    returned_parts = []
+    for chunk_index in range(MOE_CHUNKS):
+        arrived_cols = lax.all_to_all(
+            placed[:, :, chunk_index * chunk : (chunk_index + 1) * chunk],
+            "req",
+            split_axis=0,
+            concat_axis=0,
+            tiled=True,
+        )
+        arrived = lax.all_gather(arrived_cols, "tp", axis=3, tiled=True)
+        partial_out = expert_math(arrived, w_gate, w_up, w_down)
+        shares = lax.psum_scatter(
+            partial_out.astype(jnp.bfloat16), "tp", scatter_dimension=3, tiled=True
+        )
+        returned_parts.append(send_home(shares))
+    returned = jnp.concatenate(returned_parts, axis=2)
     combined = jnp.dot(
         weight_rows, returned.reshape(slot_count, col_share).astype(jnp.float32), precision=highest
     )

time: 427 us -> 441 us (1.033)
  waiting for transfers between devices: 244 us -> 125 us
  blocking collectives: 70.8 us -> 120 us
  starting transfers between devices: 11.2 us -> 48.4 us
  local copies, waits for them, and re-layouts: 16.3 us -> 39.7 us
  matrix products: 47.3 us -> 65.8 us
    all_to_all x1 -> x4, blocking collectives: 53.2 us -> 102 us  [local(): lax.all_to_all(placed[:, :, chunk_index * chunk:(chunk_index + 1) * chunk...]
    all_gather x1 -> x4, waiting for transfers between devices: 63.6 us -> 15.6 us  [local(): arrived = lax.all_gather(arrived_cols, 'tp', axis=3, tiled=True)]
    reduce_scatter x1 -> x4, waiting for transfers between devices: 118 us -> 71.2 us  [local(): lax.psum_scatter(partial_out.astype(jnp.bfloat16), 'tp', scatter_dimensio...]
    all_to_all x1 -> x4, starting transfers between devices: 10.9 us -> 47.7 us  [send_home(): lax.all_to_all(shares, 'req', split_axis=0, concat_axis=0, tiled=True)]
    all_to_all x1 -> x4, waiting for transfers between devices: 37.4 us -> 16.1 us  [send_home(): lax.all_to_all(shares, 'req', split_axis=0, concat_axis=0, tiled=True)]
    dot_general x1 -> x4, matrix products: 12.3 us -> 22 us  [expert_math(): jnp.einsum('nesf,efd->nesd', active, down_w, preferred_element_type=jnp.f...]
    reduce_scatter x0 -> x4, local copies, waits for them, and re-layouts: none -> 8.04 us  [local(): lax.psum_scatter(partial_out.astype(jnp.bfloat16), 'tp', scatter_dimensio...]
    dot_general x1 -> x4, matrix products: 7.64 us -> 14.8 us  [expert_math(): jnp.einsum('nesd,edf->nesf', arrived, gate_w, preferred_element_type=jnp....]
  transfers between devices with their start and end apart: 4 -> 13, of which waited for: 4 -> 7; matrix products, arithmetic and copies ran while one was open for 1% -> 13% of each run, Pallas kernels for 0% -> 0%
where the time goes in v3:
time: 441 us; the launch traced here: 439 us
  waiting for transfers between devices  125 us (28%)
  blocking collectives  120 us (27%)
  matrix products  65.8 us (15%)
  starting transfers between devices  48.4 us (11%)
  local copies, waits for them, and re-layouts  39.7 us (9%)
  other arithmetic  27 us (6%)
  between operations  13.7 us (3%)
    all_to_all x4, blocking collectives, local(): lax.all_to_all(placed[:, :, chunk_index * chunk:(chunk_index + 1) * chunk...  102 us
    reduce_scatter x4, waiting for transfers between devices, local(): lax.psum_scatter(partial_out.astype(jnp.bfloat16), 'tp', scatter_dimensio...  71.2 us
    all_to_all x4, starting transfers between devices, send_home(): lax.all_to_all(shares, 'req', split_axis=0, concat_axis=0, tiled=True)  47.7 us
    reduce_scatter x1, waiting for transfers between devices, local(): lax.psum_scatter(attn_part, 'tp', scatter_dimension=1, tiled=True)  22.1 us
    dot_general x4, matrix products, expert_math(): jnp.einsum('nesf,efd->nesd', active, down_w, preferred_element_type=jnp.f...  22 us
    all_to_all x4, waiting for transfers between devices, send_home(): lax.all_to_all(shares, 'req', split_axis=0, concat_axis=0, tiled=True)  16.1 us
    all_gather x4, waiting for transfers between devices, local(): arrived = lax.all_gather(arrived_cols, 'tp', axis=3, tiled=True)  15.6 us
    dot_general x4, matrix products, expert_math(): jnp.einsum('nesd,edf->nesf', arrived, gate_w, preferred_element_type=jnp....  14.8 us
  transfers between devices with their start and end apart: 13, of which 7 were waited for; matrix products, arithmetic and copies ran while one was open for 13% of the time, Pallas kernels for 0%

profile of v3, /device:TPU:1, one launch (start us, length us, event | category | flops | bytes accessed | tf_op | source)
XLA Modules:
  0.0 439.2 jit_solution(9429141945775908812)
XLA Ops:
  8.1 1.2 multiply_reduce_fusion
  9.4 1.6 fusion.199
  11.0 11.2 %all_gather.15 = f32[128,576]{0,1:T(8,128)S(1)} all-gather(f32[128,144]{0,1:T(8,128)S(1)} %fusion.199), channel_id=1, replica_groups=mesh['req'=64,'tp'=4] {'tp'}, dimensions={1}, use_global_device_ids=true | all-gather | bytes 368640 | tf_op jit(solution)/shard_map/all_gather | solution.py:95
  25.2 1.0 copy.187
  32.1 1.3 iota_compare_fusion.4
  38.4 1.0 maximum_bitcast_fusion
  41.2 1.4 fusion.200
  43.3 1.7 copy.232
  45.0 1.7 copy.231
  46.6 1.4 copy.183
  48.8 1.4 fusion.96
  50.2 1.1 subtract_convert_fusion
  52.3 1.4 copy.184
  53.7 2.2 reshape.335
  55.9 3.0 fusion.227
  59.0 4.2 gather_fusion
  63.2 2.1 bitcast_select_fusion
  65.3 2.0 fusion.226
  67.4 2.5 reshape.337
  69.9 1.5 exponential_reduce_fusion
  71.8 1.2 fusion.194
  73.2 1.9 fusion.185
  75.1 2.1 fusion.35
  78.1 2.0 copy.230
  80.2 1.5 convolution_convert_fusion.6
  81.7 3.0 fusion.228
  85.0 2.2 convert_element_type.135
  87.6 1.8 reduce-window.6
  90.8 1.5 convert_reduce_fusion
  92.3 22.1 %reduce-scatter.6.cloned.1.call-done = f32[128,512]{1,0:T(8,128)} async-done(((f32[128,2048]{1,0:T(8,128)}), f32[128,512]{1,0:T(8,128)}) %reduce-scatter.6.cloned.1.call-update) | async-done | bytes 262160 | tf_op jit(solution)/shard_map/reduce_scatter | solution.py:183
  114.5 1.1 multiply_reduce_fusion.1
  115.6 6.5 %psum.7 = f32[128,1]{0,1:T(1,128)S(1)} all-reduce(f32[128,1]{0,1:T(1,128)S(1)} %bitcast.433), channel_id=1, replica_groups=mesh['req'=64,'tp'=4] {'tp'}, use_global_device_ids=true, to_apply=%region_13.14 | all-reduce | flops 128 | bytes 1024 | tf_op jit(solution)/shard_map/psum | solution.py:186
  122.1 1.8 convolution_convert_fusion
  123.9 1.5 fusion.224
  125.3 31.6 %all_to_all.40 = bf16[64,1,6,512]{3,2,1,0:T(8,128)(2,1)S(1)} all-to-all(bf16[64,1,6,512]{3,2,1,0:T(8,128)(2,1)S(1)} %get-tuple-element.10), channel_id=1, replica_groups=mesh['req'=64,'tp'=4] {'req'}, dimensions={0} | all-to-all | bytes 786432 | tf_op jit(solution)/shard_map/all_to_all | solution.py:197
  157.9 23.4 %all_to_all.41 = bf16[64,1,6,512]{3,2,1,0:T(8,128)(2,1)S(1)} all-to-all(bf16[64,1,6,512]{3,2,1,0:T(8,128)(2,1)} %get-tuple-element.11), channel_id=1, replica_groups=mesh['req'=64,'tp'=4] {'req'}, dimensions={0} | all-to-all | bytes 786432 | tf_op jit(solution)/shard_map/all_to_all | solution.py:197
  182.3 23.4 %all_to_all.42 = bf16[64,1,6,512]{3,2,1,0:T(8,128)(2,1)S(1)} all-to-all(bf16[64,1,6,512]{3,2,1,0:T(8,128)(2,1)} %get-tuple-element.12), channel_id=1, replica_groups=mesh['req'=64,'tp'=4] {'req'}, dimensions={0} | all-to-all | bytes 786432 | tf_op jit(solution)/shard_map/all_to_all | solution.py:197
  206.7 23.4 %all_to_all.43 = bf16[64,1,6,512]{3,2,1,0:T(8,128)(2,1)S(1)} all-to-all(bf16[64,1,6,512]{3,2,1,0:T(8,128)(2,1)} %get-tuple-element.9), channel_id=1, replica_groups=mesh['req'=64,'tp'=4] {'req'}, dimensions={0} | all-to-all | bytes 786432 | tf_op jit(solution)/shard_map/all_to_all | solution.py:197
  230.1 0.9 copy.208
  231.1 3.7 fusion.81
  234.8 5.5 %fusion.3 = bf16[64,1,6,2048]{3,0,2,1:T(8,128)(2,1)} fusion(bf16[1,352,2048]{2,1,0:T(8,128)(2,1)} %param.29, bf16[1,2048,352]{1,2,0:T(8,128)(2,1)} %param.28, bf16[64,1,6,2048]{3,0,2,1:T(8,128)(2,1)} %all-gather.11.cloned.1.call-done, f32[64,1,6,352]{3,0,2,1:T(8,128)} %fusion.81), kind=kOutput, calls=%fused_computation.13 | convolution fusion | flops 1108893696 | bytes 6569984 | tf_op jit(solution)/shard_map/nesf,efd->nesd/dot_general | solution.py:41
  240.5 3.7 fusion.66
  244.2 5.5 %fusion.2 = bf16[64,1,6,2048]{3,0,2,1:T(8,128)(2,1)} fusion(bf16[1,352,2048]{2,1,0:T(8,128)(2,1)} %param.29, bf16[1,2048,352]{1,2,0:T(8,128)(2,1)} %param.28, bf16[64,1,6,2048]{3,0,2,1:T(8,128)(2,1)} %all-gather.9.cloned.1.call-done, f32[64,1,6,352]{3,0,2,1:T(8,128)} %fusion.66), kind=kOutput, calls=%fused_computation.12 | convolution fusion | flops 1108893696 | bytes 6569984 | tf_op jit(solution)/shard_map/nesf,efd->nesd/dot_general | solution.py:41
  250.0 3.7 fusion.51
  253.7 5.5 %fusion.1 = bf16[64,1,6,2048]{3,0,2,1:T(8,128)(2,1)} fusion(bf16[1,352,2048]{2,1,0:T(8,128)(2,1)} %param.29, bf16[1,2048,352]{1,2,0:T(8,128)(2,1)} %param.28, bf16[64,1,6,2048]{3,0,2,1:T(8,128)(2,1)} %all-gather.7.cloned.1.call-done, f32[64,1,6,352]{3,0,2,1:T(8,128)} %fusion.51), kind=kOutput, calls=%fused_computation.11 | convolution fusion | flops 1108893696 | bytes 6569984 | tf_op jit(solution)/shard_map/nesf,efd->nesd/dot_general | solution.py:41
  259.3 15.5 %all-gather.5.cloned.1.call-done = bf16[64,1,6,2048]{3,0,2,1:T(8,128)(2,1)} async-done(((bf16[64,1,6,512]{3,0,2,1:T(8,128)(2,1)}), bf16[64,1,6,2048]{3,0,2,1:T(8,128)(2,1)}) %all-gather.5.cloned.1.call-update) | async-done | bytes 1572880 | tf_op jit(solution)/shard_map/all_gather | solution.py:204
  274.8 3.7 fusion.36
  278.5 5.5 %fusion = bf16[64,1,6,2048]{3,0,2,1:T(8,128)(2,1)} fusion(bf16[1,352,2048]{2,1,0:T(8,128)(2,1)} %param.29, bf16[1,2048,352]{1,2,0:T(8,128)(2,1)} %param.28, bf16[64,1,6,2048]{3,0,2,1:T(8,128)(2,1)} %all-gather.5.cloned.1.call-done, f32[64,1,6,352]{3,0,2,1:T(8,128)} %fusion.36), kind=kOutput, calls=%fused_computation.10 | convolution fusion | flops 1108893696 | bytes 6569984 | tf_op jit(solution)/shard_map/nesf,efd->nesd/dot_general | solution.py:41
  284.0 20.7 %reduce-scatter.14.cloned.1.call-done = bf16[64,1,6,512]{3,0,2,1:T(8,128)(2,1)} async-done(((bf16[64,1,6,2048]{3,0,2,1:T(8,128)(2,1)}), bf16[64,1,6,512]{3,0,2,1:T(8,128)(2,1)}) %reduce-scatter.14.cloned.1.call-update) | async-done | bytes 393232 | tf_op jit(solution)/shard_map/reduce_scatter | solution.py:206
  304.7 2.0 copy.218
  306.8 11.9 %all-to-all-start.7 = ((bf16[64,1,6,512]{3,2,1,0:T(8,128)(2,1)}), bf16[64,1,6,512]{3,2,1,0:T(8,128)(2,1)}, u32[]{:S(2)}, u32[]{:S(2)}) async-start(bf16[64,1,6,512]{3,2,1,0:T(8,128)(2,1)} %copy.218), calls=%async_computation.12 | async-start | bytes 1048576 | tf_op jit(solution)/shard_map/all_to_all | solution.py:45
  318.6 16.8 %reduce-scatter.12.cloned.1.call-done = bf16[64,1,6,512]{3,0,2,1:T(8,128)(2,1)} async-done(((bf16[64,1,6,2048]{3,0,2,1:T(8,128)(2,1)}), bf16[64,1,6,512]{3,0,2,1:T(8,128)(2,1)}) %reduce-scatter.12.cloned.1.call-update) | async-done | bytes 393232 | tf_op jit(solution)/shard_map/reduce_scatter | solution.py:206
  335.5 2.0 copy.215
  337.5 11.9 %all-to-all-start.5 = ((bf16[64,1,6,512]{3,2,1,0:T(8,128)(2,1)}), bf16[64,1,6,512]{3,2,1,0:T(8,128)(2,1)}, u32[]{:S(2)}, u32[]{:S(2)}) async-start(bf16[64,1,6,512]{3,2,1,0:T(8,128)(2,1)} %copy.215), calls=%async_computation.9 | async-start | bytes 1048576 | tf_op jit(solution)/shard_map/all_to_all | solution.py:45
  349.4 16.9 %reduce-scatter.10.cloned.1.call-done = bf16[64,1,6,512]{3,0,2,1:T(8,128)(2,1)} async-done(((bf16[64,1,6,2048]{3,0,2,1:T(8,128)(2,1)}), bf16[64,1,6,512]{3,0,2,1:T(8,128)(2,1)}) %reduce-scatter.10.cloned.1.call-update) | async-done | bytes 393232 | tf_op jit(solution)/shard_map/reduce_scatter | solution.py:206
  366.2 2.0 copy.212
  368.2 12.0 %all-to-all-start.3 = ((bf16[64,1,6,512]{3,2,1,0:T(8,128)(2,1)}), bf16[64,1,6,512]{3,2,1,0:T(8,128)(2,1)}, u32[]{:S(2)}, u32[]{:S(2)}) async-start(bf16[64,1,6,512]{3,2,1,0:T(8,128)(2,1)} %copy.212), calls=%async_computation.6 | async-start | bytes 1048576 | tf_op jit(solution)/shard_map/all_to_all | solution.py:45
  380.3 16.7 %reduce-scatter.8.cloned.1.call-done = bf16[64,1,6,512]{3,0,2,1:T(8,128)(2,1)} async-done(((bf16[64,1,6,2048]{3,0,2,1:T(8,128)(2,1)}), bf16[64,1,6,512]{3,0,2,1:T(8,128)(2,1)}) %reduce-scatter.8.cloned.1.call-update) | async-done | bytes 393232 | tf_op jit(solution)/shard_map/reduce_scatter | solution.py:206
  397.0 2.0 copy.209
  399.0 11.9 %all-to-all-start.1 = ((bf16[64,1,6,512]{3,2,1,0:T(8,128)(2,1)}), bf16[64,1,6,512]{3,2,1,0:T(8,128)(2,1)}, u32[]{:S(2)}, u32[]{:S(2)}) async-start(bf16[64,1,6,512]{3,2,1,0:T(8,128)(2,1)} %copy.209), calls=%async_computation.3 | async-start | bytes 1048576 | tf_op jit(solution)/shard_map/all_to_all | solution.py:45
  410.9 1.5 select_reduce_fusion
  412.5 16.1 %all-to-all-done.1 = bf16[64,1,6,512]{3,2,1,0:T(8,128)(2,1)} async-done(((bf16[64,1,6,512]{3,2,1,0:T(8,128)(2,1)}), bf16[64,1,6,512]{3,2,1,0:T(8,128)(2,1)}, u32[]{:S(2)}, u32[]{:S(2)}) %all-to-all-start.1) | async-done | bytes 393248 | tf_op jit(solution)/shard_map/all_to_all | solution.py:45
  428.5 2.6 pad_maximum_fusion
  431.2 1.5 fusion.138
  (131 shorter events, 26.6 us)
Async XLA Ops:
  6.5 34.7 %copy-start = (bf16[2048,768]{1,0:T(8,128)(2,1)S(1)}, bf16[2048,768]{1,0:T(8,128)(2,1)}, u32[]{:S(2)}) copy-start(bf16[2048,768]{1,0:T(8,128)(2,1)} %param.20) | copy-start | bytes 9437188
  6.5 17.9 %copy-start.14 = (f32[512]{0:T(512)S(1)}, f32[512]{0:T(512)}, u32[]{:S(2)}) copy-start(f32[512]{0:T(512)} %param.22) | copy-start | bytes 6148
  6.5 107.9 %reduce-scatter.6.cloned.1.call-start = ((), (), s32[]{:S(2)}) async-start(), calls=%async_computation.13 | async-start | bytes 1310720 | tf_op jit(solution)/shard_map/reduce_scatter | solution.py:183
  9.3 14.2 %copy-start.15 = (f32[128]{0:T(128)}, f32[128]{0:T(128)S(1)}, u32[]{:S(2)}) copy-start(f32[128]{0:T(128)S(1)} %add_rsqrt_fusion.1) | copy-start | bytes 1540
  9.4 17.3 %copy-start.12 = (s32[4,3,8]{2,0,1:T(4,128)S(1)}, s32[4,3,8]{2,0,1:T(4,128)}, u32[]{:S(2)}) copy-start(s32[4,3,8]{2,0,1:T(4,128)} %param.33) | copy-start | bytes 1156
  38.4 2.8 copy-start.3
  38.4 2.8 copy-start.10
  38.4 2.8 copy-start.16
  39.5 0.8 copy-start.7
  51.4 0.8 copy-start.6
  52.3 3.6 copy-start.17
  59.0 4.2 copy-start.11
  63.2 2.1 copy-start.5
  63.2 2.1 copy-start.9
  65.3 2.0 copy-start.1
  73.2 2.0 copy-start.2
  84.7 2.4 copy-start.8
  84.7 146.4 %all-gather.11.cloned.1.call-start = ((), (), s32[]{:S(2)}) async-start(), calls=%async_computation.20 | async-start | bytes 1966080 | tf_op jit(solution)/shard_map/all_gather | solution.py:204
  157.8 82.6 %all-gather.9.cloned.1.call-start = ((), (), s32[]{:S(2)}) async-start(), calls=%async_computation.18 | async-start | bytes 1966080 | tf_op jit(solution)/shard_map/all_gather | solution.py:204
  182.2 67.8 %all-gather.7.cloned.1.call-start = ((), (), s32[]{:S(2)}) async-start(), calls=%async_computation.16 | async-start | bytes 1966080 | tf_op jit(solution)/shard_map/all_gather | solution.py:204
  206.6 68.1 %all-gather.5.cloned.1.call-start = ((), (), s32[]{:S(2)}) async-start(), calls=%async_computation.14 | async-start | bytes 1966080 | tf_op jit(solution)/shard_map/all_gather | solution.py:204
  231.1 73.7 %reduce-scatter.14.cloned.1.call-start = ((), (), s32[]{:S(2)}) async-start(), calls=%async_computation.21 | async-start | bytes 1966080 | tf_op jit(solution)/shard_map/reduce_scatter | solution.py:206
  240.4 95.1 %reduce-scatter.12.cloned.1.call-start = ((), (), s32[]{:S(2)}) async-start(), calls=%async_computation.19 | async-start | bytes 1966080 | tf_op jit(solution)/shard_map/reduce_scatter | solution.py:206
  249.7 116.5 %reduce-scatter.10.cloned.1.call-start = ((), (), s32[]{:S(2)}) async-start(), calls=%async_computation.17 | async-start | bytes 1966080 | tf_op jit(solution)/shard_map/reduce_scatter | solution.py:206
  259.2 137.8 %reduce-scatter.8.cloned.1.call-start = ((), (), s32[]{:S(2)}) async-start(), calls=%async_computation.15 | async-start | bytes 1966080 | tf_op jit(solution)/shard_map/reduce_scatter | solution.py:206
  306.8 30.7 %all-to-all-start.7 = ((bf16[64,1,6,512]{3,2,1,0:T(8,128)(2,1)}), bf16[64,1,6,512]{3,2,1,0:T(8,128)(2,1)}, u32[]{:S(2)}, u32[]{:S(2)}) async-start(bf16[64,1,6,512]{3,2,1,0:T(8,128)(2,1)} %copy.218), calls=%async_computation.12 | async-start | bytes 1048576 | tf_op jit(solution)/shard_map/all_to_all | solution.py:45
  337.5 30.8 %all-to-all-start.5 = ((bf16[64,1,6,512]{3,2,1,0:T(8,128)(2,1)}), bf16[64,1,6,512]{3,2,1,0:T(8,128)(2,1)}, u32[]{:S(2)}, u32[]{:S(2)}) async-start(bf16[64,1,6,512]{3,2,1,0:T(8,128)(2,1)} %copy.215), calls=%async_computation.9 | async-start | bytes 1048576 | tf_op jit(solution)/shard_map/all_to_all | solution.py:45
  368.2 42.7 %copy-start.13 = (f32[128,6]{0,1:T(8,128)S(1)}, f32[128,6]{0,1:T(8,128)}, u32[]{:S(2)}) copy-start(f32[128,6]{0,1:T(8,128)} %param.35) | copy-start | bytes 9220
  368.2 30.8 %all-to-all-start.3 = ((bf16[64,1,6,512]{3,2,1,0:T(8,128)(2,1)}), bf16[64,1,6,512]{3,2,1,0:T(8,128)(2,1)}, u32[]{:S(2)}, u32[]{:S(2)}) async-start(bf16[64,1,6,512]{3,2,1,0:T(8,128)(2,1)} %copy.212), calls=%async_computation.6 | async-start | bytes 1048576 | tf_op jit(solution)/shard_map/all_to_all | solution.py:45
  399.0 29.5 %all-to-all-start.1 = ((bf16[64,1,6,512]{3,2,1,0:T(8,128)(2,1)}), bf16[64,1,6,512]{3,2,1,0:T(8,128)(2,1)}, u32[]{:S(2)}, u32[]{:S(2)}) async-start(bf16[64,1,6,512]{3,2,1,0:T(8,128)(2,1)} %copy.209), calls=%async_computation.3 | async-start | bytes 1048576 | tf_op jit(solution)/shard_map/all_to_all | solution.py:45
  428.5 2.6 copy-start.4
Sparse Core Ops, SparseCore 0:
  84.9 29.5 reduce-scatter.5
  157.9 23.6 all-gather.10
  183.6 29.1 all-gather.8
  214.6 29.1 all-gather.6
  245.6 29.1 all-gather.4
  277.3 27.3 reduce-scatter.13
  307.5 27.9 reduce-scatter.11
  338.2 27.9 reduce-scatter.9
  369.0 27.9 reduce-scatter.7

commit v4 on v2

--- a/solution.py
+++ b/solution.py
@@ -33,11 +33,32 @@
     )
 
 
-def expert_math(arrived, gate_w, up_w, down_w):
+def expert_math(arrived, gate_w, up_w, down_cols):
     gate_val = jnp.einsum("nesd,edf->nesf", arrived, gate_w, preferred_element_type=jnp.float32)
     up_val = jnp.einsum("nesd,edf->nesf", arrived, up_w, preferred_element_type=jnp.float32)
     active = (jax.nn.silu(gate_val) * up_val).astype(jnp.bfloat16)
-    return jnp.einsum("nesf,efd->nesd", active, down_w, preferred_element_type=jnp.float32)
+    active_all = lax.all_gather(active, "tp", axis=3, tiled=True)
+    return jnp.einsum(
+        "nesf,efd->nesd", active_all, down_cols, preferred_element_type=jnp.float32
+    ).astype(jnp.bfloat16)
+
+
+def down_by_columns(down_w):
+    tp_count = lax.axis_size("tp")
+    tp_index = lax.axis_index("tp")
+    col_share = down_w.shape[2] // tp_count
+    pieces = [None] * tp_count
+    for shift in range(tp_count):
+        target = (tp_index + shift) % tp_count
+        piece = lax.dynamic_slice_in_dim(down_w, target * col_share, col_share, 2)
+        if shift:
+            piece = lax.ppermute(
+                piece, "tp", [(s, (s + shift) % tp_count) for s in range(tp_count)]
+            )
+        pieces[shift] = piece
+    stacked = jnp.stack(pieces, axis=0)
+    ordered = jnp.take(stacked, (tp_index - jnp.arange(tp_count)) % tp_count, axis=0)
+    return jnp.concatenate([ordered[i] for i in range(tp_count)], axis=1)
 
 
 def send_home(shares):
@@ -179,6 +200,7 @@
     weight_rows = jnp.sum(jnp.where(slot_hot, route_weights[:, :, None], 0.0), axis=1)
     tp_index = lax.axis_index("tp")
     col_start = tp_index * col_share
+    attn_part, down_cols = lax.optimization_barrier((attn_part, down_by_columns(w_down)))
     attn_cols = lax.psum_scatter(attn_part, "tp", scatter_dimension=1, tiled=True)
     hidden_cols = lax.dynamic_slice_in_dim(hidden_f, col_start, col_share, 1)
     resid_cols = hidden_cols + attn_cols
@@ -197,10 +219,7 @@
         tiled=True,
     )
     arrived = lax.all_gather(arrived_cols, "tp", axis=3, tiled=True)
-    partial_out = expert_math(arrived, w_gate, w_up, w_down)
-    shares = lax.psum_scatter(
-        partial_out.astype(jnp.bfloat16), "tp", scatter_dimension=3, tiled=True
-    )
+    shares = expert_math(arrived, w_gate, w_up, down_cols)
     returned = send_home(shares)
     combined = jnp.dot(
         weight_rows, returned.reshape(slot_count, col_share).astype(jnp.float32), precision=highest

time: 387 us -> 423 us (1.093)
  waiting for transfers between devices: 190 us -> 215 us
  matrix products: 51.1 us -> 42 us
  local copies, waits for them, and re-layouts: 26.5 us -> 35.4 us
  blocking collectives: 70.6 us -> 77.9 us
  starting transfers between devices: 11.1 us -> 16.9 us
    all_gather x0 -> x1, waiting for transfers between devices: none -> 88.8 us  [expert_math(): active_all = lax.all_gather(active, 'tp', axis=3, tiled=True)]
    reduce_scatter x1 -> x0, waiting for transfers between devices: 67.4 us -> none  [local(): lax.psum_scatter(partial_out.astype(jnp.bfloat16), 'tp', scatter_dimensio...]
    all_gather x0 -> x1, local copies, waits for them, and re-layouts: none -> 10.8 us  [expert_math(): active_all = lax.all_gather(active, 'tp', axis=3, tiled=True)]
    all_gather x1, blocking collectives: 11.2 us -> 18.4 us  [local(): kv_all = lax.all_gather(kv_part, 'tp', axis=1, tiled=True)]
    ppermute x0 -> x3, starting transfers between devices: none -> 5.64 us  [down_by_columns(): lax.ppermute(piece, 'tp', [(s, (s + shift) % tp_count) for s in range(tp_...]
    unnamed x45 -> x69, local copies, waits for them, and re-layouts: 5.89 us -> 0.52 us
    convert_element_type x0 -> x2, local copies, waits for them, and re-layouts: none -> 4.98 us  [the longest x1 2.98 us: expert_math(): active = (jax.nn.silu(gate_val) * up_val).astype(jnp.bfloat16)]
    dot_general x1 -> x2, matrix products: 11.7 us -> 9.95 us  [the longest x1 5.13 us: expert_math(): jnp.einsum('nesd,edf->nesf', arrived, up_w, preferred_element_type=jnp.fl...]
  transfers between devices with their start and end apart: 4 -> 7, of which waited for: 4 -> 4; matrix products, arithmetic and copies ran while one was open for 2% -> 13% of each run, Pallas kernels for 0% -> 0%
where the time goes in v4:
time: 423 us; the launch traced here: 421 us
  waiting for transfers between devices  215 us (51%)
  blocking collectives  77.9 us (18%)
  matrix products  42 us (10%)
  local copies, waits for them, and re-layouts  35.4 us (8%)
  other arithmetic  20.5 us (5%)
  starting transfers between devices  16.9 us (4%)
  between operations  13.9 us (3%)
    all_gather x1, waiting for transfers between devices, expert_math(): active_all = lax.all_gather(active, 'tp', axis=3, tiled=True)  88.8 us
    all_gather x1, waiting for transfers between devices, local(): arrived = lax.all_gather(arrived_cols, 'tp', axis=3, tiled=True)  63.6 us
    all_to_all x1, blocking collectives, local(): lax.all_to_all(placed.reshape(req_count, EXP_DEV, capacity, col_share), '...  53 us
    all_to_all x1, waiting for transfers between devices, send_home(): lax.all_to_all(shares, 'req', split_axis=0, concat_axis=0, tiled=True)  37.4 us
    reduce_scatter x1, waiting for transfers between devices, local(): lax.psum_scatter(attn_part, 'tp', scatter_dimension=1, tiled=True)  24.9 us
    all_gather x1, blocking collectives, local(): kv_all = lax.all_gather(kv_part, 'tp', axis=1, tiled=True)  18.4 us
    all_to_all x1, starting transfers between devices, send_home(): lax.all_to_all(shares, 'req', split_axis=0, concat_axis=0, tiled=True)  11 us
    all_gather x1, local copies, waits for them, and re-layouts, expert_math(): active_all = lax.all_gather(active, 'tp', axis=3, tiled=True)  10.8 us
  transfers between devices with their start and end apart: 7, of which 4 were waited for; matrix products, arithmetic and copies ran while one was open for 13% of the time, Pallas kernels for 0%

profile of v4, /device:TPU:1, one launch (start us, length us, event | category | flops | bytes accessed | tf_op | source)
XLA Modules:
  0.0 421.5 jit_solution(4326087865901527149)
XLA Ops:
  6.6 2.6 dynamic-slice_bitcast_fusion
  9.3 2.0 collective-permute-start
  11.3 2.5 collective-permute-start.1
  13.8 1.2 collective-permute-start.2
  14.9 0.6 fusion.79
  15.5 0.5 multiply_power_fusion
  17.0 18.4 %all_gather.9 = f32[128,576]{0,1:T(8,128)S(1)} all-gather(f32[128,144]{0,1:T(8,128)S(1)} %fusion.56), channel_id=1, replica_groups=mesh['req'=64,'tp'=4] {'tp'}, dimensions={1}, use_global_device_ids=true | all-gather | bytes 368640 | tf_op jit(solution)/shard_map/all_gather | solution.py:115
  35.5 0.8 multiply_convert_fusion.2
  36.3 1.7 copy.171
  38.2 0.8 multiply_cosine_fusion
  39.5 1.0 pad_maximum_fusion.3
  40.5 0.8 fusion.35
  41.5 0.8 fusion.32
  42.3 0.8 fusion.36
  43.2 0.8 fusion.28
  44.0 0.8 fusion.30
  44.8 0.8 fusion.33
  45.6 0.8 fusion.37
  46.3 0.6 iota_compare_fusion.6
  46.9 0.6 iota_multiply_fusion
  47.6 0.7 pad_clamp_fusion
  48.3 0.8 fusion.34
  49.0 0.8 fusion.31
  49.8 0.8 fusion.29
  50.6 0.7 copy.165
  51.3 0.7 copy.167
  52.1 2.4 fusion.57
  54.8 1.4 fusion.25
  57.0 1.2 reshape.355
  58.5 4.1 gather_fusion
  62.6 2.1 bitcast_select_fusion
  64.8 2.0 fusion.81
  67.0 0.9 maximum_bitcast_fusion.1
  68.1 3.1 fusion.82
  71.5 1.2 fusion.51
  72.7 2.5 reshape.357
  75.2 1.5 exponential_reduce_fusion
  77.1 1.7 fusion.46
  78.8 0.9 fusion.24
  79.8 1.4 copy.206
  81.5 1.5 fusion.83
  83.0 1.4 maximum_bitcast_fusion
  84.4 0.6 gather_fusion.1
  85.6 1.2 pad_maximum_fusion
  87.6 1.8 reduce-window.6
  90.1 0.8 dynamic_slice.23
  90.9 0.6 convert_reduce_fusion
  91.5 24.9 %reduce-scatter.2.cloned.1.call-done = f32[128,512]{1,0:T(8,128)} async-done(((f32[128,2048]{1,0:T(8,128)}), f32[128,512]{1,0:T(8,128)}) %reduce-scatter.2.cloned.1.call-update) | async-done | bytes 262160 | tf_op jit(solution)/shard_map/reduce_scatter | solution.py:204
  116.4 1.1 multiply_reduce_fusion.1
  117.5 6.6 %psum.7 = f32[128,1]{0,1:T(1,128)S(1)} all-reduce(f32[128,1]{0,1:T(1,128)S(1)} %bitcast.241), channel_id=1, replica_groups=mesh['req'=64,'tp'=4] {'tp'}, use_global_device_ids=true, to_apply=%region_13.14 | all-reduce | flops 128 | bytes 1024 | tf_op jit(solution)/shard_map/psum | solution.py:207
  124.1 0.6 convolution_convert_fusion
  124.7 53.0 %all_to_all.10 = bf16[64,1,24,512]{3,2,1,0:T(8,128)(2,1)} all-to-all(bf16[64,1,24,512]{3,2,1,0:T(8,128)(2,1)S(1)} %bitcast.230), channel_id=1, replica_groups=mesh['req'=64,'tp'=4] {'req'}, dimensions={0} | all-to-all | bytes 3145728 | tf_op jit(solution)/shard_map/all_to_all | solution.py:214
  177.8 63.6 %all-gather.3.cloned.1.call-done = bf16[64,1,24,2048]{3,2,0,1:T(8,128)(2,1)} async-done(((bf16[64,1,24,512]{3,2,0,1:T(8,128)(2,1)}), bf16[64,1,24,2048]{3,2,0,1:T(8,128)(2,1)}) %all-gather.3.cloned.1.call-update) | async-done | bytes 6291472 | tf_op jit(solution)/shard_map/all_gather | solution.py:221
  241.4 6.0 %fusion.2 = f32[64,24,352]{2,1,0:T(8,128)S(1)} fusion(bf16[64,1,24,2048]{3,2,0,1:T(8,128)(2,1)} %all-gather.3.cloned.1.call-done, bf16[1,2048,352]{1,2,0:T(8,128)(2,1)S(1)} %copy-done.30), kind=kOutput, calls=%fused_computation.4 | convolution fusion | flops 2214592512 | bytes 9895936 | tf_op jit(solution)/shard_map/nesd,edf->nesf/dot_general | solution.py:37
  247.4 5.1 %fusion.6 = bf16[64,1,24,352]{3,2,0,1:T(8,128)(2,1)S(1)} fusion(f32[64,24,352]{2,1,0:T(8,128)S(1)} %fusion.2, bf16[64,1,24,2048]{3,2,0,1:T(8,128)(2,1)S(1)} %copy-done.29, bf16[1,2048,352]{1,2,0:T(8,128)(2,1)} %param.28), kind=kOutput, calls=%fused_computation.14 | convolution fusion | flops 2217836544 | bytes 10977280 | tf_op jit(solution)/shard_map/nesd,edf->nesf/dot_general | solution.py:38
  252.6 3.0 copy.196
  255.6 88.8 %all-gather.5.cloned.1.call-done = bf16[64,1,24,1408]{0,2,1,3:T(8,128)(2,1)} async-done(((bf16[64,1,24,352]{0,2,1,3:T(8,128)(2,1)}), bf16[64,1,24,1408]{0,2,1,3:T(8,128)(2,1)}) %all-gather.5.cloned.1.call-update) | async-done | bytes 4325392 | tf_op jit(solution)/shard_map/all_gather | solution.py:40
  344.3 10.8 %copy.197 = bf16[64,1,24,1408]{3,0,2,1:T(8,128)(2,1)} copy(bf16[64,1,24,1408]{0,2,1,3:T(8,128)(2,1)} %all-gather.5.cloned.1.call-done) | data formatting | bytes 8650752 | tf_op jit(solution)/shard_map/all_gather | solution.py:40
  355.1 4.8 %fusion.16 = bf16[64,1,24,512]{3,0,2,1:T(8,128)(2,1)S(1)} fusion(bf16[64,1,24,1408]{3,0,2,1:T(8,128)(2,1)} %copy.197, bf16[1,1408,512]{2,1,0:T(8,128)(2,1)S(1)} %copy-done.9), kind=kOutput, calls=%fused_computation.23 | convolution fusion | flops 2215378944 | bytes 7340032 | tf_op jit(solution)/shard_map/nesf,efd->nesd/dot_general | solution.py:41
  359.9 2.0 copy.198
  361.9 11.0 %all-to-all-start.1 = ((bf16[64,1,24,512]{3,2,1,0:T(8,128)(2,1)}), bf16[64,1,24,512]{3,2,1,0:T(8,128)(2,1)}, u32[]{:S(2)}, u32[]{:S(2)}) async-start(bf16[64,1,24,512]{3,2,1,0:T(8,128)(2,1)} %copy.198), calls=%async_computation.2 | async-start | bytes 3145728 | tf_op jit(solution)/shard_map/all_to_all | solution.py:65
  372.9 1.5 select_reduce_fusion
  374.5 37.4 %all-to-all-done.1 = bf16[64,1,24,512]{3,2,1,0:T(8,128)(2,1)} async-done(((bf16[64,1,24,512]{3,2,1,0:T(8,128)(2,1)}), bf16[64,1,24,512]{3,2,1,0:T(8,128)(2,1)}, u32[]{:S(2)}, u32[]{:S(2)}) %all-to-all-start.1) | async-done | bytes 1572896 | tf_op jit(solution)/shard_map/all_to_all | solution.py:65
  411.9 3.1 fusion.27
  (140 shorter events, 6.8 us)
Async XLA Ops:
  6.5 45.5 %copy-start = (bf16[2048,768]{1,0:T(8,128)(2,1)S(1)}, bf16[2048,768]{1,0:T(8,128)(2,1)}, u32[]{:S(2)}) copy-start(bf16[2048,768]{1,0:T(8,128)(2,1)} %param.20) | copy-start | bytes 9437188
  6.5 9.5 %copy-start.22 = (s32[4,3,8]{2,0,1:T(4,128)S(1)}, s32[4,3,8]{2,0,1:T(4,128)}, u32[]{:S(2)}) copy-start(s32[4,3,8]{2,0,1:T(4,128)} %param.33) | copy-start | bytes 1156
  6.5 10.1 %copy-start.21 = (f32[2048]{0:T(1024)S(1)}, f32[2048]{0:T(1024)}, u32[]{:S(2)}) copy-start(f32[2048]{0:T(1024)} %param.19) | copy-start | bytes 24580
  6.5 109.9 %reduce-scatter.2.cloned.1.call-start = ((), (), s32[]{:S(2)}) async-start(), calls=%async_computation.3 | async-start | bytes 1310720 | tf_op jit(solution)/shard_map/reduce_scatter | solution.py:204
  6.6 9.8 %copy-start.2 = (bf16[128,2048]{1,0:T(8,128)(2,1)S(1)}, bf16[128,2048]{1,0:T(8,128)(2,1)}, u32[]{:S(2)}) copy-start(bf16[128,2048]{1,0:T(8,128)(2,1)} %param.18) | copy-start | bytes 1572868
  6.6 10.0 %copy-start.31 = (bf16[2048,144]{0,1:T(8,128)(2,1)S(1)}, bf16[2048,144]{0,1:T(8,128)(2,1)}, u32[]{:S(2)}) copy-start(bf16[2048,144]{0,1:T(8,128)(2,1)} %param.21) | copy-start | bytes 1769476
  6.6 28.9 %copy-start.24 = (f32[512]{0:T(512)S(1)}, f32[512]{0:T(512)}, u32[]{:S(2)}) copy-start(f32[512]{0:T(512)} %param.22) | copy-start | bytes 6148
  9.3 28.7 %copy-start.27 = (s32[4]{0:T(128)S(1)}, s32[4]{0:T(128)}, u32[]{:S(2)}) copy-start(s32[4]{0:T(128)} %param.32) | copy-start | bytes 52
  9.3 73.7 %collective-permute-start = (bf16[1,352,512]{2,1,0:T(8,128)(2,1)}, bf16[1,352,512]{2,1,0:T(8,128)(2,1)}, u32[]{:S(2)}, u32[]{:S(2)}) collective-permute-start(bf16[1,352,512]{2,1,0:T(8,128)(2,1)} %get-tuple-element.17), channel_id=1, source_target_pairs={{0,1},{1,2},{2,3},{3,0},{4,5},{5,6},{6,7},{7,4},{8,9},{9,10},{10,1... | collective-permute-start | bytes 1081352 | tf_op jit(solution)/shard_map/ppermute | solution.py:55
  11.3 71.7 %collective-permute-start.1 = (bf16[1,352,512]{2,1,0:T(8,128)(2,1)}, bf16[1,352,512]{2,1,0:T(8,128)(2,1)}, u32[]{:S(2)}, u32[]{:S(2)}) collective-permute-start(bf16[1,352,512]{2,1,0:T(8,128)(2,1)} %get-tuple-element.19), channel_id=1, source_target_pairs={{0,2},{1,3},{2,0},{3,1},{4,6},{5,7},{6,4},{7,5},{8,10},{9,11},{10,... | collective-permute-start | bytes 1081352 | tf_op jit(solution)/shard_map/ppermute | solution.py:55
  13.8 69.2 %collective-permute-start.2 = (bf16[1,352,512]{2,1,0:T(8,128)(2,1)}, bf16[1,352,512]{2,1,0:T(8,128)(2,1)}, u32[]{:S(2)}, u32[]{:S(2)}) collective-permute-start(bf16[1,352,512]{2,1,0:T(8,128)(2,1)} %get-tuple-element.18), channel_id=1, source_target_pairs={{0,3},{1,0},{2,1},{3,2},{4,7},{5,4},{6,5},{7,6},{8,11},{9,8},{10,9... | collective-permute-start | bytes 1081352 | tf_op jit(solution)/shard_map/ppermute | solution.py:55
  16.6 21.4 %copy-start.26 = (f32[128]{0:T(128)}, f32[128]{0:T(128)S(1)}, u32[]{:S(2)}) copy-start(f32[128]{0:T(128)S(1)} %add_rsqrt_fusion.1) | copy-start | bytes 1540
  54.5 1.7 copy-start.11
  54.5 1.7 copy-start.12
  56.3 1.9 copy-start.25
  56.3 1.8 copy-start.28
  56.5 6.2 %copy-start.5 = (bf16[128,4,576]{2,0,1:T(8,128)(2,1)}, bf16[128,4,576]{2,0,1:T(8,128)(2,1)S(1)}, u32[]{:S(2)}) copy-start(bf16[128,4,576]{2,0,1:T(8,128)(2,1)S(1)} %pad_maximum_fusion.1) | copy-start | bytes 1769476
  62.6 2.1 copy-start.4
  64.7 2.3 copy-start.13
  64.7 2.3 copy-start.14
  64.7 2.3 copy-start.15
  64.7 2.3 copy-start.16
  64.7 2.3 copy-start.17
  64.7 2.3 copy-start.18
  64.8 2.3 copy-start.19
  66.8 1.4 copy-start.32
  68.1 3.1 copy-start.6
  71.3 5.8 %slice-start = ((bf16[4,4,8,4,576]{4,2,0,3,1:T(8,128)(2,1)}), bf16[4,4,8,4,512]{4,2,0,3,1:T(8,128)(2,1)S(1)}, s32[]{:S(2)}) async-start(bf16[4,4,8,4,576]{4,2,0,3,1:T(8,128)(2,1)} %copy-done.6), calls=%async_computation.6 | async-start | bytes 1048576 | tf_op jit(solution)/shard_map/slice | solution.py:176
  77.1 1.7 copy-start.10
  79.7 1.8 copy-start.7
  81.2 1.8 copy-start.8
  85.6 1.5 copy-start.3
  85.6 1.6 copy-start.20
  86.8 154.6 %all-gather.3.cloned.1.call-start = ((), (), s32[]{:S(2)}) async-start(), calls=%async_computation.4 | async-start | bytes 7864320 | tf_op jit(solution)/shard_map/all_gather | solution.py:221
  124.7 116.7 %copy-start.30 = (bf16[1,2048,352]{1,2,0:T(8,128)(2,1)S(1)}, bf16[1,2048,352]{1,2,0:T(8,128)(2,1)}, u32[]{:S(2)}) copy-start(bf16[1,2048,352]{1,2,0:T(8,128)(2,1)} %param.27) | copy-start | bytes 4325380
  177.7 166.6 %all-gather.5.cloned.1.call-start = ((), (), s32[]{:S(2)}) async-start(), calls=%async_computation.5 | async-start | bytes 10813440 | tf_op jit(solution)/shard_map/all_gather | solution.py:40
  241.4 6.0 %copy-start.29 = (bf16[64,1,24,2048]{3,2,0,1:T(8,128)(2,1)S(1)}, bf16[64,1,24,2048]{3,2,0,1:T(8,128)(2,1)}, u32[]{:S(2)}) copy-start(bf16[64,1,24,2048]{3,2,0,1:T(8,128)(2,1)} %all-gather.3.cloned.1.call-done) | copy-start | bytes 18874372
  255.6 99.5 %copy-start.9 = (bf16[1,1408,512]{2,1,0:T(8,128)(2,1)S(1)}, bf16[1,1408,512]{2,1,0:T(8,128)(2,1)}, u32[]{:S(2)}) copy-start(bf16[1,1408,512]{2,1,0:T(8,128)(2,1)} %pad_maximum_fusion) | copy-start | bytes 4325380
  361.9 11.0 %copy-start.23 = (f32[128,6]{0,1:T(8,128)S(1)}, f32[128,6]{0,1:T(8,128)}, u32[]{:S(2)}) copy-start(f32[128,6]{0,1:T(8,128)} %param.35) | copy-start | bytes 9220
  361.9 49.9 %all-to-all-start.1 = ((bf16[64,1,24,512]{3,2,1,0:T(8,128)(2,1)}), bf16[64,1,24,512]{3,2,1,0:T(8,128)(2,1)}, u32[]{:S(2)}, u32[]{:S(2)}) async-start(bf16[64,1,24,512]{3,2,1,0:T(8,128)(2,1)} %copy.198), calls=%async_computation.2 | async-start | bytes 3145728 | tf_op jit(solution)/shard_map/all_to_all | solution.py:65
  372.9 42.0 %copy-start.1 = (bf16[2048,768]{1,0:T(8,128)(2,1)S(1)}, bf16[2048,768]{1,0:T(8,128)(2,1)}, u32[]{:S(2)}) copy-start(bf16[2048,768]{1,0:T(8,128)(2,1)} %param.20) | copy-start | bytes 9437188
Sparse Core Ops, SparseCore 0:
  86.9 29.4 reduce-scatter.1
  177.8 63.5 all-gather.2
  255.7 88.5 all-gather.4

commit v5 on v4

--- a/solution.py
+++ b/solution.py
@@ -37,9 +37,9 @@
     gate_val = jnp.einsum("nesd,edf->nesf", arrived, gate_w, preferred_element_type=jnp.float32)
     up_val = jnp.einsum("nesd,edf->nesf", arrived, up_w, preferred_element_type=jnp.float32)
     active = (jax.nn.silu(gate_val) * up_val).astype(jnp.bfloat16)
-    active_all = lax.all_gather(active, "tp", axis=3, tiled=True)
+    active_all = lax.all_gather(active, "tp", axis=0)
     return jnp.einsum(
-        "nesf,efd->nesd", active_all, down_cols, preferred_element_type=jnp.float32
+        "tnesf,etfd->nesd", active_all, down_cols, preferred_element_type=jnp.float32
     ).astype(jnp.bfloat16)
 
 
@@ -56,9 +56,8 @@
                 piece, "tp", [(s, (s + shift) % tp_count) for s in range(tp_count)]
             )
         pieces[shift] = piece
-    stacked = jnp.stack(pieces, axis=0)
-    ordered = jnp.take(stacked, (tp_index - jnp.arange(tp_count)) % tp_count, axis=0)
-    return jnp.concatenate([ordered[i] for i in range(tp_count)], axis=1)
+    stacked = jnp.stack(pieces, axis=1)
+    return jnp.take(stacked, (tp_index - jnp.arange(tp_count)) % tp_count, axis=1)
 
 
 def send_home(shares):

time: 423 us -> 377 us (0.89)
  waiting for transfers between devices: 215 us -> 182 us
  local copies, waits for them, and re-layouts: 35.4 us -> 24.8 us
    all_gather x1, waiting for transfers between devices: 88.8 us -> 56 us  [expert_math(): active_all = lax.all_gather(active, 'tp', axis=0)]
    all_gather x1, local copies, waits for them, and re-layouts: 10.8 us -> 3.17 us  [expert_math(): active_all = lax.all_gather(active, 'tp', axis=0)]
  transfers between devices with their start and end apart: 7 -> 7, of which waited for: 4 -> 4; matrix products, arithmetic and copies ran while one was open for 13% -> 15% of each run, Pallas kernels for 0% -> 0%
where the time goes in v5:
time: 377 us; the launch traced here: 376 us
  waiting for transfers between devices  182 us (48%)
  blocking collectives  78.5 us (21%)
  matrix products  39.6 us (11%)
  local copies, waits for them, and re-layouts  24.8 us (7%)
  other arithmetic  20.3 us (5%)
  starting transfers between devices  16.9 us (4%)
  between operations  13.9 us (4%)
    all_gather x1, waiting for transfers between devices, local(): arrived = lax.all_gather(arrived_cols, 'tp', axis=3, tiled=True)  63.6 us
    all_gather x1, waiting for transfers between devices, expert_math(): active_all = lax.all_gather(active, 'tp', axis=0)  56 us
    all_to_all x1, blocking collectives, local(): lax.all_to_all(placed.reshape(req_count, EXP_DEV, capacity, col_share), '...  52.9 us
    all_to_all x1, waiting for transfers between devices, send_home(): lax.all_to_all(shares, 'req', split_axis=0, concat_axis=0, tiled=True)  37.4 us
    reduce_scatter x1, waiting for transfers between devices, local(): lax.psum_scatter(attn_part, 'tp', scatter_dimension=1, tiled=True)  24.9 us
    all_gather x1, blocking collectives, local(): kv_all = lax.all_gather(kv_part, 'tp', axis=1, tiled=True)  19 us
    all_to_all x1, starting transfers between devices, send_home(): lax.all_to_all(shares, 'req', split_axis=0, concat_axis=0, tiled=True)  11 us
    dot_general x10, matrix products, local(): jnp.einsum('rba,rad->rbd', lineage, fresh[:, earlier], precision=highest)  7.9 us
  transfers between devices with their start and end apart: 7, of which 4 were waited for; matrix products, arithmetic and copies ran while one was open for 15% of the time, Pallas kernels for 0%

profile of v5, /device:TPU:1, one launch (start us, length us, event | category | flops | bytes accessed | tf_op | source)
XLA Modules:
  0.0 376.0 jit_solution(12474010976081259075)
XLA Ops:
  6.6 2.6 dynamic-slice_bitcast_fusion
  9.3 2.0 collective-permute-start
  11.3 2.5 collective-permute-start.1
  13.8 1.2 collective-permute-start.2
  14.9 0.6 multiply_power_fusion
  16.5 19.0 %all_gather.12 = f32[128,576]{0,1:T(8,128)S(1)} all-gather(f32[128,144]{0,1:T(8,128)S(1)} %fusion.54), channel_id=1, replica_groups=mesh['req'=64,'tp'=4] {'tp'}, dimensions={1}, use_global_device_ids=true | all-gather | bytes 368640 | tf_op jit(solution)/shard_map/all_gather | solution.py:114
  35.5 0.8 multiply_convert_fusion.2
  36.3 1.7 copy.159
  38.2 0.8 multiply_cosine_fusion
  39.6 1.0 pad_maximum_fusion.2
  40.6 0.8 fusion.33
  41.5 0.8 fusion.30
  42.3 0.8 fusion.34
  43.2 0.8 fusion.26
  44.0 0.8 fusion.28
  44.8 0.8 fusion.31
  45.6 0.8 fusion.35
  46.4 0.5 iota_compare_fusion.6
  46.8 0.6 iota_multiply_fusion
  47.4 0.7 iota_compare_fusion.4
  48.2 0.6 fusion.77
  48.7 0.8 fusion.32
  49.5 0.8 fusion.29
  50.3 0.8 fusion.27
  51.1 0.7 copy.153
  51.8 0.7 copy.155
  52.6 2.4 fusion.55
  55.3 1.4 fusion.23
  57.0 0.5 copy.156
  57.5 1.2 reshape.355
  59.0 4.1 %gather_fusion = bf16[32,64,576]{2,1,0:T(8,128)(2,1)} fusion(bf16[32,64,576]{2,1,0:T(8,128)(2,1)} %param.30, s32[1024]{0:T(1024)S(1)} %pad_clamp_fusion.1), kind=kCustom, calls=%fused_computation | custom fusion | bytes 4718720 | tf_op jit(solution)/shard_map/jit(_take)/gather | solution.py:124
  63.1 2.1 bitcast_select_fusion
  65.3 2.0 fusion.79
  67.5 0.9 maximum_bitcast_fusion.1
  68.6 3.1 fusion.80
  72.0 1.2 fusion.49
  73.2 2.5 reshape.357
  75.7 1.5 exponential_reduce_fusion
  77.6 1.7 fusion.44
  79.3 0.9 fusion.22
  80.3 1.4 copy.192
  82.0 1.5 fusion.81
  83.5 1.4 maximum_bitcast_fusion
  84.9 0.6 gather_fusion.1
  85.6 1.4 bitcast_select_fusion.1
  87.8 1.8 reduce-window.6
  90.3 0.8 dynamic_slice.23
  91.1 0.6 convert_reduce_fusion
  91.7 24.9 %reduce-scatter.2.cloned.1.call-done = f32[128,512]{1,0:T(8,128)} async-done(((f32[128,2048]{1,0:T(8,128)}), f32[128,512]{1,0:T(8,128)}) %reduce-scatter.2.cloned.1.call-update) | async-done | bytes 262160 | tf_op jit(solution)/shard_map/reduce_scatter | solution.py:203
  116.6 1.1 multiply_reduce_fusion.1
  117.7 6.7 %psum.7 = f32[128,1]{0,1:T(1,128)S(1)} all-reduce(f32[128,1]{0,1:T(1,128)S(1)} %bitcast.238), channel_id=1, replica_groups=mesh['req'=64,'tp'=4] {'tp'}, use_global_device_ids=true, to_apply=%region_13.14 | all-reduce | flops 128 | bytes 1024 | tf_op jit(solution)/shard_map/psum | solution.py:206
  124.3 0.6 convolution_convert_fusion
  125.0 52.9 %all_to_all.10 = bf16[64,1,24,512]{3,2,1,0:T(8,128)(2,1)} all-to-all(bf16[64,1,24,512]{3,2,1,0:T(8,128)(2,1)S(1)} %bitcast.226), channel_id=1, replica_groups=mesh['req'=64,'tp'=4] {'req'}, dimensions={0} | all-to-all | bytes 3145728 | tf_op jit(solution)/shard_map/all_to_all | solution.py:213
  178.0 63.6 %all-gather.4.cloned.1.call-done = bf16[64,1,24,2048]{3,2,0,1:T(8,128)(2,1)} async-done(((bf16[64,1,24,512]{3,2,0,1:T(8,128)(2,1)}), bf16[64,1,24,2048]{3,2,0,1:T(8,128)(2,1)}) %all-gather.4.cloned.1.call-update) | async-done | bytes 6291472 | tf_op jit(solution)/shard_map/all_gather | solution.py:220
  241.6 6.0 %fusion.2 = f32[64,24,352]{2,1,0:T(8,128)S(1)} fusion(bf16[64,1,24,2048]{3,2,0,1:T(8,128)(2,1)} %all-gather.4.cloned.1.call-done, bf16[1,2048,352]{1,2,0:T(8,128)(2,1)S(1)} %copy-done.30), kind=kOutput, calls=%fused_computation.4 | convolution fusion | flops 2214592512 | bytes 9895936 | tf_op jit(solution)/shard_map/nesd,edf->nesf/dot_general | solution.py:37
  247.6 4.8 %fusion.15 = bf16[64,1,24,352]{3,2,1,0:T(8,128)(2,1)} fusion(bf16[1,2048,352]{1,2,0:T(8,128)(2,1)S(1)} %copy-done.31, bf16[64,1,24,2048]{3,2,0,1:T(8,128)(2,1)S(1)} %copy-done.29, f32[64,24,352]{2,1,0:T(8,128)S(1)} %fusion.2), kind=kOutput, calls=%fused_computation.27 | convolution fusion | flops 2217836544 | bytes 10977280 | tf_op jit(solution)/shard_map/nesd,edf->nesf/dot_general | solution.py:38
  252.5 56.0 %all-gather.6.cloned.1.call-done = bf16[256,1,24,352]{3,2,1,0:T(8,128)(2,1)} async-done(((bf16[64,1,24,352]{3,2,1,0:T(8,128)(2,1)}), bf16[256,1,24,352]{3,2,1,0:T(8,128)(2,1)}) %all-gather.6.cloned.1.call-update) | async-done | bytes 4325392 | tf_op jit(solution)/shard_map/all_gather | solution.py:40
  308.5 3.2 copy.182
  311.7 2.7 fusion.11
  314.4 2.0 copy.183
  316.4 11.0 %all-to-all-start.1 = ((bf16[64,1,24,512]{3,2,1,0:T(8,128)(2,1)}), bf16[64,1,24,512]{3,2,1,0:T(8,128)(2,1)}, u32[]{:S(2)}, u32[]{:S(2)}) async-start(bf16[64,1,24,512]{3,2,1,0:T(8,128)(2,1)} %copy.183), calls=%async_computation.2 | async-start | bytes 3145728 | tf_op jit(solution)/shard_map/all_to_all | solution.py:64
  327.4 1.5 select_reduce_fusion
  329.0 37.4 %all-to-all-done.1 = bf16[64,1,24,512]{3,2,1,0:T(8,128)(2,1)} async-done(((bf16[64,1,24,512]{3,2,1,0:T(8,128)(2,1)}), bf16[64,1,24,512]{3,2,1,0:T(8,128)(2,1)}, u32[]{:S(2)}, u32[]{:S(2)}) %all-to-all-start.1) | async-done | bytes 1572896 | tf_op jit(solution)/shard_map/all_to_all | solution.py:64
  366.4 3.1 fusion.25
  (137 shorter events, 5.8 us)
Async XLA Ops:
  6.5 46.0 %copy-start = (bf16[2048,768]{1,0:T(8,128)(2,1)S(1)}, bf16[2048,768]{1,0:T(8,128)(2,1)}, u32[]{:S(2)}) copy-start(bf16[2048,768]{1,0:T(8,128)(2,1)} %param.20) | copy-start | bytes 9437188
  6.5 9.0 %copy-start.22 = (s32[4,3,8]{2,0,1:T(4,128)S(1)}, s32[4,3,8]{2,0,1:T(4,128)}, u32[]{:S(2)}) copy-start(s32[4,3,8]{2,0,1:T(4,128)} %param.33) | copy-start | bytes 1156
  6.5 9.5 %copy-start.21 = (f32[2048]{0:T(1024)S(1)}, f32[2048]{0:T(1024)}, u32[]{:S(2)}) copy-start(f32[2048]{0:T(1024)} %param.19) | copy-start | bytes 24580
  6.5 110.1 %reduce-scatter.2.cloned.1.call-start = ((), (), s32[]{:S(2)}) async-start(), calls=%async_computation.3 | async-start | bytes 1310720 | tf_op jit(solution)/shard_map/reduce_scatter | solution.py:203
  6.6 9.2 %copy-start.2 = (bf16[128,2048]{1,0:T(8,128)(2,1)S(1)}, bf16[128,2048]{1,0:T(8,128)(2,1)}, u32[]{:S(2)}) copy-start(bf16[128,2048]{1,0:T(8,128)(2,1)} %param.18) | copy-start | bytes 1572868
  6.6 9.4 %copy-start.32 = (bf16[2048,144]{0,1:T(8,128)(2,1)S(1)}, bf16[2048,144]{0,1:T(8,128)(2,1)}, u32[]{:S(2)}) copy-start(bf16[2048,144]{0,1:T(8,128)(2,1)} %param.21) | copy-start | bytes 1769476
  6.6 28.9 %copy-start.24 = (f32[512]{0:T(512)S(1)}, f32[512]{0:T(512)}, u32[]{:S(2)}) copy-start(f32[512]{0:T(512)} %param.22) | copy-start | bytes 6148
  9.3 28.7 %copy-start.26 = (s32[4]{0:T(128)S(1)}, s32[4]{0:T(128)}, u32[]{:S(2)}) copy-start(s32[4]{0:T(128)} %param.32) | copy-start | bytes 52
  9.3 74.2 %collective-permute-start = (bf16[1,352,512]{2,1,0:T(8,128)(2,1)}, bf16[1,352,512]{2,1,0:T(8,128)(2,1)}, u32[]{:S(2)}, u32[]{:S(2)}) collective-permute-start(bf16[1,352,512]{2,1,0:T(8,128)(2,1)} %get-tuple-element.14), channel_id=1, source_target_pairs={{0,1},{1,2},{2,3},{3,0},{4,5},{5,6},{6,7},{7,4},{8,9},{9,10},{10,1... | collective-permute-start | bytes 1081352 | tf_op jit(solution)/shard_map/ppermute | solution.py:55
  11.3 72.2 %collective-permute-start.1 = (bf16[1,352,512]{2,1,0:T(8,128)(2,1)}, bf16[1,352,512]{2,1,0:T(8,128)(2,1)}, u32[]{:S(2)}, u32[]{:S(2)}) collective-permute-start(bf16[1,352,512]{2,1,0:T(8,128)(2,1)} %get-tuple-element.16), channel_id=1, source_target_pairs={{0,2},{1,3},{2,0},{3,1},{4,6},{5,7},{6,4},{7,5},{8,10},{9,11},{10,... | collective-permute-start | bytes 1081352 | tf_op jit(solution)/shard_map/ppermute | solution.py:55
  13.8 69.7 %collective-permute-start.2 = (bf16[1,352,512]{2,1,0:T(8,128)(2,1)}, bf16[1,352,512]{2,1,0:T(8,128)(2,1)}, u32[]{:S(2)}, u32[]{:S(2)}) collective-permute-start(bf16[1,352,512]{2,1,0:T(8,128)(2,1)} %get-tuple-element.15), channel_id=1, source_target_pairs={{0,3},{1,0},{2,1},{3,2},{4,7},{5,4},{6,5},{7,6},{8,11},{9,8},{10,9... | collective-permute-start | bytes 1081352 | tf_op jit(solution)/shard_map/ppermute | solution.py:55
  55.0 1.7 copy-start.11
  55.0 1.7 copy-start.12
  56.8 1.9 copy-start.25
  56.8 1.8 copy-start.28
  56.9 6.2 %copy-start.5 = (bf16[128,4,576]{2,0,1:T(8,128)(2,1)}, bf16[128,4,576]{2,0,1:T(8,128)(2,1)S(1)}, u32[]{:S(2)}) copy-start(bf16[128,4,576]{2,0,1:T(8,128)(2,1)S(1)} %pad_maximum_fusion) | copy-start | bytes 1769476
  63.1 2.1 copy-start.4
  65.2 2.3 copy-start.13
  65.2 2.3 copy-start.14
  65.2 2.3 copy-start.15
  65.2 2.3 copy-start.16
  65.2 2.3 copy-start.17
  65.2 2.3 copy-start.18
  65.2 2.3 copy-start.19
  67.3 1.4 copy-start.33
  68.6 3.1 copy-start.6
  71.8 5.8 %slice-start = ((bf16[4,4,8,4,576]{4,2,0,3,1:T(8,128)(2,1)}), bf16[4,4,8,4,512]{4,2,0,3,1:T(8,128)(2,1)S(1)}, s32[]{:S(2)}) async-start(bf16[4,4,8,4,576]{4,2,0,3,1:T(8,128)(2,1)} %copy-done.6), calls=%async_computation.6 | async-start | bytes 1048576 | tf_op jit(solution)/shard_map/slice | solution.py:175
  77.6 1.7 copy-start.10
  79.3 2.4 copy-start.27
  80.2 1.8 copy-start.7
  81.7 1.8 copy-start.8
  85.6 1.7 copy-start.3
  85.6 1.8 copy-start.20
  87.0 154.6 %all-gather.4.cloned.1.call-start = ((), (), s32[]{:S(2)}) async-start(), calls=%async_computation.4 | async-start | bytes 7864320 | tf_op jit(solution)/shard_map/all_gather | solution.py:220
  125.0 116.6 %copy-start.30 = (bf16[1,2048,352]{1,2,0:T(8,128)(2,1)S(1)}, bf16[1,2048,352]{1,2,0:T(8,128)(2,1)}, u32[]{:S(2)}) copy-start(bf16[1,2048,352]{1,2,0:T(8,128)(2,1)} %param.27) | copy-start | bytes 4325380
  177.9 69.7 %copy-start.31 = (bf16[1,2048,352]{1,2,0:T(8,128)(2,1)S(1)}, bf16[1,2048,352]{1,2,0:T(8,128)(2,1)}, u32[]{:S(2)}) copy-start(bf16[1,2048,352]{1,2,0:T(8,128)(2,1)} %param.28) | copy-start | bytes 4325380
  177.9 130.6 %all-gather.6.cloned.1.call-start = ((), (), s32[]{:S(2)}) async-start(), calls=%async_computation.5 | async-start | bytes 5898240 | tf_op jit(solution)/shard_map/all_gather | solution.py:40
  241.6 6.0 %copy-start.29 = (bf16[64,1,24,2048]{3,2,0,1:T(8,128)(2,1)S(1)}, bf16[64,1,24,2048]{3,2,0,1:T(8,128)(2,1)}, u32[]{:S(2)}) copy-start(bf16[64,1,24,2048]{3,2,0,1:T(8,128)(2,1)} %all-gather.4.cloned.1.call-done) | copy-start | bytes 18874372
  252.5 59.2 %copy-start.9 = (bf16[1,4,352,512]{3,2,1,0:T(8,128)(2,1)S(1)}, bf16[1,4,352,512]{3,2,1,0:T(8,128)(2,1)}, u32[]{:S(2)}) copy-start(bf16[1,4,352,512]{3,2,1,0:T(8,128)(2,1)} %bitcast_select_fusion.1) | copy-start | bytes 4325380
  316.4 11.0 %copy-start.23 = (f32[128,6]{0,1:T(8,128)S(1)}, f32[128,6]{0,1:T(8,128)}, u32[]{:S(2)}) copy-start(f32[128,6]{0,1:T(8,128)} %param.35) | copy-start | bytes 9220
  316.4 49.9 %all-to-all-start.1 = ((bf16[64,1,24,512]{3,2,1,0:T(8,128)(2,1)}), bf16[64,1,24,512]{3,2,1,0:T(8,128)(2,1)}, u32[]{:S(2)}, u32[]{:S(2)}) async-start(bf16[64,1,24,512]{3,2,1,0:T(8,128)(2,1)} %copy.183), calls=%async_computation.2 | async-start | bytes 3145728 | tf_op jit(solution)/shard_map/all_to_all | solution.py:64
  327.4 42.0 %copy-start.1 = (bf16[2048,768]{1,0:T(8,128)(2,1)S(1)}, bf16[2048,768]{1,0:T(8,128)(2,1)}, u32[]{:S(2)}) copy-start(bf16[2048,768]{1,0:T(8,128)(2,1)} %param.20) | copy-start | bytes 9437188
Sparse Core Ops, SparseCore 0:
  87.1 29.4 reduce-scatter.1
  178.0 63.5 all-gather.3
  252.6 55.8 all-gather.5

commit v6 on v5

--- a/solution.py
+++ b/solution.py
@@ -112,6 +112,7 @@
     )
     kv_part = jnp.dot(normed, w_latent, preferred_element_type=jnp.float32)
     kv_all = lax.all_gather(kv_part, "tp", axis=1, tiled=True)
+    kv_all, down_late = lax.optimization_barrier((kv_all, w_down))
     new_lat = kv_all[:, :LATENT] * rms_scale(kv_all[:, :LATENT]) * kv_gain
     new_rope = rotate(kv_all[:, LATENT:], cos_val, sin_val)
     new_keys = jnp.concatenate([new_lat, new_rope], axis=1).astype(jnp.bfloat16)
@@ -120,11 +121,15 @@
         jnp.bfloat16
     )
     query_key = jnp.concatenate([q_lat, q_rope], axis=2)
-    pool_index = (jnp.arange(req_local, dtype=jnp.int32) * PAGES)[:, None] + page_table
-    cache_keys = jnp.take(latent_cache, pool_index.reshape(-1), axis=0).reshape(
-        req_local, max_len, LATENT + ROPE
-    )
-    live_mask = jnp.arange(max_len, dtype=jnp.int32)[None, :] < cache_len[:, None]
+    cache_keys = latent_cache.reshape(req_local, max_len, LATENT + ROPE)
+    page_hot = page_table[:, :, None] == jnp.arange(PAGES, dtype=jnp.int32)[None, None, :]
+    logical_page = jnp.sum(
+        jnp.where(page_hot, jnp.arange(PAGES, dtype=jnp.int32)[None, :, None], 0), axis=1
+    )
+    logical_pos = (
+        logical_page[:, :, None] * PAGE + jnp.arange(PAGE, dtype=jnp.int32)[None, None, :]
+    ).reshape(req_local, max_len)
+    live_mask = logical_pos < cache_len[:, None]
     score_scale = (NOPE + ROPE) ** (-0.5)
     grouped = query_key.reshape(req_local, STEPS * BEAMS * heads_local, LATENT + ROPE)
     s_cache = (
@@ -134,25 +139,27 @@
     s_cache = jnp.where(live_mask[:, None, :], s_cache, -jnp.inf).reshape(
         req_local, STEPS, BEAMS, heads_local, max_len
     )
-    fresh = new_keys.reshape(req_local, STEPS, BEAMS, LATENT + ROPE).astype(jnp.float32)
-    parent_hot = (parents[..., None] == jnp.arange(BEAMS, dtype=jnp.int32)).astype(jnp.float32)
-    identity = jnp.broadcast_to(jnp.eye(BEAMS, dtype=jnp.float32), (req_local, BEAMS, BEAMS))
-    tail_rows = []
+    fresh = new_keys.reshape(req_local, STEPS, BEAMS, LATENT + ROPE)
+    beam_ids = jnp.arange(BEAMS, dtype=jnp.int32)
+    lineage_rows = []
     for step_index in range(STEPS):
-        lineage = identity
+        lineage = jnp.broadcast_to(beam_ids[None, :], (req_local, BEAMS))
         pieces = [None] * STEPS
         for earlier in range(step_index, -1, -1):
-            pieces[earlier] = jnp.einsum(
-                "rba,rad->rbd", lineage, fresh[:, earlier], precision=highest
-            )
+            pieces[earlier] = lineage
             if earlier > 0:
-                lineage = jnp.einsum(
-                    "rba,rac->rbc", lineage, parent_hot[:, earlier - 1], precision=highest
+                lineage_hot = lineage[:, :, None] == beam_ids[None, None, :]
+                lineage = jnp.sum(
+                    jnp.where(lineage_hot, parents[:, earlier - 1][:, None, :], 0), axis=2
                 )
         for later in range(step_index + 1, STEPS):
-            pieces[later] = jnp.zeros_like(pieces[0])
-        tail_rows.append(jnp.stack(pieces, axis=2))
-    tail_keys = jnp.stack(tail_rows, axis=1).astype(jnp.bfloat16)
+            pieces[later] = jnp.full((req_local, BEAMS), -1, jnp.int32)
+        lineage_rows.append(jnp.stack(pieces, axis=2))
+    lineage_all = jnp.stack(lineage_rows, axis=1)
+    pick = (lineage_all[..., None] == beam_ids).astype(jnp.bfloat16)
+    tail_keys = jnp.einsum(
+        "rsbja,rjad->rsbjd", pick, fresh, preferred_element_type=jnp.float32
+    ).astype(jnp.bfloat16)
     queries_tail = query_key.reshape(req_local, STEPS, BEAMS, heads_local, LATENT + ROPE)
     s_tail = (
         jnp.einsum(
@@ -199,7 +206,7 @@
     weight_rows = jnp.sum(jnp.where(slot_hot, route_weights[:, :, None], 0.0), axis=1)
     tp_index = lax.axis_index("tp")
     col_start = tp_index * col_share
-    attn_part, down_cols = lax.optimization_barrier((attn_part, down_by_columns(w_down)))
+    attn_part, down_cols = lax.optimization_barrier((attn_part, down_by_columns(down_late)))
     attn_cols = lax.psum_scatter(attn_part, "tp", scatter_dimension=1, tiled=True)
     hidden_cols = lax.dynamic_slice_in_dim(hidden_f, col_start, col_share, 1)
     resid_cols = hidden_cols + attn_cols

time: 377 us -> 374 us (level)
  local copies, waits for them, and re-layouts: 24.8 us -> 33.7 us
  blocking collectives: 78.5 us -> 70.8 us
    dot_general x16 -> x0, matrix products: 8.71 us -> none  [the longest x10 7.9 us: local(): jnp.einsum('rba,rad->rbd', lineage, fresh[:, earlier], precision=highest)]
    all_gather x1, blocking collectives: 19 us -> 11.2 us  [local(): kv_all = lax.all_gather(kv_part, 'tp', axis=1, tiled=True)]
    gather x1 -> x0, local copies, waits for them, and re-layouts: 4.11 us -> none  [local(): jnp.take(latent_cache, pool_index.reshape(-1), axis=0)]
    unnamed x71 -> x45, local copies, waits for them, and re-layouts: 0.53 us -> 4.41 us
where the time goes in v6:
time: 374 us; the launch traced here: 372 us
  waiting for transfers between devices  180 us (48%)
  blocking collectives  70.8 us (19%)
  matrix products  38.6 us (10%)
  local copies, waits for them, and re-layouts  33.7 us (9%)
  other arithmetic  21.6 us (6%)
  starting transfers between devices  14.3 us (4%)
  between operations  13.5 us (4%)
    all_gather x1, waiting for transfers between devices, local(): arrived = lax.all_gather(arrived_cols, 'tp', axis=3, tiled=True)  63.6 us
    all_gather x1, waiting for transfers between devices, expert_math(): active_all = lax.all_gather(active, 'tp', axis=0)  56 us
    all_to_all x1, blocking collectives, local(): lax.all_to_all(placed.reshape(req_count, EXP_DEV, capacity, col_share), '...  53 us
    all_to_all x1, waiting for transfers between devices, send_home(): lax.all_to_all(shares, 'req', split_axis=0, concat_axis=0, tiled=True)  37.4 us
    reduce_scatter x1, waiting for transfers between devices, local(): lax.psum_scatter(attn_part, 'tp', scatter_dimension=1, tiled=True)  22.7 us
    all_gather x1, blocking collectives, local(): kv_all = lax.all_gather(kv_part, 'tp', axis=1, tiled=True)  11.2 us
    all_to_all x1, starting transfers between devices, send_home(): lax.all_to_all(shares, 'req', split_axis=0, concat_axis=0, tiled=True)  11 us
  transfers between devices with their start and end apart: 7, of which 4 were waited for; matrix products, arithmetic and copies ran while one was open for 15% of the time, Pallas kernels for 0%

profile of v6, /device:TPU:1, one launch (start us, length us, event | category | flops | bytes accessed | tf_op | source)
XLA Modules:
  0.0 372.5 jit_solution(3719212597073300574)
XLA Ops:
  6.5 1.4 multiply_reduce_fusion
  7.9 1.6 fusion.53
  9.6 11.2 %all_gather.12 = f32[128,576]{0,1:T(8,128)S(1)} all-gather(f32[128,144]{0,1:T(8,128)S(1)} %fusion.53), channel_id=1, replica_groups=mesh['req'=64,'tp'=4] {'tp'}, dimensions={1}, use_global_device_ids=true | all-gather | bytes 368640 | tf_op jit(solution)/shard_map/all_gather | solution.py:114
  20.8 2.5 dynamic-slice_bitcast_fusion
  23.2 0.8 collective-permute-start
  24.1 2.4 collective-permute-start.1
  26.5 0.5 iota_compare_fusion.9
  27.3 0.2 select_reduce_fusion.5
  27.5 0.3 select_reduce_fusion.6
  28.1 0.6 copy.177
  28.8 0.8 multiply_convert_fusion.2
  29.6 1.7 copy.170
  31.6 0.7 copy.171
  32.3 0.7 copy.172
  33.0 0.7 copy.164
  33.8 0.7 copy.166
  34.5 2.4 fusion.54
  36.9 0.6 fusion.64
  37.5 1.7 copy.205
  39.2 1.7 copy.206
  40.9 1.4 fusion.25
  42.3 1.1 subtract_convert_fusion
  43.5 0.8 copy-done.2
  44.4 1.3 copy.167
  45.7 2.2 reshape.339
  48.4 4.0 %fusion.65 = (f32[4,128]{1,0:T(4,128)S(1)}, f32[4,128,512]{2,1,0:T(8,128)}) fusion(bf16[4,128,576]{2,1,0:T(8,128)(2,1)} %reshape.339, bf16[4,512,576]{2,1,0:T(8,128)(2,1)} %bitcast.185, pred[4,512]{1,0:T(4,128)(4,1)S(1)} %add_compare_fusion), kind=kOutput, calls=%fused_computation.145 | convolution fusion | flops 302775808 | bytes 4001792 | tf_op jit(solution)/shard_map/rqd,rld->rql/dot_general | solution.py:136
  52.5 0.4 fusion.24
  52.9 0.9 slice.69
  53.8 1.7 fusion.66
  55.6 0.2 copy.180
  55.7 1.2 fusion.43
  56.9 2.6 reshape.341
  59.5 1.5 exponential_reduce_fusion
  61.2 0.2 copy.182
  61.3 1.9 fusion.36
  63.3 2.1 fusion.23
  65.5 0.8 copy.186
  66.3 2.1 copy.204
  68.4 1.5 convolution_convert_fusion.2
  69.9 3.1 fusion.67
  73.0 2.5 maximum_bitcast_fusion
  75.5 3.2 gather_fusion
  78.7 2.7 bitcast_select_fusion
  81.5 2.1 convert_element_type.76
  84.1 1.8 reduce-window.6
  85.9 0.3 slice_reduce_fusion
  86.5 0.8 dynamic_slice.23
  87.3 1.5 convert_reduce_fusion
  88.8 22.7 %reduce-scatter.2.cloned.1.call-done = f32[128,512]{1,0:T(8,128)} async-done(((f32[128,2048]{1,0:T(8,128)}), f32[128,512]{1,0:T(8,128)}) %reduce-scatter.2.cloned.1.call-update) | async-done | bytes 262160 | tf_op jit(solution)/shard_map/reduce_scatter | solution.py:210
  111.5 1.1 multiply_reduce_fusion.1
  112.7 6.6 %psum.7 = f32[128,1]{0,1:T(1,128)S(1)} all-reduce(f32[128,1]{0,1:T(1,128)S(1)} %bitcast.205), channel_id=1, replica_groups=mesh['req'=64,'tp'=4] {'tp'}, use_global_device_ids=true, to_apply=%region_20.21 | all-reduce | flops 128 | bytes 1024 | tf_op jit(solution)/shard_map/psum | solution.py:213
  119.3 1.8 convolution_convert_fusion
  121.1 53.0 %all_to_all.10 = bf16[64,1,24,512]{3,2,1,0:T(8,128)(2,1)} all-to-all(bf16[64,1,24,512]{3,2,1,0:T(8,128)(2,1)S(1)} %bitcast.183), channel_id=1, replica_groups=mesh['req'=64,'tp'=4] {'req'}, dimensions={0} | all-to-all | bytes 3145728 | tf_op jit(solution)/shard_map/all_to_all | solution.py:220
  174.2 63.6 %all-gather.4.cloned.1.call-done = bf16[64,1,24,2048]{3,2,0,1:T(8,128)(2,1)} async-done(((bf16[64,1,24,512]{3,2,0,1:T(8,128)(2,1)}), bf16[64,1,24,2048]{3,2,0,1:T(8,128)(2,1)}) %all-gather.4.cloned.1.call-update) | async-done | bytes 6291472 | tf_op jit(solution)/shard_map/all_gather | solution.py:227
  237.9 6.1 %fusion.2 = f32[64,24,352]{2,1,0:T(8,128)S(1)} fusion(bf16[64,1,24,2048]{3,2,0,1:T(8,128)(2,1)} %all-gather.4.cloned.1.call-done, bf16[1,2048,352]{1,2,0:T(8,128)(2,1)} %param.27), kind=kOutput, calls=%fused_computation.3 | convolution fusion | flops 2214592512 | bytes 9895936 | tf_op jit(solution)/shard_map/nesd,edf->nesf/dot_general | solution.py:37
  244.0 4.8 %fusion.15 = bf16[64,1,24,352]{3,2,1,0:T(8,128)(2,1)} fusion(bf16[1,2048,352]{1,2,0:T(8,128)(2,1)S(1)} %copy-done.19, bf16[64,1,24,2048]{3,2,0,1:T(8,128)(2,1)S(1)} %copy-done.18, f32[64,24,352]{2,1,0:T(8,128)S(1)} %fusion.2), kind=kOutput, calls=%fused_computation.26 | convolution fusion | flops 2217836544 | bytes 10977280 | tf_op jit(solution)/shard_map/nesd,edf->nesf/dot_general | solution.py:38
  248.8 56.0 %all-gather.6.cloned.1.call-done = bf16[256,1,24,352]{3,2,1,0:T(8,128)(2,1)} async-done(((bf16[64,1,24,352]{3,2,1,0:T(8,128)(2,1)}), bf16[256,1,24,352]{3,2,1,0:T(8,128)(2,1)}) %all-gather.6.cloned.1.call-update) | async-done | bytes 4325392 | tf_op jit(solution)/shard_map/all_gather | solution.py:40
  304.9 3.3 copy.195
  308.2 2.7 fusion.11
  310.9 2.0 copy.196
  312.9 11.0 %all-to-all-start.1 = ((bf16[64,1,24,512]{3,2,1,0:T(8,128)(2,1)}), bf16[64,1,24,512]{3,2,1,0:T(8,128)(2,1)}, u32[]{:S(2)}, u32[]{:S(2)}) async-start(bf16[64,1,24,512]{3,2,1,0:T(8,128)(2,1)} %copy.196), calls=%async_computation.2 | async-start | bytes 3145728 | tf_op jit(solution)/shard_map/all_to_all | solution.py:64
  323.9 1.5 select_reduce_fusion
  325.4 37.4 %all-to-all-done.1 = bf16[64,1,24,512]{3,2,1,0:T(8,128)(2,1)} async-done(((bf16[64,1,24,512]{3,2,1,0:T(8,128)(2,1)}), bf16[64,1,24,512]{3,2,1,0:T(8,128)(2,1)}, u32[]{:S(2)}, u32[]{:S(2)}) %all-to-all-start.1) | async-done | bytes 1572896 | tf_op jit(solution)/shard_map/all_to_all | solution.py:64
  362.8 3.1 fusion.27
  (101 shorter events, 2.8 us)
Async XLA Ops:
  6.5 27.9 %copy-start = (bf16[2048,768]{1,0:T(8,128)(2,1)S(1)}, bf16[2048,768]{1,0:T(8,128)(2,1)}, u32[]{:S(2)}) copy-start(bf16[2048,768]{1,0:T(8,128)(2,1)} %param.20) | copy-start | bytes 9437188
  6.5 105.0 %reduce-scatter.2.cloned.1.call-start = ((), (), s32[]{:S(2)}) async-start(), calls=%async_computation.3 | async-start | bytes 1310720 | tf_op jit(solution)/shard_map/reduce_scatter | solution.py:210
  9.6 17.5 %copy-start.12 = (s32[4,3,8]{2,0,1:T(4,128)S(1)}, s32[4,3,8]{2,0,1:T(4,128)}, u32[]{:S(2)}) copy-start(s32[4,3,8]{2,0,1:T(4,128)} %param.33) | copy-start | bytes 1156
  20.7 8.0 %copy-start.14 = (f32[512]{0:T(512)S(1)}, f32[512]{0:T(512)}, u32[]{:S(2)}) copy-start(f32[512]{0:T(512)} %param.22) | copy-start | bytes 6148
  20.8 10.5 %copy-start.16 = (s32[4]{0:T(128)S(1)}, s32[4]{0:T(128)}, u32[]{:S(2)}) copy-start(s32[4]{0:T(128)} %param.32) | copy-start | bytes 52
  20.8 13.7 %copy-start.11 = (f32[2048]{0:T(1024)S(1)}, f32[2048]{0:T(1024)}, u32[]{:S(2)}) copy-start(f32[2048]{0:T(1024)} %param.19) | copy-start | bytes 24580
  23.2 49.8 %collective-permute-start = (bf16[1,352,512]{2,1,0:T(8,128)(2,1)}, bf16[1,352,512]{2,1,0:T(8,128)(2,1)}, u32[]{:S(2)}, u32[]{:S(2)}) collective-permute-start(bf16[1,352,512]{2,1,0:T(8,128)(2,1)} %get-tuple-element.23), channel_id=1, source_target_pairs={{0,1},{1,2},{2,3},{3,0},{4,5},{5,6},{6,7},{7,4},{8,9},{9,10},{10,1... | collective-permute-start | bytes 1081352 | tf_op jit(solution)/shard_map/ppermute | solution.py:55
  24.1 48.9 %collective-permute-start.1 = (bf16[1,352,512]{2,1,0:T(8,128)(2,1)}, bf16[1,352,512]{2,1,0:T(8,128)(2,1)}, u32[]{:S(2)}, u32[]{:S(2)}) collective-permute-start(bf16[1,352,512]{2,1,0:T(8,128)(2,1)} %get-tuple-element.22), channel_id=1, source_target_pairs={{0,2},{1,3},{2,0},{3,1},{4,6},{5,7},{6,4},{7,5},{8,10},{9,11},{10,... | collective-permute-start | bytes 1081352 | tf_op jit(solution)/shard_map/ppermute | solution.py:55
  26.5 46.5 %collective-permute-start.2 = (bf16[1,352,512]{2,1,0:T(8,128)(2,1)}, bf16[1,352,512]{2,1,0:T(8,128)(2,1)}, u32[]{:S(2)}, u32[]{:S(2)}) collective-permute-start(bf16[1,352,512]{2,1,0:T(8,128)(2,1)} %get-tuple-element.21), channel_id=1, source_target_pairs={{0,3},{1,0},{2,1},{3,2},{4,7},{5,4},{6,5},{7,6},{8,11},{9,8},{10,9... | collective-permute-start | bytes 1081352 | tf_op jit(solution)/shard_map/ppermute | solution.py:55
  43.5 0.9 copy-start.2
  44.4 3.6 copy-start.15
  44.4 3.9 %copy-start.17 = (s32[4]{0:T(128)S(1)}, s32[4]{0:T(128)}, u32[]{:S(2)}) copy-start(s32[4]{0:T(128)} %param.32) | copy-start | bytes 52
  48.3 4.1 %copy-start.6 = (bf16[128,512]{1,0:T(8,128)(2,1)S(1)}, bf16[128,512]{1,0:T(8,128)(2,1)}, u32[]{:S(2)}) copy-start(bf16[128,512]{1,0:T(8,128)(2,1)} %copy.170) | copy-start | bytes 393220
  48.3 4.1 %copy-start.7 = (bf16[128,32]{1,0:T(8,128)(2,1)S(1)}, bf16[128,32]{1,0:T(8,128)(2,1)}, u32[]{:S(2)}) copy-start(bf16[128,32]{1,0:T(8,128)(2,1)} %copy.171) | copy-start | bytes 24580
  48.3 4.1 %copy-start.8 = (bf16[128,32]{1,0:T(8,128)(2,1)S(1)}, bf16[128,32]{1,0:T(8,128)(2,1)}, u32[]{:S(2)}) copy-start(bf16[128,32]{1,0:T(8,128)(2,1)} %copy.172) | copy-start | bytes 24580
  48.3 4.1 %copy-start.9 = (s32[4,4,8,4]{2,1,3,0:T(4,128)S(1)}, s32[4,4,8,4]{2,1,3,0:T(4,128)}, u32[]{:S(2)}) copy-start(s32[4,4,8,4]{2,1,3,0:T(4,128)} %copy.177) | copy-start | bytes 6148
  52.3 1.4 copy-start.20
  52.4 1.3 copy-start.3
  61.3 2.0 copy-start.1
  69.9 3.1 copy-start.4
  81.4 2.2 copy-start.10
  81.5 156.4 %all-gather.4.cloned.1.call-start = ((), (), s32[]{:S(2)}) async-start(), calls=%async_computation.4 | async-start | bytes 7864320 | tf_op jit(solution)/shard_map/all_gather | solution.py:227
  174.2 130.7 %all-gather.6.cloned.1.call-start = ((), (), s32[]{:S(2)}) async-start(), calls=%async_computation.5 | async-start | bytes 5898240 | tf_op jit(solution)/shard_map/all_gather | solution.py:40
  237.9 6.1 %copy-start.18 = (bf16[64,1,24,2048]{3,2,0,1:T(8,128)(2,1)S(1)}, bf16[64,1,24,2048]{3,2,0,1:T(8,128)(2,1)}, u32[]{:S(2)}) copy-start(bf16[64,1,24,2048]{3,2,0,1:T(8,128)(2,1)} %all-gather.4.cloned.1.call-done) | copy-start | bytes 18874372
  237.9 6.1 %copy-start.19 = (bf16[1,2048,352]{1,2,0:T(8,128)(2,1)S(1)}, bf16[1,2048,352]{1,2,0:T(8,128)(2,1)}, u32[]{:S(2)}) copy-start(bf16[1,2048,352]{1,2,0:T(8,128)(2,1)} %param.28) | copy-start | bytes 4325380
  304.9 3.3 copy-start.5
  312.9 11.0 %copy-start.13 = (f32[128,6]{0,1:T(8,128)S(1)}, f32[128,6]{0,1:T(8,128)}, u32[]{:S(2)}) copy-start(f32[128,6]{0,1:T(8,128)} %param.35) | copy-start | bytes 9220
  312.9 49.9 %all-to-all-start.1 = ((bf16[64,1,24,512]{3,2,1,0:T(8,128)(2,1)}), bf16[64,1,24,512]{3,2,1,0:T(8,128)(2,1)}, u32[]{:S(2)}, u32[]{:S(2)}) async-start(bf16[64,1,24,512]{3,2,1,0:T(8,128)(2,1)} %copy.196), calls=%async_computation.2 | async-start | bytes 3145728 | tf_op jit(solution)/shard_map/all_to_all | solution.py:64
Sparse Core Ops, SparseCore 0:
  81.6 29.9 reduce-scatter.1
  174.3 63.5 all-gather.3
  249.0 55.8 all-gather.5

commit v7 on v6

--- a/solution.py
+++ b/solution.py
@@ -56,8 +56,10 @@
                 piece, "tp", [(s, (s + shift) % tp_count) for s in range(tp_count)]
             )
         pieces[shift] = piece
-    stacked = jnp.stack(pieces, axis=1)
-    return jnp.take(stacked, (tp_index - jnp.arange(tp_count)) % tp_count, axis=1)
+    reverse = [pieces[(-shift) % tp_count] for shift in range(tp_count)]
+    doubled = jnp.stack(reverse + reverse, axis=1)
+    start = (tp_count - tp_index) % tp_count
+    return lax.dynamic_slice_in_dim(doubled, start, tp_count, 1)
 
 
 def send_home(shares):
@@ -112,7 +114,8 @@
     )
     kv_part = jnp.dot(normed, w_latent, preferred_element_type=jnp.float32)
     kv_all = lax.all_gather(kv_part, "tp", axis=1, tiled=True)
-    kv_all, down_late = lax.optimization_barrier((kv_all, w_down))
+    kv_all, down_late, out_late = lax.optimization_barrier((kv_all, w_down, w_out))
+    out_all = lax.all_gather(out_late, "tp", axis=0, tiled=True)
     new_lat = kv_all[:, :LATENT] * rms_scale(kv_all[:, :LATENT]) * kv_gain
     new_rope = rotate(kv_all[:, LATENT:], cos_val, sin_val)
     new_keys = jnp.concatenate([new_lat, new_rope], axis=1).astype(jnp.bfloat16)
@@ -188,7 +191,6 @@
         .astype(jnp.bfloat16)
         .reshape(row_count, heads_local * VDIM)
     )
-    attn_part = jnp.dot(head_out, w_out, preferred_element_type=jnp.float32)
     expert_count = EXP_DEV * req_count
     capacity = min(row_count, 2 * row_count * TOPK // expert_count)
     slot_count = expert_count * capacity
@@ -206,14 +208,13 @@
     weight_rows = jnp.sum(jnp.where(slot_hot, route_weights[:, :, None], 0.0), axis=1)
     tp_index = lax.axis_index("tp")
     col_start = tp_index * col_share
-    attn_part, down_cols = lax.optimization_barrier((attn_part, down_by_columns(down_late)))
-    attn_cols = lax.psum_scatter(attn_part, "tp", scatter_dimension=1, tiled=True)
-    hidden_cols = lax.dynamic_slice_in_dim(hidden_f, col_start, col_share, 1)
-    resid_cols = hidden_cols + attn_cols
-    square_sum = lax.psum(jnp.sum(resid_cols * resid_cols, axis=-1, keepdims=True), "tp")
-    moe_scale = lax.rsqrt(square_sum / D + eps)
-    gain_cols = lax.dynamic_slice_in_dim(moe_gain, col_start, col_share, 0)
-    moe_in_cols = (resid_cols * moe_scale * gain_cols).astype(jnp.bfloat16)
+    head_all = lax.all_gather(head_out, "tp", axis=1, tiled=True)
+    head_all, down_cols = lax.optimization_barrier((head_all, down_by_columns(down_late)))
+    attn_full = jnp.dot(head_all, out_all, preferred_element_type=jnp.float32)
+    resid_full = hidden_f + attn_full
+    moe_in = (resid_full * rms_scale(resid_full) * moe_gain).astype(jnp.bfloat16)
+    moe_in_cols = lax.dynamic_slice_in_dim(moe_in, col_start, col_share, 1)
+    resid_cols = lax.dynamic_slice_in_dim(resid_full, col_start, col_share, 1)
     placed = jnp.dot(gather_rows.T, moe_in_cols, preferred_element_type=jnp.float32).astype(
         jnp.bfloat16
     )

time: 374 us -> 372 us (level)
  waiting for transfers between devices: 180 us -> 194 us
  other arithmetic: 21.6 us -> 9.32 us
  blocking collectives: 70.8 us -> 76.1 us
  local copies, waits for them, and re-layouts: 33.7 us -> 28.6 us
    all_gather x0 -> x1, waiting for transfers between devices: none -> 37.6 us  [local(): out_all = lax.all_gather(out_late, 'tp', axis=0, tiled=True)]
    reduce_scatter x1 -> x0, waiting for transfers between devices: 22.7 us -> none  [local(): lax.psum_scatter(attn_part, 'tp', scatter_dimension=1, tiled=True)]
    all_gather x0 -> x1, blocking collectives: none -> 14.3 us  [local(): head_all = lax.all_gather(head_out, 'tp', axis=1, tiled=True)]
    psum x1 -> x0, blocking collectives: 6.64 us -> none  [local(): lax.psum(jnp.sum(resid_cols * resid_cols, axis=-1, keepdims=True), 'tp')]
    unnamed x45 -> x54, local copies, waits for them, and re-layouts: 4.41 us -> 7.7 us
  transfers between devices with their start and end apart: 7 -> 7, of which waited for: 4 -> 4; matrix products, arithmetic and copies ran while one was open for 15% -> 11% of each run, Pallas kernels for 0% -> 0%
where the time goes in v7:
time: 372 us; the launch traced here: 371 us
  waiting for transfers between devices  194 us (52%)
  blocking collectives  76.1 us (20%)
  matrix products  35 us (9%)
  local copies, waits for them, and re-layouts  28.6 us (8%)
  between operations  13.8 us (4%)
  starting transfers between devices  13.6 us (4%)
  other arithmetic  9.32 us (3%)
    all_gather x1, waiting for transfers between devices, local(): arrived = lax.all_gather(arrived_cols, 'tp', axis=3, tiled=True)  63.2 us
    all_gather x1, waiting for transfers between devices, expert_math(): active_all = lax.all_gather(active, 'tp', axis=0)  56 us
    all_to_all x1, blocking collectives, local(): lax.all_to_all(placed.reshape(req_count, EXP_DEV, capacity, col_share), '...  50.7 us
    all_gather x1, waiting for transfers between devices, local(): out_all = lax.all_gather(out_late, 'tp', axis=0, tiled=True)  37.6 us
    all_to_all x1, waiting for transfers between devices, send_home(): lax.all_to_all(shares, 'req', split_axis=0, concat_axis=0, tiled=True)  37.4 us
    all_gather x1, blocking collectives, local(): head_all = lax.all_gather(head_out, 'tp', axis=1, tiled=True)  14.3 us
    all_gather x1, blocking collectives, local(): kv_all = lax.all_gather(kv_part, 'tp', axis=1, tiled=True)  11.2 us
    all_to_all x1, starting transfers between devices, send_home(): lax.all_to_all(shares, 'req', split_axis=0, concat_axis=0, tiled=True)  10.9 us
  transfers between devices with their start and end apart: 7, of which 4 were waited for; matrix products, arithmetic and copies ran while one was open for 11% of the time, Pallas kernels for 0%

profile of v7, /device:TPU:1, one launch (start us, length us, event | category | flops | bytes accessed | tf_op | source)
XLA Modules:
  0.0 370.8 jit_solution(11645912084184203207)
XLA Ops:
  6.5 1.4 fusion.28
  7.9 1.6 fusion.56
  9.6 11.2 %all_gather.18 = f32[128,576]{0,1:T(8,128)S(1)} all-gather(f32[128,144]{0,1:T(8,128)S(1)} %fusion.56), channel_id=1, replica_groups=mesh['req'=64,'tp'=4] {'tp'}, dimensions={1}, use_global_device_ids=true | all-gather | bytes 368640 | tf_op jit(solution)/shard_map/all_gather | solution.py:116
  20.9 2.3 constant_dynamic-slice_fusion.1
  23.2 2.1 collective-permute-start
  25.2 0.6 collective-permute-start.1
  26.3 0.1 select_reduce_fusion.3
  26.4 0.3 select_reduce_fusion.5
  26.7 0.3 select_reduce_fusion.6
  27.2 0.6 copy.177
  27.9 0.8 multiply_convert_fusion.1
  28.7 1.7 copy.170
  30.6 0.2 multiply_cosine_fusion
  30.8 0.7 copy.171
  31.5 0.7 copy.172
  32.2 0.7 copy.164
  32.9 0.7 copy.166
  33.6 2.4 fusion.58
  36.4 1.0 subtract_convert_fusion
  37.4 1.5 fusion.25
  39.0 0.5 copy.167
  39.5 0.3 reshape.285
  40.3 3.0 fusion.68
  43.4 0.4 fusion.24
  43.8 0.8 slice.67
  44.7 1.0 fusion.69
  45.8 1.4 reshape.287
  47.2 0.3 exponential_reduce_fusion
  47.6 0.2 copy.180
  47.8 0.2 fusion.46
  48.1 0.2 copy.182
  48.2 1.8 fusion.39
  50.1 0.9 fusion.23
  51.1 0.2 copy.204
  51.3 1.8 reduce-window.6
  53.1 0.3 slice_reduce_fusion
  53.8 0.3 convolution_convert_fusion.2
  54.1 0.6 convert_reduce_fusion
  54.8 0.8 dynamic-slice
  55.5 14.3 %all_gather.19 = bf16[128,2048]{0,1:T(8,128)(2,1)S(1)} all-gather(bf16[128,512]{0,1:T(8,128)(2,1)S(1)} %bitcast.190), channel_id=1, replica_groups=mesh['req'=64,'tp'=4] {'tp'}, dimensions={1}, use_global_device_ids=true | all-gather | bytes 655360 | tf_op jit(solution)/shard_map/all_gather | solution.py:211
  69.9 1.0 bitcast_dynamic-update-slice_fusion.6
  70.9 1.0 bitcast_dynamic-update-slice_fusion.4
  71.9 1.0 bitcast_dynamic-update-slice_fusion.2
  72.9 1.0 bitcast_dynamic-update-slice_fusion
  74.0 1.0 bitcast_dynamic-update-slice_fusion.7
  75.0 1.1 bitcast_dynamic-update-slice_fusion.5
  76.1 1.0 bitcast_dynamic-update-slice_fusion.3
  77.1 1.0 bitcast_dynamic-update-slice_fusion.1
  78.1 1.3 constant_dynamic-slice_fusion
  79.4 37.6 %all-gather.5.cloned.1.call-done = bf16[2048,2048]{1,0:T(8,128)(2,1)} async-done(((bf16[512,2048]{1,0:T(8,128)(2,1)}), bf16[2048,2048]{1,0:T(8,128)(2,1)}) %all-gather.5.cloned.1.call-update) | async-done | bytes 8388624 | tf_op jit(solution)/shard_map/all_gather | solution.py:118
  117.0 4.7 %multiply_reduce_fusion = (f32[128]{0:T(128)S(1)}, f32[128,2048]{1,0:T(8,128)S(1)}) fusion(bf16[128,2048]{0,1:T(8,128)(2,1)S(1)} %all_gather.19, bf16[2048,2048]{1,0:T(8,128)(2,1)} %all-gather.5.cloned.1.call-done, bf16[128,2048]{1,0:T(8,128)(2,1)S(1)} %copy-done.2), kind=kOutput, calls=%fused_computation.46 | convolution fusion | flops 1074790272 | bytes 10486272 | tf_op jit(solution)/shard_map/dot_general | solution.py:213
  121.8 0.6 convolution_convert_fusion
  122.4 50.7 %all_to_all.10 = bf16[64,1,24,512]{3,2,1,0:T(8,128)(2,1)} all-to-all(bf16[64,1,24,512]{3,2,1,0:T(8,128)(2,1)S(1)} %bitcast.181), channel_id=1, replica_groups=mesh['req'=64,'tp'=4] {'req'}, dimensions={0} | all-to-all | bytes 3145728 | tf_op jit(solution)/shard_map/all_to_all | solution.py:221
  173.2 63.2 %all-gather.7.cloned.1.call-done = bf16[64,1,24,2048]{3,2,0,1:T(8,128)(2,1)} async-done(((bf16[64,1,24,512]{3,2,0,1:T(8,128)(2,1)}), bf16[64,1,24,2048]{3,2,0,1:T(8,128)(2,1)}) %all-gather.7.cloned.1.call-update) | async-done | bytes 6291472 | tf_op jit(solution)/shard_map/all_gather | solution.py:228
  236.4 6.1 %fusion.2 = f32[64,24,352]{2,1,0:T(8,128)S(1)} fusion(bf16[64,1,24,2048]{3,2,0,1:T(8,128)(2,1)} %all-gather.7.cloned.1.call-done, bf16[1,2048,352]{1,2,0:T(8,128)(2,1)S(1)} %copy-done.20), kind=kOutput, calls=%fused_computation.2 | convolution fusion | flops 2214592512 | bytes 9895936 | tf_op jit(solution)/shard_map/nesd,edf->nesf/dot_general | solution.py:37
  242.5 4.8 %fusion.15 = bf16[64,1,24,352]{3,2,1,0:T(8,128)(2,1)} fusion(bf16[1,2048,352]{1,2,0:T(8,128)(2,1)S(1)} %copy-done.21, bf16[64,1,24,2048]{3,2,0,1:T(8,128)(2,1)S(1)} %copy-done.19, f32[64,24,352]{2,1,0:T(8,128)S(1)} %fusion.2), kind=kOutput, calls=%fused_computation.26 | convolution fusion | flops 2217836544 | bytes 10977280 | tf_op jit(solution)/shard_map/nesd,edf->nesf/dot_general | solution.py:38
  247.4 56.0 %all-gather.9.cloned.1.call-done = bf16[256,1,24,352]{3,2,1,0:T(8,128)(2,1)} async-done(((bf16[64,1,24,352]{3,2,1,0:T(8,128)(2,1)}), bf16[256,1,24,352]{3,2,1,0:T(8,128)(2,1)}) %all-gather.9.cloned.1.call-update) | async-done | bytes 4325392 | tf_op jit(solution)/shard_map/all_gather | solution.py:40
  303.4 3.2 copy.195
  306.6 2.7 fusion.11
  309.3 2.0 copy.196
  311.3 10.9 %all-to-all-start.1 = ((bf16[64,1,24,512]{3,2,1,0:T(8,128)(2,1)}), bf16[64,1,24,512]{3,2,1,0:T(8,128)(2,1)}, u32[]{:S(2)}, u32[]{:S(2)}) async-start(bf16[64,1,24,512]{3,2,1,0:T(8,128)(2,1)} %copy.196), calls=%async_computation.1 | async-start | bytes 3145728 | tf_op jit(solution)/shard_map/all_to_all | solution.py:66
  322.2 1.5 select_reduce_fusion
  323.7 37.4 %all-to-all-done.1 = bf16[64,1,24,512]{3,2,1,0:T(8,128)(2,1)} async-done(((bf16[64,1,24,512]{3,2,1,0:T(8,128)(2,1)}), bf16[64,1,24,512]{3,2,1,0:T(8,128)(2,1)}, u32[]{:S(2)}, u32[]{:S(2)}) %all-to-all-start.1) | async-done | bytes 1572896 | tf_op jit(solution)/shard_map/all_to_all | solution.py:66
  361.1 3.1 fusion.27
  (104 shorter events, 2.8 us)
Async XLA Ops:
  6.5 27.1 %copy-start = (bf16[2048,768]{1,0:T(8,128)(2,1)S(1)}, bf16[2048,768]{1,0:T(8,128)(2,1)}, u32[]{:S(2)}) copy-start(bf16[2048,768]{1,0:T(8,128)(2,1)} %param.20) | copy-start | bytes 9437188
  6.5 110.5 %all-gather.5.cloned.1.call-start = ((), (), s32[]{:S(2)}) async-start(), calls=%async_computation.2 | async-start | bytes 10485760 | tf_op jit(solution)/shard_map/all_gather | solution.py:118
  9.6 16.2 %copy-start.12 = (s32[128,6]{0,1:T(8,128)S(1)}, s32[128,6]{0,1:T(8,128)}, u32[]{:S(2)}) copy-start(s32[128,6]{0,1:T(8,128)} %param.34) | copy-start | bytes 9220
  9.6 16.7 %copy-start.13 = (s32[4,3,8]{2,0,1:T(4,128)S(1)}, s32[4,3,8]{2,0,1:T(4,128)}, u32[]{:S(2)}) copy-start(s32[4,3,8]{2,0,1:T(4,128)} %param.33) | copy-start | bytes 1156
  20.8 7.1 %copy-start.15 = (f32[512]{0:T(512)S(1)}, f32[512]{0:T(512)}, u32[]{:S(2)}) copy-start(f32[512]{0:T(512)} %param.22) | copy-start | bytes 6148
  20.8 9.6 %copy-start.17 = (s32[4]{0:T(128)S(1)}, s32[4]{0:T(128)}, u32[]{:S(2)}) copy-start(s32[4]{0:T(128)} %param.32) | copy-start | bytes 52
  20.8 215.6 %all-gather.7.cloned.1.call-start = ((), (), s32[]{:S(2)}) async-start(), calls=%async_computation.3 | async-start | bytes 7864320 | tf_op jit(solution)/shard_map/all_gather | solution.py:228
  23.2 47.7 %collective-permute-start = (bf16[1,352,512]{2,1,0:T(8,128)(2,1)}, bf16[1,352,512]{2,1,0:T(8,128)(2,1)}, u32[]{:S(2)}, u32[]{:S(2)}) collective-permute-start(bf16[1,352,512]{2,1,0:T(8,128)(2,1)} %get-tuple-element.22), channel_id=1, source_target_pairs={{0,3},{1,0},{2,1},{3,2},{4,7},{5,4},{6,5},{7,6},{8,11},{9,8},{10,9... | collective-permute-start | bytes 1081352 | tf_op jit(solution)/shard_map/ppermute | solution.py:55
  25.2 46.7 %collective-permute-start.1 = (bf16[1,352,512]{2,1,0:T(8,128)(2,1)}, bf16[1,352,512]{2,1,0:T(8,128)(2,1)}, u32[]{:S(2)}, u32[]{:S(2)}) collective-permute-start(bf16[1,352,512]{2,1,0:T(8,128)(2,1)} %get-tuple-element.21), channel_id=1, source_target_pairs={{0,2},{1,3},{2,0},{3,1},{4,6},{5,7},{6,4},{7,5},{8,10},{9,11},{10,... | collective-permute-start | bytes 1081352 | tf_op jit(solution)/shard_map/ppermute | solution.py:55
  25.8 47.1 %collective-permute-start.2 = (bf16[1,352,512]{2,1,0:T(8,128)(2,1)}, bf16[1,352,512]{2,1,0:T(8,128)(2,1)}, u32[]{:S(2)}, u32[]{:S(2)}) collective-permute-start(bf16[1,352,512]{2,1,0:T(8,128)(2,1)} %get-tuple-element.20), channel_id=1, source_target_pairs={{0,1},{1,2},{2,3},{3,0},{4,5},{5,6},{6,7},{7,4},{8,9},{9,10},{10,1... | collective-permute-start | bytes 1081352 | tf_op jit(solution)/shard_map/ppermute | solution.py:55
  37.3 2.5 copy-start.16
  37.3 2.8 copy-start.18
  39.5 3.9 %copy-start.8 = (bf16[128,512]{1,0:T(8,128)(2,1)S(1)}, bf16[128,512]{1,0:T(8,128)(2,1)}, u32[]{:S(2)}) copy-start(bf16[128,512]{1,0:T(8,128)(2,1)} %copy.170) | copy-start | bytes 393220
  39.5 3.9 %copy-start.9 = (bf16[128,32]{1,0:T(8,128)(2,1)S(1)}, bf16[128,32]{1,0:T(8,128)(2,1)}, u32[]{:S(2)}) copy-start(bf16[128,32]{1,0:T(8,128)(2,1)} %copy.171) | copy-start | bytes 24580
  39.5 3.9 %copy-start.10 = (bf16[128,32]{1,0:T(8,128)(2,1)S(1)}, bf16[128,32]{1,0:T(8,128)(2,1)}, u32[]{:S(2)}) copy-start(bf16[128,32]{1,0:T(8,128)(2,1)} %copy.172) | copy-start | bytes 24580
  39.5 3.9 %copy-start.11 = (s32[4,4,8,4]{2,1,3,0:T(4,128)S(1)}, s32[4,4,8,4]{2,1,3,0:T(4,128)}, u32[]{:S(2)}) copy-start(s32[4,4,8,4]{2,1,3,0:T(4,128)} %copy.177) | copy-start | bytes 6148
  47.5 2.5 copy-start.3
  48.2 1.8 copy-start.6
  50.1 1.0 copy-start.7
  75.0 42.0 %copy-start.2 = (bf16[128,2048]{1,0:T(8,128)(2,1)S(1)}, bf16[128,2048]{1,0:T(8,128)(2,1)}, u32[]{:S(2)}) copy-start(bf16[128,2048]{1,0:T(8,128)(2,1)} %param.18) | copy-start | bytes 1572868
  121.7 51.3 %copy-start.4 = (f32[128,2048]{1,0:T(8,128)}, f32[128,2048]{1,0:T(8,128)S(1)}, u32[]{:S(2)}) copy-start(f32[128,2048]{1,0:T(8,128)S(1)} %get-tuple-element.43) | copy-start | bytes 3145732
  122.4 114.0 %copy-start.20 = (bf16[1,2048,352]{1,2,0:T(8,128)(2,1)S(1)}, bf16[1,2048,352]{1,2,0:T(8,128)(2,1)}, u32[]{:S(2)}) copy-start(bf16[1,2048,352]{1,2,0:T(8,128)(2,1)} %param.27) | copy-start | bytes 4325380
  173.1 69.4 %copy-start.21 = (bf16[1,2048,352]{1,2,0:T(8,128)(2,1)S(1)}, bf16[1,2048,352]{1,2,0:T(8,128)(2,1)}, u32[]{:S(2)}) copy-start(bf16[1,2048,352]{1,2,0:T(8,128)(2,1)} %param.28) | copy-start | bytes 4325380
  173.1 130.3 %all-gather.9.cloned.1.call-start = ((), (), s32[]{:S(2)}) async-start(), calls=%async_computation.4 | async-start | bytes 5898240 | tf_op jit(solution)/shard_map/all_gather | solution.py:40
  236.4 6.1 %copy-start.19 = (bf16[64,1,24,2048]{3,2,0,1:T(8,128)(2,1)S(1)}, bf16[64,1,24,2048]{3,2,0,1:T(8,128)(2,1)}, u32[]{:S(2)}) copy-start(bf16[64,1,24,2048]{3,2,0,1:T(8,128)(2,1)} %all-gather.7.cloned.1.call-done) | copy-start | bytes 18874372
  247.4 59.2 %copy-start.5 = (bf16[1,4,352,512]{3,2,1,0:T(8,128)(2,1)S(1)}, bf16[1,4,352,512]{3,2,1,0:T(8,128)(2,1)}, u32[]{:S(2)}) copy-start(bf16[1,4,352,512]{3,2,1,0:T(8,128)(2,1)} %constant_dynamic-slice_fusion) | copy-start | bytes 4325380
  309.3 12.9 %copy-start.14 = (f32[128,6]{0,1:T(8,128)S(1)}, f32[128,6]{0,1:T(8,128)}, u32[]{:S(2)}) copy-start(f32[128,6]{0,1:T(8,128)} %param.35) | copy-start | bytes 9220
  309.3 54.9 %copy-start.1 = (bf16[2048,768]{1,0:T(8,128)(2,1)S(1)}, bf16[2048,768]{1,0:T(8,128)(2,1)}, u32[]{:S(2)}) copy-start(bf16[2048,768]{1,0:T(8,128)(2,1)} %param.20) | copy-start | bytes 9437188
  311.3 49.8 %all-to-all-start.1 = ((bf16[64,1,24,512]{3,2,1,0:T(8,128)(2,1)}), bf16[64,1,24,512]{3,2,1,0:T(8,128)(2,1)}, u32[]{:S(2)}, u32[]{:S(2)}) async-start(bf16[64,1,24,512]{3,2,1,0:T(8,128)(2,1)} %copy.196), calls=%async_computation.1 | async-start | bytes 3145728 | tf_op jit(solution)/shard_map/all_to_all | solution.py:66
Sparse Core Ops, SparseCore 0:
  20.9 96.0 all-gather.4
  173.2 63.1 all-gather.6
  247.5 55.8 all-gather.8

commit v8 on v6

--- a/solution.py
+++ b/solution.py
@@ -43,21 +43,23 @@
     ).astype(jnp.bfloat16)
 
 
-def down_by_columns(down_w):
+def by_columns(weight):
     tp_count = lax.axis_size("tp")
     tp_index = lax.axis_index("tp")
-    col_share = down_w.shape[2] // tp_count
+    col_share = weight.shape[-1] // tp_count
     pieces = [None] * tp_count
     for shift in range(tp_count):
         target = (tp_index + shift) % tp_count
-        piece = lax.dynamic_slice_in_dim(down_w, target * col_share, col_share, 2)
+        piece = lax.dynamic_slice_in_dim(weight, target * col_share, col_share, weight.ndim - 1)
         if shift:
             piece = lax.ppermute(
                 piece, "tp", [(s, (s + shift) % tp_count) for s in range(tp_count)]
             )
         pieces[shift] = piece
-    stacked = jnp.stack(pieces, axis=1)
-    return jnp.take(stacked, (tp_index - jnp.arange(tp_count)) % tp_count, axis=1)
+    reverse = [pieces[(-shift) % tp_count] for shift in range(tp_count)]
+    doubled = jnp.stack(reverse + reverse, axis=weight.ndim - 2)
+    start = (tp_count - tp_index) % tp_count
+    return lax.dynamic_slice_in_dim(doubled, start, tp_count, weight.ndim - 2)
 
 
 def send_home(shares):
@@ -112,7 +114,7 @@
     )
     kv_part = jnp.dot(normed, w_latent, preferred_element_type=jnp.float32)
     kv_all = lax.all_gather(kv_part, "tp", axis=1, tiled=True)
-    kv_all, down_late = lax.optimization_barrier((kv_all, w_down))
+    kv_all, down_late, out_late = lax.optimization_barrier((kv_all, w_down, w_out))
     new_lat = kv_all[:, :LATENT] * rms_scale(kv_all[:, :LATENT]) * kv_gain
     new_rope = rotate(kv_all[:, LATENT:], cos_val, sin_val)
     new_keys = jnp.concatenate([new_lat, new_rope], axis=1).astype(jnp.bfloat16)
@@ -188,7 +190,6 @@
         .astype(jnp.bfloat16)
         .reshape(row_count, heads_local * VDIM)
     )
-    attn_part = jnp.dot(head_out, w_out, preferred_element_type=jnp.float32)
     expert_count = EXP_DEV * req_count
     capacity = min(row_count, 2 * row_count * TOPK // expert_count)
     slot_count = expert_count * capacity
@@ -206,8 +207,13 @@
     weight_rows = jnp.sum(jnp.where(slot_hot, route_weights[:, :, None], 0.0), axis=1)
     tp_index = lax.axis_index("tp")
     col_start = tp_index * col_share
-    attn_part, down_cols = lax.optimization_barrier((attn_part, down_by_columns(down_late)))
-    attn_cols = lax.psum_scatter(attn_part, "tp", scatter_dimension=1, tiled=True)
+    head_all = lax.all_gather(head_out, "tp", axis=1, tiled=True)
+    head_all, down_cols, out_cols = lax.optimization_barrier(
+        (head_all, by_columns(down_late), by_columns(out_late))
+    )
+    attn_cols = jnp.dot(
+        head_all, out_cols.reshape(-1, col_share), preferred_element_type=jnp.float32
+    )
     hidden_cols = lax.dynamic_slice_in_dim(hidden_f, col_start, col_share, 1)
     resid_cols = hidden_cols + attn_cols
     square_sum = lax.psum(jnp.sum(resid_cols * resid_cols, axis=-1, keepdims=True), "tp")

time: 374 us -> 368 us (0.984)
  blocking collectives: 70.8 us -> 88.3 us
  waiting for transfers between devices: 180 us -> 164 us
  other arithmetic: 21.6 us -> 11.9 us
  matrix products: 38.6 us -> 33.8 us
  local copies, waits for them, and re-layouts: 33.7 us -> 37.6 us
    reduce_scatter x1 -> x0, waiting for transfers between devices: 22.7 us -> none  [local(): lax.psum_scatter(attn_part, 'tp', scatter_dimension=1, tiled=True)]
    all_gather x0 -> x1, blocking collectives: none -> 10.7 us  [local(): head_all = lax.all_gather(head_out, 'tp', axis=1, tiled=True)]
    unnamed x45 -> x65, local copies, waits for them, and re-layouts: 4.41 us -> 13.2 us
    all_to_all x1, blocking collectives: 53 us -> 60.4 us  [local(): lax.all_to_all(placed.reshape(req_count, EXP_DEV, capacity, col_share), '...]
    ppermute x3 -> x6, waiting for transfers between devices: 0.01 us -> 6.36 us  [by_columns(): lax.ppermute(piece, 'tp', [(s, (s + shift) % tp_count) for s in range(tp_...]
    dynamic_slice x0 -> x4, local copies, waits for them, and re-layouts: none -> 5.03 us  [the longest x2 3.69 us: by_columns(): lax.dynamic_slice_in_dim(weight, target * col_share, col_share, weight.nd...]
  transfers between devices with their start and end apart: 7 -> 9, of which waited for: 4 -> 4; matrix products, arithmetic and copies ran while one was open for 15% -> 13% of each run, Pallas kernels for 0% -> 0%
where the time goes in v8:
time: 368 us; the launch traced here: 367 us
  waiting for transfers between devices  164 us (45%)
  blocking collectives  88.3 us (24%)
  local copies, waits for them, and re-layouts  37.6 us (10%)
  matrix products  33.8 us (9%)
  starting transfers between devices  17.7 us (5%)
  between operations  14.1 us (4%)
  other arithmetic  11.9 us (3%)
    all_gather x1, waiting for transfers between devices, local(): arrived = lax.all_gather(arrived_cols, 'tp', axis=3, tiled=True)  64.2 us
    all_to_all x1, blocking collectives, local(): lax.all_to_all(placed.reshape(req_count, EXP_DEV, capacity, col_share), '...  60.4 us
    all_gather x1, waiting for transfers between devices, expert_math(): active_all = lax.all_gather(active, 'tp', axis=0)  56 us
    all_to_all x1, waiting for transfers between devices, send_home(): lax.all_to_all(shares, 'req', split_axis=0, concat_axis=0, tiled=True)  37.4 us
    unnamed x65, local copies, waits for them, and re-layouts  13.2 us
    all_gather x1, blocking collectives, local(): kv_all = lax.all_gather(kv_part, 'tp', axis=1, tiled=True)  11.2 us
    all_to_all x1, starting transfers between devices, send_home(): lax.all_to_all(shares, 'req', split_axis=0, concat_axis=0, tiled=True)  10.9 us
    all_gather x1, blocking collectives, local(): head_all = lax.all_gather(head_out, 'tp', axis=1, tiled=True)  10.7 us
  transfers between devices with their start and end apart: 9, of which 4 were waited for; matrix products, arithmetic and copies ran while one was open for 13% of the time, Pallas kernels for 0%

profile of v8, /device:TPU:1, one launch (start us, length us, event | category | flops | bytes accessed | tf_op | source)
XLA Modules:
  0.0 367.3 jit_solution(1001966158409923773)
XLA Ops:
  6.5 1.4 multiply_reduce_fusion
  7.9 1.6 fusion.53
  9.6 11.2 %all_gather.15 = f32[128,576]{0,1:T(8,128)S(1)} all-gather(f32[128,144]{0,1:T(8,128)S(1)} %fusion.53), channel_id=1, replica_groups=mesh['req'=64,'tp'=4] {'tp'}, dimensions={1}, use_global_device_ids=true | all-gather | bytes 368640 | tf_op jit(solution)/shard_map/all_gather | solution.py:116
  20.8 2.7 constant_dynamic-slice_fusion.1
  23.4 2.0 collective-permute-start.3
  25.5 0.6 collective-permute-start.4
  26.1 1.0 constant_dynamic-slice_fusion.5
  27.1 2.7 collective-permute-start
  29.8 1.2 collective-permute-start.1
  31.0 0.5 iota_compare_fusion.9
  32.9 0.6 copy.177
  33.6 0.8 multiply_convert_fusion.2
  34.4 1.7 copy.170
  36.5 0.7 copy.171
  37.2 0.7 copy.172
  37.9 0.7 copy.164
  38.7 0.7 copy.166
  39.4 2.4 fusion.54
  42.1 1.4 fusion.25
  43.5 0.9 subtract_convert_fusion
  44.6 0.5 copy.167
  45.9 2.8 fusion.62
  49.3 0.8 slice.67
  50.1 1.0 fusion.63
  51.7 1.3 reshape.282
  53.6 1.9 fusion.36
  55.5 2.1 fusion.23
  57.7 2.2 copy.204
  60.0 1.8 reduce-window.6
  62.4 1.6 convert_reduce_fusion
  64.0 1.3 convolution_convert_fusion.2
  65.3 0.9 bitcast_dynamic-update-slice_fusion.6
  66.2 1.1 convert_element_type.76
  67.3 0.8 dynamic_slice.47
  68.0 10.7 %all_gather.16 = bf16[128,2048]{0,1:T(8,128)(2,1)S(1)} all-gather(bf16[128,512]{0,1:T(8,128)(2,1)S(1)} %bitcast.207), channel_id=1, replica_groups=mesh['req'=64,'tp'=4] {'tp'}, dimensions={1}, use_global_device_ids=true | all-gather | bytes 655360 | tf_op jit(solution)/shard_map/all_gather | solution.py:210
  78.8 1.0 bitcast_dynamic-update-slice_fusion.14
  79.9 1.0 bitcast_dynamic-update-slice_fusion.12
  80.9 1.0 bitcast_dynamic-update-slice_fusion.10
  81.9 6.4 %collective-permute-done.2 = bf16[1,352,512]{2,1,0:T(8,128)(2,1)S(1)} collective-permute-done((bf16[1,352,512]{2,1,0:T(8,128)(2,1)}, bf16[1,352,512]{2,1,0:T(8,128)(2,1)S(1)}, u32[]{:S(2)}, u32[]{:S(2)}) %collective-permute-start.2) | collective-permute-done | bytes 360480 | tf_op jit(solution)/shard_map/ppermute | solution.py:55
  88.3 1.2 bitcast_dynamic-update-slice_fusion.15
  89.5 1.2 bitcast_dynamic-update-slice_fusion.13
  90.7 1.0 bitcast_dynamic-update-slice_fusion.11
  91.7 1.2 constant_dynamic-slice_fusion.4
  92.9 1.1 bitcast_dynamic-update-slice_fusion.4
  94.0 1.1 bitcast_dynamic-update-slice_fusion.2
  95.1 1.1 bitcast_dynamic-update-slice_fusion
  96.3 1.1 bitcast_dynamic-update-slice_fusion.5
  97.3 1.1 bitcast_dynamic-update-slice_fusion.3
  98.4 1.1 bitcast_dynamic-update-slice_fusion.1
  99.7 1.6 multiply_reduce_fusion.1
  101.2 6.0 %psum.7 = f32[128,1]{0,1:T(1,128)S(1)} all-reduce(f32[128,1]{0,1:T(1,128)S(1)} %bitcast.220), channel_id=1, replica_groups=mesh['req'=64,'tp'=4] {'tp'}, use_global_device_ids=true, to_apply=%region_19.20 | all-reduce | flops 128 | bytes 1024 | tf_op jit(solution)/shard_map/psum | solution.py:219
  107.3 0.6 convolution_convert_fusion
  107.9 60.4 %all_to_all.10 = bf16[64,1,24,512]{3,2,1,0:T(8,128)(2,1)} all-to-all(bf16[64,1,24,512]{3,2,1,0:T(8,128)(2,1)S(1)} %bitcast.198), channel_id=1, replica_groups=mesh['req'=64,'tp'=4] {'req'}, dimensions={0} | all-to-all | bytes 3145728 | tf_op jit(solution)/shard_map/all_to_all | solution.py:226
  168.6 64.2 %all-gather.4.cloned.1.call-done = bf16[64,1,24,2048]{3,2,0,1:T(8,128)(2,1)} async-done(((bf16[64,1,24,512]{3,2,0,1:T(8,128)(2,1)}), bf16[64,1,24,2048]{3,2,0,1:T(8,128)(2,1)}) %all-gather.4.cloned.1.call-update) | async-done | bytes 6291472 | tf_op jit(solution)/shard_map/all_gather | solution.py:233
  232.7 6.0 %fusion.2 = f32[64,24,352]{2,1,0:T(8,128)S(1)} fusion(bf16[64,1,24,2048]{3,2,0,1:T(8,128)(2,1)} %all-gather.4.cloned.1.call-done, bf16[1,2048,352]{1,2,0:T(8,128)(2,1)S(1)} %copy-done.21), kind=kOutput, calls=%fused_computation.2 | convolution fusion | flops 2214592512 | bytes 9895936 | tf_op jit(solution)/shard_map/nesd,edf->nesf/dot_general | solution.py:37
  238.8 4.8 %fusion.15 = bf16[64,1,24,352]{3,2,1,0:T(8,128)(2,1)} fusion(bf16[1,2048,352]{1,2,0:T(8,128)(2,1)S(1)} %copy-done.22, bf16[64,1,24,2048]{3,2,0,1:T(8,128)(2,1)S(1)} %copy-done.20, f32[64,24,352]{2,1,0:T(8,128)S(1)} %fusion.2), kind=kOutput, calls=%fused_computation.23 | convolution fusion | flops 2217836544 | bytes 10977280 | tf_op jit(solution)/shard_map/nesd,edf->nesf/dot_general | solution.py:38
  243.6 56.0 %all-gather.6.cloned.1.call-done = bf16[256,1,24,352]{3,2,1,0:T(8,128)(2,1)} async-done(((bf16[64,1,24,352]{3,2,1,0:T(8,128)(2,1)}), bf16[256,1,24,352]{3,2,1,0:T(8,128)(2,1)}) %all-gather.6.cloned.1.call-update) | async-done | bytes 4325392 | tf_op jit(solution)/shard_map/all_gather | solution.py:40
  299.7 3.2 copy.195
  302.8 2.7 fusion.11
  305.6 2.0 copy.196
  307.6 10.9 %all-to-all-start.1 = ((bf16[64,1,24,512]{3,2,1,0:T(8,128)(2,1)}), bf16[64,1,24,512]{3,2,1,0:T(8,128)(2,1)}, u32[]{:S(2)}, u32[]{:S(2)}) async-start(bf16[64,1,24,512]{3,2,1,0:T(8,128)(2,1)} %copy.196), calls=%async_computation.1 | async-start | bytes 3145728 | tf_op jit(solution)/shard_map/all_to_all | solution.py:66
  318.5 1.5 select_reduce_fusion
  320.0 37.4 %all-to-all-done.1 = bf16[64,1,24,512]{3,2,1,0:T(8,128)(2,1)} async-done(((bf16[64,1,24,512]{3,2,1,0:T(8,128)(2,1)}), bf16[64,1,24,512]{3,2,1,0:T(8,128)(2,1)}, u32[]{:S(2)}, u32[]{:S(2)}) %all-to-all-start.1) | async-done | bytes 1572896 | tf_op jit(solution)/shard_map/all_to_all | solution.py:66
  357.4 3.1 fusion.27
  (123 shorter events, 6.0 us)
Async XLA Ops:
  6.5 32.9 %copy-start = (bf16[2048,768]{1,0:T(8,128)(2,1)S(1)}, bf16[2048,768]{1,0:T(8,128)(2,1)}, u32[]{:S(2)}) copy-start(bf16[2048,768]{1,0:T(8,128)(2,1)} %param.20) | copy-start | bytes 9437188
  6.5 226.2 %all-gather.4.cloned.1.call-start = ((), (), s32[]{:S(2)}) async-start(), calls=%async_computation.2 | async-start | bytes 7864320 | tf_op jit(solution)/shard_map/all_gather | solution.py:233
  9.6 21.9 %copy-start.13 = (s32[128,6]{0,1:T(8,128)S(1)}, s32[128,6]{0,1:T(8,128)}, u32[]{:S(2)}) copy-start(s32[128,6]{0,1:T(8,128)} %param.34) | copy-start | bytes 9220
  9.6 22.3 %copy-start.14 = (s32[4,3,8]{2,0,1:T(4,128)S(1)}, s32[4,3,8]{2,0,1:T(4,128)}, u32[]{:S(2)}) copy-start(s32[4,3,8]{2,0,1:T(4,128)} %param.33) | copy-start | bytes 1156
  20.8 5.3 %copy-start.6 = (bf16[1,352,2048]{2,1,0:T(8,128)(2,1)S(1)}, bf16[1,352,2048]{2,1,0:T(8,128)(2,1)}, u32[]{:S(2)}) copy-start(bf16[1,352,2048]{2,1,0:T(8,128)(2,1)} %param.29) | copy-start | bytes 4325380
  20.8 12.9 %copy-start.16 = (f32[512]{0:T(512)S(1)}, f32[512]{0:T(512)}, u32[]{:S(2)}) copy-start(f32[512]{0:T(512)} %param.22) | copy-start | bytes 6148
  20.8 15.3 %copy-start.18 = (s32[4]{0:T(128)S(1)}, s32[4]{0:T(128)}, u32[]{:S(2)}) copy-start(s32[4]{0:T(128)} %param.32) | copy-start | bytes 52
  23.4 69.5 %collective-permute-start.3 = (bf16[512,512]{1,0:T(8,128)(2,1)}, bf16[512,512]{1,0:T(8,128)(2,1)}, u32[]{:S(2)}, u32[]{:S(2)}) collective-permute-start(bf16[512,512]{1,0:T(8,128)(2,1)} %get-tuple-element.24), channel_id=1, source_target_pairs={{0,3},{1,0},{2,1},{3,2},{4,7},{5,4},{6,5},{7,6},{8,11},{9,8},{10,9... | collective-permute-start | bytes 1572872 | tf_op jit(solution)/shard_map/ppermute | solution.py:55
  25.5 68.5 %collective-permute-start.4 = (bf16[512,512]{1,0:T(8,128)(2,1)}, bf16[512,512]{1,0:T(8,128)(2,1)}, u32[]{:S(2)}, u32[]{:S(2)}) collective-permute-start(bf16[512,512]{1,0:T(8,128)(2,1)} %get-tuple-element.23), channel_id=1, source_target_pairs={{0,2},{1,3},{2,0},{3,1},{4,6},{5,7},{6,4},{7,5},{8,10},{9,11},{10,... | collective-permute-start | bytes 1572872 | tf_op jit(solution)/shard_map/ppermute | solution.py:55
  26.1 69.0 %collective-permute-start.5 = (bf16[512,512]{1,0:T(8,128)(2,1)}, bf16[512,512]{1,0:T(8,128)(2,1)}, u32[]{:S(2)}, u32[]{:S(2)}) collective-permute-start(bf16[512,512]{1,0:T(8,128)(2,1)} %get-tuple-element.22), channel_id=1, source_target_pairs={{0,1},{1,2},{2,3},{3,0},{4,5},{5,6},{6,7},{7,4},{8,9},{9,10},{10,1... | collective-permute-start | bytes 1572872 | tf_op jit(solution)/shard_map/ppermute | solution.py:55
  27.1 52.7 %collective-permute-start = (bf16[1,352,512]{2,1,0:T(8,128)(2,1)}, bf16[1,352,512]{2,1,0:T(8,128)(2,1)}, u32[]{:S(2)}, u32[]{:S(2)}) collective-permute-start(bf16[1,352,512]{2,1,0:T(8,128)(2,1)} %get-tuple-element.27), channel_id=1, source_target_pairs={{0,3},{1,0},{2,1},{3,2},{4,7},{5,4},{6,5},{7,6},{8,11},{9,8},{10,9... | collective-permute-start | bytes 1081352 | tf_op jit(solution)/shard_map/ppermute | solution.py:55
  29.8 51.1 %collective-permute-start.1 = (bf16[1,352,512]{2,1,0:T(8,128)(2,1)}, bf16[1,352,512]{2,1,0:T(8,128)(2,1)}, u32[]{:S(2)}, u32[]{:S(2)}) collective-permute-start(bf16[1,352,512]{2,1,0:T(8,128)(2,1)} %get-tuple-element.26), channel_id=1, source_target_pairs={{0,2},{1,3},{2,0},{3,1},{4,6},{5,7},{6,4},{7,5},{8,10},{9,11},{10,... | collective-permute-start | bytes 1081352 | tf_op jit(solution)/shard_map/ppermute | solution.py:55
  42.1 3.4 copy-start.17
  42.1 3.7 %copy-start.19 = (s32[4]{0:T(128)S(1)}, s32[4]{0:T(128)}, u32[]{:S(2)}) copy-start(s32[4]{0:T(128)} %param.32) | copy-start | bytes 52
  45.1 3.7 %copy-start.9 = (bf16[128,512]{1,0:T(8,128)(2,1)S(1)}, bf16[128,512]{1,0:T(8,128)(2,1)}, u32[]{:S(2)}) copy-start(bf16[128,512]{1,0:T(8,128)(2,1)} %copy.170) | copy-start | bytes 393220
  45.1 3.7 %copy-start.10 = (bf16[128,32]{1,0:T(8,128)(2,1)S(1)}, bf16[128,32]{1,0:T(8,128)(2,1)}, u32[]{:S(2)}) copy-start(bf16[128,32]{1,0:T(8,128)(2,1)} %copy.171) | copy-start | bytes 24580
  45.2 3.7 %copy-start.11 = (bf16[128,32]{1,0:T(8,128)(2,1)S(1)}, bf16[128,32]{1,0:T(8,128)(2,1)}, u32[]{:S(2)}) copy-start(bf16[128,32]{1,0:T(8,128)(2,1)} %copy.172) | copy-start | bytes 24580
  45.2 3.7 %copy-start.12 = (s32[4,4,8,4]{2,1,3,0:T(4,128)S(1)}, s32[4,4,8,4]{2,1,3,0:T(4,128)}, u32[]{:S(2)}) copy-start(s32[4,4,8,4]{2,1,3,0:T(4,128)} %copy.177) | copy-start | bytes 6148
  45.9 4.2 %copy-start.23 = (pred[4,4]{1,0:T(4,128)(4,1)S(1)}, pred[4,4]{1,0:T(4,128)(4,1)}, u32[]{:S(2)}) copy-start(pred[4,4]{1,0:T(4,128)(4,1)} %iota_compare_fusion.9) | copy-start | bytes 52
  53.3 2.2 copy-start.5
  57.6 7.7 %copy-start.3 = (bf16[512,2048]{1,0:T(8,128)(2,1)S(1)}, bf16[512,2048]{1,0:T(8,128)(2,1)}, u32[]{:S(2)}) copy-start(bf16[512,2048]{1,0:T(8,128)(2,1)} %param.25) | copy-start | bytes 6291460
  57.7 8.5 %copy-start.2 = (bf16[128,2048]{1,0:T(8,128)(2,1)S(1)}, bf16[128,2048]{1,0:T(8,128)(2,1)}, u32[]{:S(2)}) copy-start(bf16[128,2048]{1,0:T(8,128)(2,1)} %param.18) | copy-start | bytes 1572868
  79.8 8.5 %collective-permute-start.2 = (bf16[1,352,512]{2,1,0:T(8,128)(2,1)}, bf16[1,352,512]{2,1,0:T(8,128)(2,1)S(1)}, u32[]{:S(2)}, u32[]{:S(2)}) collective-permute-start(bf16[1,352,512]{2,1,0:T(8,128)(2,1)} %get-tuple-element.25), channel_id=1, source_target_pairs={{0,1},{1,2},{2,3},{3,0},{4,5},{5,6},{6,7},{7,4},{8,9},{9,10},{10,1... | collective-permute-start | bytes 1081352 | tf_op jit(solution)/shard_map/ppermute | solution.py:55
  88.3 4.6 %copy-start.7 = (bf16[8,512,512]{2,1,0:T(8,128)(2,1)S(1)}, bf16[8,512,512]{2,1,0:T(8,128)(2,1)}, u32[]{:S(2)}) copy-start(bf16[8,512,512]{2,1,0:T(8,128)(2,1)} %bitcast_dynamic-update-slice_fusion.6) | copy-start | bytes 12582916
  99.5 7.8 %copy-start.4 = (s32[128,1536]{1,0:T(8,128)S(1)}, s32[128,1536]{1,0:T(8,128)}, u32[]{:S(2)}) copy-start(s32[128,1536]{1,0:T(8,128)} %convert_reduce_fusion) | copy-start | bytes 2359300
  107.9 124.8 %copy-start.21 = (bf16[1,2048,352]{1,2,0:T(8,128)(2,1)S(1)}, bf16[1,2048,352]{1,2,0:T(8,128)(2,1)}, u32[]{:S(2)}) copy-start(bf16[1,2048,352]{1,2,0:T(8,128)(2,1)} %param.27) | copy-start | bytes 4325380
  168.3 70.5 %copy-start.22 = (bf16[1,2048,352]{1,2,0:T(8,128)(2,1)S(1)}, bf16[1,2048,352]{1,2,0:T(8,128)(2,1)}, u32[]{:S(2)}) copy-start(bf16[1,2048,352]{1,2,0:T(8,128)(2,1)} %param.28) | copy-start | bytes 4325380
  168.3 131.3 %all-gather.6.cloned.1.call-start = ((), (), s32[]{:S(2)}) async-start(), calls=%async_computation.3 | async-start | bytes 5898240 | tf_op jit(solution)/shard_map/all_gather | solution.py:40
  232.7 6.1 %copy-start.20 = (bf16[64,1,24,2048]{3,2,0,1:T(8,128)(2,1)S(1)}, bf16[64,1,24,2048]{3,2,0,1:T(8,128)(2,1)}, u32[]{:S(2)}) copy-start(bf16[64,1,24,2048]{3,2,0,1:T(8,128)(2,1)} %all-gather.4.cloned.1.call-done) | copy-start | bytes 18874372
  243.6 59.2 %copy-start.8 = (bf16[1,4,352,512]{3,2,1,0:T(8,128)(2,1)S(1)}, bf16[1,4,352,512]{3,2,1,0:T(8,128)(2,1)}, u32[]{:S(2)}) copy-start(bf16[1,4,352,512]{3,2,1,0:T(8,128)(2,1)} %constant_dynamic-slice_fusion.4) | copy-start | bytes 4325380
  305.6 12.9 %copy-start.15 = (f32[128,6]{0,1:T(8,128)S(1)}, f32[128,6]{0,1:T(8,128)}, u32[]{:S(2)}) copy-start(f32[128,6]{0,1:T(8,128)} %param.35) | copy-start | bytes 9220
  305.6 54.9 %copy-start.1 = (bf16[2048,768]{1,0:T(8,128)(2,1)S(1)}, bf16[2048,768]{1,0:T(8,128)(2,1)}, u32[]{:S(2)}) copy-start(bf16[2048,768]{1,0:T(8,128)(2,1)} %param.20) | copy-start | bytes 9437188
  307.6 49.8 %all-to-all-start.1 = ((bf16[64,1,24,512]{3,2,1,0:T(8,128)(2,1)}), bf16[64,1,24,512]{3,2,1,0:T(8,128)(2,1)}, u32[]{:S(2)}, u32[]{:S(2)}) async-start(bf16[64,1,24,512]{3,2,1,0:T(8,128)(2,1)} %copy.196), calls=%async_computation.1 | async-start | bytes 3145728 | tf_op jit(solution)/shard_map/all_to_all | solution.py:66
Sparse Core Ops, SparseCore 0:
  168.4 64.2 all-gather.3
  243.7 55.8 all-gather.5

commit v9 on v8

--- a/solution.py
+++ b/solution.py
@@ -33,14 +33,23 @@
     )
 
 
-def expert_math(arrived, gate_w, up_w, down_cols):
+def expert_math(arrived, gate_w, up_w, down_pieces):
     gate_val = jnp.einsum("nesd,edf->nesf", arrived, gate_w, preferred_element_type=jnp.float32)
     up_val = jnp.einsum("nesd,edf->nesf", arrived, up_w, preferred_element_type=jnp.float32)
     active = (jax.nn.silu(gate_val) * up_val).astype(jnp.bfloat16)
     active_all = lax.all_gather(active, "tp", axis=0)
-    return jnp.einsum(
-        "tnesf,etfd->nesd", active_all, down_cols, preferred_element_type=jnp.float32
-    ).astype(jnp.bfloat16)
+    tp_count = lax.axis_size("tp")
+    tp_index = lax.axis_index("tp")
+    total = None
+    for shift in range(tp_count):
+        source = lax.dynamic_index_in_dim(
+            active_all, (tp_index - shift) % tp_count, 0, keepdims=False
+        )
+        term = jnp.einsum(
+            "nesf,efd->nesd", source, down_pieces[shift], preferred_element_type=jnp.float32
+        )
+        total = term if total is None else total + term
+    return total.astype(jnp.bfloat16)
 
 
 def by_columns(weight):
@@ -56,10 +65,7 @@
                 piece, "tp", [(s, (s + shift) % tp_count) for s in range(tp_count)]
             )
         pieces[shift] = piece
-    reverse = [pieces[(-shift) % tp_count] for shift in range(tp_count)]
-    doubled = jnp.stack(reverse + reverse, axis=weight.ndim - 2)
-    start = (tp_count - tp_index) % tp_count
-    return lax.dynamic_slice_in_dim(doubled, start, tp_count, weight.ndim - 2)
+    return pieces
 
 
 def send_home(shares):
@@ -208,11 +214,18 @@
     tp_index = lax.axis_index("tp")
     col_start = tp_index * col_share
     head_all = lax.all_gather(head_out, "tp", axis=1, tiled=True)
-    head_all, down_cols, out_cols = lax.optimization_barrier(
+    head_all, down_pieces, out_pieces = lax.optimization_barrier(
         (head_all, by_columns(down_late), by_columns(out_late))
     )
+    head_blocks = [
+        head_all[:, block * col_share : (block + 1) * col_share] for block in range(tp_count)
+    ]
+    head_doubled = jnp.concatenate(head_blocks[::-1] + head_blocks[::-1], axis=1)
+    head_shift = lax.dynamic_slice_in_dim(
+        head_doubled, (tp_count - 1 - tp_index) * col_share, tp_count * col_share, 1
+    )
     attn_cols = jnp.dot(
-        head_all, out_cols.reshape(-1, col_share), preferred_element_type=jnp.float32
+        head_shift, jnp.concatenate(out_pieces, axis=0), preferred_element_type=jnp.float32
     )
     hidden_cols = lax.dynamic_slice_in_dim(hidden_f, col_start, col_share, 1)
     resid_cols = hidden_cols + attn_cols
@@ -231,7 +244,7 @@
         tiled=True,
     )
     arrived = lax.all_gather(arrived_cols, "tp", axis=3, tiled=True)
-    shares = expert_math(arrived, w_gate, w_up, down_cols)
+    shares = expert_math(arrived, w_gate, w_up, down_pieces)
     returned = send_home(shares)
     combined = jnp.dot(
         weight_rows, returned.reshape(slot_count, col_share).astype(jnp.float32), precision=highest

time: 368 us -> 349 us (0.948)
  local copies, waits for them, and re-layouts: 37.6 us -> 20.7 us
  waiting for transfers between devices: 164 us -> 157 us
    unnamed x65 -> x58, local copies, waits for them, and re-layouts: 13.2 us -> 0.61 us
    ppermute x6, waiting for transfers between devices: 6.36 us -> 0.02 us  [by_columns(): lax.ppermute(piece, 'tp', [(s, (s + shift) % tp_count) for s in range(tp_...]
    psum x1, blocking collectives: 6.01 us -> 9.97 us  [local(): lax.psum(jnp.sum(resid_cols * resid_cols, axis=-1, keepdims=True), 'tp')]
    dot_general x2 -> x5, matrix products: 4.28 us -> 8.03 us  [the longest x4 6.03 us: expert_math(): jnp.einsum('nesf,efd->nesd', source, down_pieces[shift], preferred_elemen...]
  transfers between devices with their start and end apart: 9 -> 9, of which waited for: 4 -> 3; matrix products, arithmetic and copies ran while one was open for 13% -> 10% of each run, Pallas kernels for 0% -> 0%
where the time goes in v9:
time: 349 us
  waiting for transfers between devices  157 us (45%)
  blocking collectives  91.1 us (26%)
  matrix products  36.7 us (11%)
  local copies, waits for them, and re-layouts  20.7 us (6%)
  starting transfers between devices  18.3 us (5%)
  between operations  14.2 us (4%)
  other arithmetic  11.1 us (3%)
    all_gather x1, waiting for transfers between devices, local(): arrived = lax.all_gather(arrived_cols, 'tp', axis=3, tiled=True)  63.2 us
    all_to_all x1, blocking collectives, local(): lax.all_to_all(placed.reshape(req_count, EXP_DEV, capacity, col_share), '...  59.8 us
    all_gather x1, waiting for transfers between devices, expert_math(): active_all = lax.all_gather(active, 'tp', axis=0)  56 us
    all_to_all x1, waiting for transfers between devices, send_home(): lax.all_to_all(shares, 'req', split_axis=0, concat_axis=0, tiled=True)  37.4 us
    all_gather x1, blocking collectives, local(): kv_all = lax.all_gather(kv_part, 'tp', axis=1, tiled=True)  11.2 us
    all_to_all x1, starting transfers between devices, send_home(): lax.all_to_all(shares, 'req', split_axis=0, concat_axis=0, tiled=True)  11 us
    all_gather x1, blocking collectives, local(): head_all = lax.all_gather(head_out, 'tp', axis=1, tiled=True)  10.1 us
    psum x1, blocking collectives, local(): lax.psum(jnp.sum(resid_cols * resid_cols, axis=-1, keepdims=True), 'tp')  9.97 us
  transfers between devices with their start and end apart: 9, of which 3 were waited for; matrix products, arithmetic and copies ran while one was open for 10% of the time, Pallas kernels for 0%

profile of v9, /device:TPU:1, one launch (start us, length us, event | category | flops | bytes accessed | tf_op | source)
XLA Modules:
  0.0 348.8 jit_solution(1744184749018806944)
XLA Ops:
  6.5 1.4 multiply_reduce_fusion
  7.9 1.6 fusion.71
  9.6 11.2 %all_gather.15 = f32[128,576]{0,1:T(8,128)S(1)} all-gather(f32[128,144]{0,1:T(8,128)S(1)} %fusion.71), channel_id=1, replica_groups=mesh['req'=64,'tp'=4] {'tp'}, dimensions={1}, use_global_device_ids=true | all-gather | bytes 368640 | tf_op jit(solution)/shard_map/all_gather | solution.py:122
  20.7 3.0 constant_dynamic-slice_fusion.4
  23.7 0.8 collective-permute-start.3
  24.6 2.4 collective-permute-start.4
  27.0 1.2 constant_dynamic-slice_fusion.8
  28.2 1.4 collective-permute-start
  29.6 0.6 collective-permute-start.1
  30.2 0.6 iota_compare_fusion.9
  30.8 2.1 convert_element_type.71
  33.3 0.1 select_reduce_fusion.3
  33.5 0.2 select_reduce_fusion.5
  33.8 0.3 select_reduce_fusion.6
  34.3 0.6 copy.189
  35.0 0.8 multiply_convert_fusion.2
  35.8 1.7 copy.182
  37.7 0.2 multiply_cosine_fusion
  37.9 0.7 copy.183
  38.6 0.7 copy.184
  39.3 0.7 copy.176
  40.0 0.7 copy.178
  40.7 2.4 fusion.72
  43.5 1.4 fusion.32
  45.1 0.5 copy.179
  45.6 0.3 reshape.305
  46.4 2.8 fusion.82
  49.4 0.4 fusion.31
  49.8 0.9 slice.83
  50.7 1.0 fusion.83
  51.8 0.2 copy.192
  52.0 0.2 fusion.61
  52.2 1.3 reshape.307
  53.6 0.3 exponential_reduce_fusion
  54.0 0.2 copy.194
  54.2 1.9 fusion.49
  56.1 2.2 fusion.30
  58.4 0.2 copy.218
  58.6 1.8 reduce-window.6
  60.4 0.3 slice_reduce_fusion
  60.7 0.1 fusion.64
  61.1 0.8 dynamic_slice.56
  61.8 0.3 convolution_convert_fusion.2
  62.2 2.0 collective-permute-start.2
  64.2 0.6 convert_reduce_fusion
  64.8 10.1 %all_gather.16 = bf16[128,2048]{0,1:T(8,128)(2,1)S(1)} all-gather(bf16[128,512]{0,1:T(8,128)(2,1)S(1)} %bitcast.197), channel_id=1, replica_groups=mesh['req'=64,'tp'=4] {'tp'}, dimensions={1}, use_global_device_ids=true | all-gather | bytes 655360 | tf_op jit(solution)/shard_map/all_gather | solution.py:216
  75.2 2.0 multiply_reduce_fusion.1
  77.2 10.0 %psum.7 = f32[128,1]{0,1:T(1,128)S(1)} all-reduce(f32[128,1]{0,1:T(1,128)S(1)} %bitcast.210), channel_id=1, replica_groups=mesh['req'=64,'tp'=4] {'tp'}, use_global_device_ids=true, to_apply=%region_19.20 | all-reduce | flops 128 | bytes 1024 | tf_op jit(solution)/shard_map/psum | solution.py:232
  87.2 0.6 convolution_convert_fusion
  87.9 59.8 %all_to_all.10 = bf16[64,1,24,512]{3,2,1,0:T(8,128)(2,1)} all-to-all(bf16[64,1,24,512]{3,2,1,0:T(8,128)(2,1)S(1)} %bitcast.188), channel_id=1, replica_groups=mesh['req'=64,'tp'=4] {'req'}, dimensions={0} | all-to-all | bytes 3145728 | tf_op jit(solution)/shard_map/all_to_all | solution.py:239
  147.7 63.2 %all-gather.4.cloned.1.call-done = bf16[64,1,24,2048]{3,2,0,1:T(8,128)(2,1)} async-done(((bf16[64,1,24,512]{3,2,0,1:T(8,128)(2,1)}), bf16[64,1,24,2048]{3,2,0,1:T(8,128)(2,1)}) %all-gather.4.cloned.1.call-update) | async-done | bytes 6291472 | tf_op jit(solution)/shard_map/all_gather | solution.py:246
  211.0 6.1 %fusion.2 = f32[64,24,352]{2,1,0:T(8,128)S(1)} fusion(bf16[64,1,24,2048]{3,2,0,1:T(8,128)(2,1)} %all-gather.4.cloned.1.call-done, bf16[1,2048,352]{1,2,0:T(8,128)(2,1)} %param.27), kind=kOutput, calls=%fused_computation.2 | convolution fusion | flops 2214592512 | bytes 9895936 | tf_op jit(solution)/shard_map/nesd,edf->nesf/dot_general | solution.py:37
  217.1 4.8 %fusion.22 = bf16[64,1,24,352]{3,2,1,0:T(8,128)(2,1)} fusion(bf16[1,2048,352]{1,2,0:T(8,128)(2,1)S(1)} %copy-done.22, bf16[64,1,24,2048]{3,2,0,1:T(8,128)(2,1)S(1)} %copy-done.21, f32[64,24,352]{2,1,0:T(8,128)S(1)} %fusion.2), kind=kOutput, calls=%fused_computation.30 | convolution fusion | flops 2217836544 | bytes 10977280 | tf_op jit(solution)/shard_map/nesd,edf->nesf/dot_general | solution.py:38
  222.0 56.0 %all-gather.6.cloned.1.call-done = bf16[256,1,24,352]{3,2,1,0:T(8,128)(2,1)} async-done(((bf16[64,1,24,352]{3,2,1,0:T(8,128)(2,1)}), bf16[256,1,24,352]{3,2,1,0:T(8,128)(2,1)}) %all-gather.6.cloned.1.call-update) | async-done | bytes 4325392 | tf_op jit(solution)/shard_map/all_gather | solution.py:40
  278.0 2.8 constant_dynamic-slice_fusion
  280.8 2.0 fusion.34
  282.8 1.0 fusion.35
  283.8 2.0 fusion.33
  285.8 1.1 fusion.19
  286.9 2.0 copy.211
  288.9 11.0 %all-to-all-start.1 = ((bf16[64,1,24,512]{3,2,1,0:T(8,128)(2,1)}), bf16[64,1,24,512]{3,2,1,0:T(8,128)(2,1)}, u32[]{:S(2)}, u32[]{:S(2)}) async-start(bf16[64,1,24,512]{3,2,1,0:T(8,128)(2,1)} %copy.211), calls=%async_computation.1 | async-start | bytes 3145728 | tf_op jit(solution)/shard_map/all_to_all | solution.py:72
  299.9 1.5 select_reduce_fusion
  301.4 37.4 %all-to-all-done.1 = bf16[64,1,24,512]{3,2,1,0:T(8,128)(2,1)} async-done(((bf16[64,1,24,512]{3,2,1,0:T(8,128)(2,1)}), bf16[64,1,24,512]{3,2,1,0:T(8,128)(2,1)}, u32[]{:S(2)}, u32[]{:S(2)}) %all-to-all-start.1) | async-done | bytes 1572896 | tf_op jit(solution)/shard_map/all_to_all | solution.py:72
  338.8 3.1 fusion.40
  (116 shorter events, 2.8 us)
Async XLA Ops:
  6.5 34.2 %copy-start = (bf16[2048,768]{1,0:T(8,128)(2,1)S(1)}, bf16[2048,768]{1,0:T(8,128)(2,1)}, u32[]{:S(2)}) copy-start(bf16[2048,768]{1,0:T(8,128)(2,1)} %param.20) | copy-start | bytes 9437188
  6.5 204.4 %all-gather.4.cloned.1.call-start = ((), (), s32[]{:S(2)}) async-start(), calls=%async_computation.2 | async-start | bytes 7864320 | tf_op jit(solution)/shard_map/all_gather | solution.py:246
  20.7 6.3 %copy-start.3 = (bf16[1,352,2048]{2,1,0:T(8,128)(2,1)S(1)}, bf16[1,352,2048]{2,1,0:T(8,128)(2,1)}, u32[]{:S(2)}) copy-start(bf16[1,352,2048]{2,1,0:T(8,128)(2,1)} %param.29) | copy-start | bytes 4325380
  23.7 51.2 %collective-permute-start.3 = (bf16[512,512]{1,0:T(8,128)(2,1)}, bf16[512,512]{1,0:T(8,128)(2,1)}, u32[]{:S(2)}, u32[]{:S(2)}) collective-permute-start(bf16[512,512]{1,0:T(8,128)(2,1)} %get-tuple-element.40), channel_id=1, source_target_pairs={{0,1},{1,2},{2,3},{3,0},{4,5},{5,6},{6,7},{7,4},{8,9},{9,10},{10,1... | collective-permute-start | bytes 1572872 | tf_op jit(solution)/shard_map/ppermute | solution.py:64
  24.6 50.4 %collective-permute-start.4 = (bf16[512,512]{1,0:T(8,128)(2,1)}, bf16[512,512]{1,0:T(8,128)(2,1)}, u32[]{:S(2)}, u32[]{:S(2)}) collective-permute-start(bf16[512,512]{1,0:T(8,128)(2,1)} %get-tuple-element.39), channel_id=1, source_target_pairs={{0,2},{1,3},{2,0},{3,1},{4,6},{5,7},{6,4},{7,5},{8,10},{9,11},{10,... | collective-permute-start | bytes 1572872 | tf_op jit(solution)/shard_map/ppermute | solution.py:64
  27.0 5.9 %copy-start.14 = (s32[128,6]{0,1:T(8,128)S(1)}, s32[128,6]{0,1:T(8,128)}, u32[]{:S(2)}) copy-start(s32[128,6]{0,1:T(8,128)} %param.34) | copy-start | bytes 9220
  27.0 6.3 %copy-start.15 = (s32[4,3,8]{2,0,1:T(4,128)S(1)}, s32[4,3,8]{2,0,1:T(4,128)}, u32[]{:S(2)}) copy-start(s32[4,3,8]{2,0,1:T(4,128)} %param.33) | copy-start | bytes 1156
  27.0 8.0 %copy-start.17 = (f32[512]{0:T(512)S(1)}, f32[512]{0:T(512)}, u32[]{:S(2)}) copy-start(f32[512]{0:T(512)} %param.22) | copy-start | bytes 6148
  27.0 48.0 %collective-permute-start.5 = (bf16[512,512]{1,0:T(8,128)(2,1)}, bf16[512,512]{1,0:T(8,128)(2,1)}, u32[]{:S(2)}, u32[]{:S(2)}) collective-permute-start(bf16[512,512]{1,0:T(8,128)(2,1)} %get-tuple-element.38), channel_id=1, source_target_pairs={{0,3},{1,0},{2,1},{3,2},{4,7},{5,4},{6,5},{7,6},{8,11},{9,8},{10,9... | collective-permute-start | bytes 1572872 | tf_op jit(solution)/shard_map/ppermute | solution.py:64
  28.2 9.3 %copy-start.19 = (s32[4]{0:T(128)S(1)}, s32[4]{0:T(128)}, u32[]{:S(2)}) copy-start(s32[4]{0:T(128)} %param.32) | copy-start | bytes 52
  28.2 34.0 %collective-permute-start = (bf16[1,352,512]{2,1,0:T(8,128)(2,1)}, bf16[1,352,512]{2,1,0:T(8,128)(2,1)}, u32[]{:S(2)}, u32[]{:S(2)}) collective-permute-start(bf16[1,352,512]{2,1,0:T(8,128)(2,1)} %get-tuple-element.44), channel_id=1, source_target_pairs={{0,1},{1,2},{2,3},{3,0},{4,5},{5,6},{6,7},{7,4},{8,9},{9,10},{10,1... | collective-permute-start | bytes 1081352 | tf_op jit(solution)/shard_map/ppermute | solution.py:64
  29.6 45.4 %collective-permute-start.1 = (bf16[1,352,512]{2,1,0:T(8,128)(2,1)}, bf16[1,352,512]{2,1,0:T(8,128)(2,1)}, u32[]{:S(2)}, u32[]{:S(2)}) collective-permute-start(bf16[1,352,512]{2,1,0:T(8,128)(2,1)} %get-tuple-element.43), channel_id=1, source_target_pairs={{0,2},{1,3},{2,0},{3,1},{4,6},{5,7},{6,4},{7,5},{8,10},{9,11},{10,... | collective-permute-start | bytes 1081352 | tf_op jit(solution)/shard_map/ppermute | solution.py:64
  43.2 1.7 copy-start.8
  43.2 1.7 copy-start.9
  45.0 1.0 copy-start.18
  45.0 1.3 copy-start.20
  46.4 3.0 copy-start.10
  46.4 3.0 copy-start.11
  46.4 3.0 copy-start.12
  46.4 3.0 copy-start.13
  49.3 1.4 copy-start.23
  53.9 2.2 copy-start.2
  56.1 2.3 copy-start.5
  58.3 3.9 %copy-start.7 = (bf16[1,352,512]{2,1,0:T(8,128)(2,1)S(1)}, bf16[1,352,512]{2,1,0:T(8,128)(2,1)}, u32[]{:S(2)}) copy-start(bf16[1,352,512]{2,1,0:T(8,128)(2,1)} %get-tuple-element.42) | copy-start | bytes 1081348
  61.8 13.4 %copy-start.6 = (bf16[512,512]{1,0:T(8,128)(2,1)S(1)}, bf16[512,512]{1,0:T(8,128)(2,1)}, u32[]{:S(2)}) copy-start(bf16[512,512]{1,0:T(8,128)(2,1)} %get-tuple-element.21) | copy-start | bytes 1572868
  62.2 12.8 %collective-permute-start.2 = (bf16[1,352,512]{2,1,0:T(8,128)(2,1)S(1)}, bf16[1,352,512]{2,1,0:T(8,128)(2,1)S(1)}, u32[]{:S(2)}, u32[]{:S(2)}) collective-permute-start(bf16[1,352,512]{2,1,0:T(8,128)(2,1)S(1)} %copy-done.7), channel_id=1, source_target_pairs={{0,3},{1,0},{2,1},{3,2},{4,7},{5,4},{6,5},{7,6},{8,11},{9,8},{10,9... | collective-permute-start | bytes 1081352 | tf_op jit(solution)/shard_map/ppermute | solution.py:64
  147.7 69.4 %copy-start.22 = (bf16[1,2048,352]{1,2,0:T(8,128)(2,1)S(1)}, bf16[1,2048,352]{1,2,0:T(8,128)(2,1)}, u32[]{:S(2)}) copy-start(bf16[1,2048,352]{1,2,0:T(8,128)(2,1)} %param.28) | copy-start | bytes 4325380
  147.7 130.3 %all-gather.6.cloned.1.call-start = ((), (), s32[]{:S(2)}) async-start(), calls=%async_computation.3 | async-start | bytes 5898240 | tf_op jit(solution)/shard_map/all_gather | solution.py:40
  211.0 6.1 %copy-start.21 = (bf16[64,1,24,2048]{3,2,0,1:T(8,128)(2,1)S(1)}, bf16[64,1,24,2048]{3,2,0,1:T(8,128)(2,1)}, u32[]{:S(2)}) copy-start(bf16[64,1,24,2048]{3,2,0,1:T(8,128)(2,1)} %all-gather.4.cloned.1.call-done) | copy-start | bytes 18874372
  280.8 2.0 copy-start.4
  288.9 11.0 %copy-start.16 = (f32[128,6]{0,1:T(8,128)S(1)}, f32[128,6]{0,1:T(8,128)}, u32[]{:S(2)}) copy-start(f32[128,6]{0,1:T(8,128)} %param.35) | copy-start | bytes 9220
  288.9 49.9 %all-to-all-start.1 = ((bf16[64,1,24,512]{3,2,1,0:T(8,128)(2,1)}), bf16[64,1,24,512]{3,2,1,0:T(8,128)(2,1)}, u32[]{:S(2)}, u32[]{:S(2)}) async-start(bf16[64,1,24,512]{3,2,1,0:T(8,128)(2,1)} %copy.211), calls=%async_computation.1 | async-start | bytes 3145728 | tf_op jit(solution)/shard_map/all_to_all | solution.py:72
  299.9 42.0 %copy-start.1 = (bf16[2048,768]{1,0:T(8,128)(2,1)S(1)}, bf16[2048,768]{1,0:T(8,128)(2,1)}, u32[]{:S(2)}) copy-start(bf16[2048,768]{1,0:T(8,128)(2,1)} %param.20) | copy-start | bytes 9437188
Sparse Core Ops, SparseCore 0:
  147.8 63.1 all-gather.3
  222.1 55.8 all-gather.5

commit v10 on v9

--- a/solution.py
+++ b/solution.py
@@ -50,6 +50,16 @@
         )
         total = term if total is None else total + term
     return total.astype(jnp.bfloat16)
+
+
+def tp_shifted(values):
+    tp_count = lax.axis_size("tp")
+    pieces = [values]
+    for shift in range(1, tp_count):
+        pieces.append(
+            lax.ppermute(values, "tp", [(s, (s + shift) % tp_count) for s in range(tp_count)])
+        )
+    return pieces
 
 
 def by_columns(weight):
@@ -119,7 +129,13 @@
         jnp.bfloat16
     )
     kv_part = jnp.dot(normed, w_latent, preferred_element_type=jnp.float32)
-    kv_all = lax.all_gather(kv_part, "tp", axis=1, tiled=True)
+    kv_pieces = tp_shifted(kv_part)[::-1]
+    kv_all = lax.dynamic_slice_in_dim(
+        jnp.concatenate(kv_pieces + kv_pieces, axis=1),
+        (tp_count - 1 - lax.axis_index("tp")) * kv_part.shape[1],
+        tp_count * kv_part.shape[1],
+        1,
+    )
     kv_all, down_late, out_late = lax.optimization_barrier((kv_all, w_down, w_out))
     new_lat = kv_all[:, :LATENT] * rms_scale(kv_all[:, :LATENT]) * kv_gain
     new_rope = rotate(kv_all[:, LATENT:], cos_val, sin_val)
@@ -213,23 +229,16 @@
     weight_rows = jnp.sum(jnp.where(slot_hot, route_weights[:, :, None], 0.0), axis=1)
     tp_index = lax.axis_index("tp")
     col_start = tp_index * col_share
-    head_all = lax.all_gather(head_out, "tp", axis=1, tiled=True)
-    head_all, down_pieces, out_pieces = lax.optimization_barrier(
-        (head_all, by_columns(down_late), by_columns(out_late))
-    )
-    head_blocks = [
-        head_all[:, block * col_share : (block + 1) * col_share] for block in range(tp_count)
-    ]
-    head_doubled = jnp.concatenate(head_blocks[::-1] + head_blocks[::-1], axis=1)
-    head_shift = lax.dynamic_slice_in_dim(
-        head_doubled, (tp_count - 1 - tp_index) * col_share, tp_count * col_share, 1
+    head_shift = jnp.concatenate(tp_shifted(head_out), axis=1)
+    head_shift, down_pieces, out_pieces = lax.optimization_barrier(
+        (head_shift, by_columns(down_late), by_columns(out_late))
     )
     attn_cols = jnp.dot(
         head_shift, jnp.concatenate(out_pieces, axis=0), preferred_element_type=jnp.float32
     )
     hidden_cols = lax.dynamic_slice_in_dim(hidden_f, col_start, col_share, 1)
     resid_cols = hidden_cols + attn_cols
-    square_sum = lax.psum(jnp.sum(resid_cols * resid_cols, axis=-1, keepdims=True), "tp")
+    square_sum = sum(tp_shifted(jnp.sum(resid_cols * resid_cols, axis=-1, keepdims=True)))
     moe_scale = lax.rsqrt(square_sum / D + eps)
     gain_cols = lax.dynamic_slice_in_dim(moe_gain, col_start, col_share, 0)
     moe_in_cols = (resid_cols * moe_scale * gain_cols).astype(jnp.bfloat16)

time: 349 us -> 365 us (1.046)
  blocking collectives: 91.1 us -> 52.7 us
  waiting for transfers between devices: 157 us -> 193 us
  starting transfers between devices: 18.3 us -> 31.1 us
  local copies, waits for them, and re-layouts: 20.7 us -> 24.6 us
    ppermute x6, waiting for transfers between devices: 0.02 us -> 28.4 us  [by_columns(): lax.ppermute(piece, 'tp', [(s, (s + shift) % tp_count) for s in range(tp_...]
    all_gather x2 -> x0, blocking collectives: 21.3 us -> none  [the longest x1 11.2 us: local(): kv_all = lax.all_gather(kv_part, 'tp', axis=1, tiled=True)]
    ppermute x0 -> x9, starting transfers between devices: none -> 13.3 us  [tp_shifted(): lax.ppermute(values, 'tp', [(s, (s + shift) % tp_count) for s in range(tp...]
    psum x1 -> x0, blocking collectives: 9.97 us -> none  [local(): lax.psum(jnp.sum(resid_cols * resid_cols, axis=-1, keepdims=True), 'tp')]
    unnamed x58 -> x66, local copies, waits for them, and re-layouts: 0.61 us -> 7.92 us
    ppermute x0 -> x9, waiting for transfers between devices: none -> 7.25 us  [tp_shifted(): lax.ppermute(values, 'tp', [(s, (s + shift) % tp_count) for s in range(tp...]
    all_to_all x1, blocking collectives: 59.8 us -> 52.7 us  [local(): lax.all_to_all(placed.reshape(req_count, EXP_DEV, capacity, col_share), '...]
  transfers between devices with their start and end apart: 9 -> 18, of which waited for: 3 -> 8; matrix products, arithmetic and copies ran while one was open for 10% -> 5% of each run, Pallas kernels for 0% -> 0%
where the time goes in v10:
time: 365 us; the launch traced here: 362 us
  waiting for transfers between devices  193 us (53%)
  blocking collectives  52.7 us (14%)
  matrix products  36.4 us (10%)
  starting transfers between devices  31.1 us (9%)
  local copies, waits for them, and re-layouts  24.6 us (7%)
  between operations  14.6 us (4%)
  other arithmetic  9.43 us (3%)
    all_gather x1, waiting for transfers between devices, local(): arrived = lax.all_gather(arrived_cols, 'tp', axis=3, tiled=True)  63.9 us
    all_gather x1, waiting for transfers between devices, expert_math(): active_all = lax.all_gather(active, 'tp', axis=0)  56 us
    all_to_all x1, blocking collectives, local(): lax.all_to_all(placed.reshape(req_count, EXP_DEV, capacity, col_share), '...  52.7 us
    all_to_all x1, waiting for transfers between devices, send_home(): lax.all_to_all(shares, 'req', split_axis=0, concat_axis=0, tiled=True)  37.4 us
    ppermute x6, waiting for transfers between devices, by_columns(): lax.ppermute(piece, 'tp', [(s, (s + shift) % tp_count) for s in range(tp_...  28.4 us
    ppermute x9, starting transfers between devices, tp_shifted(): lax.ppermute(values, 'tp', [(s, (s + shift) % tp_count) for s in range(tp...  13.3 us
    all_to_all x1, starting transfers between devices, send_home(): lax.all_to_all(shares, 'req', split_axis=0, concat_axis=0, tiled=True)  11 us
    unnamed x66, local copies, waits for them, and re-layouts  7.92 us
  transfers between devices with their start and end apart: 18, of which 8 were waited for; matrix products, arithmetic and copies ran while one was open for 5% of the time, Pallas kernels for 0%

profile of v10, /device:TPU:1, one launch (start us, length us, event | category | flops | bytes accessed | tf_op | source)
XLA Modules:
  0.0 361.7 jit_solution(17902060149573003389)
XLA Ops:
  6.6 1.4 multiply_reduce_fusion
  8.0 2.3 fusion.70
  10.3 3.3 collective-permute-start
  13.6 0.5 collective-permute-start.1
  14.1 0.8 collective-permute-start.2
  14.8 0.5 multiply_power_fusion
  15.4 0.8 copy.200
  17.5 0.6 copy.189
  18.2 0.7 mul.197
  18.9 2.4 fusion.71
  21.7 1.4 fusion.32
  23.4 1.0 copy.218
  24.5 1.8 reduce-window.6
  26.7 0.9 constant_dynamic-update-slice_fusion.7
  27.6 0.9 constant_dynamic-update-slice_fusion.6
  28.4 0.9 constant_dynamic-update-slice_fusion.5
  29.3 0.9 constant_dynamic-update-slice_fusion.4
  30.2 0.9 constant_dynamic-update-slice_fusion.3
  31.1 0.9 constant_dynamic-update-slice_fusion.2
  32.0 0.9 constant_dynamic-update-slice_fusion.1
  32.9 0.9 constant_dynamic-update-slice_fusion
  35.0 0.5 copy.179
  35.9 2.8 fusion.80
  39.2 0.8 slice.67
  40.0 1.0 fusion.81
  41.6 1.3 reshape.307
  43.5 1.9 fusion.49
  45.4 2.2 fusion.30
  47.7 1.1 constant_dynamic-slice_fusion.8
  48.8 1.5 collective-permute-start.6
  50.8 2.3 collective-permute-start.4
  53.1 1.7 collective-permute-start.5
  54.8 1.4 constant_dynamic-slice_fusion.4
  56.2 1.2 collective-permute-start.10
  57.4 4.2 %collective-permute-done.3 = bf16[128,512]{0,1:T(8,128)(2,1)S(1)} collective-permute-done((bf16[128,512]{0,1:T(8,128)(2,1)S(1)}, bf16[128,512]{0,1:T(8,128)(2,1)S(1)}, u32[]{:S(2)}, u32[]{:S(2)}) %collective-permute-start.3) | collective-permute-done | bytes 131104 | tf_op jit(solution)/shard_map/ppermute | solution.py:60
  61.6 0.9 collective-permute-start.11
  62.4 2.1 collective-permute-done.4
  65.5 1.3 collective-permute-start.7
  66.8 1.6 collective-permute-start.8
  68.4 1.1 pad_maximum_fusion.1
  69.5 25.6 %collective-permute-done.7 = bf16[1,352,512]{2,1,0:T(8,128)(2,1)S(1)} collective-permute-done((bf16[1,352,512]{2,1,0:T(8,128)(2,1)}, bf16[1,352,512]{2,1,0:T(8,128)(2,1)S(1)}, u32[]{:S(2)}, u32[]{:S(2)}) %collective-permute-start.7) | collective-permute-done | bytes 360480 | tf_op jit(solution)/shard_map/ppermute | solution.py:74
  95.1 2.8 collective-permute-done.8
  97.9 2.0 multiply_reduce_fusion.1
  99.9 2.1 collective-permute-start.12
  102.0 2.5 collective-permute-start.13
  104.5 0.6 convert_reduce_fusion
  105.2 0.8 dynamic_slice.56
  105.9 0.9 collective-permute-done.14
  106.9 0.6 convolution_convert_fusion
  107.5 52.7 %all_to_all.10 = bf16[64,1,24,512]{3,2,1,0:T(8,128)(2,1)} all-to-all(bf16[64,1,24,512]{3,2,1,0:T(8,128)(2,1)S(1)} %bitcast.190), channel_id=1, replica_groups=mesh['req'=64,'tp'=4] {'req'}, dimensions={0} | all-to-all | bytes 3145728 | tf_op jit(solution)/shard_map/all_to_all | solution.py:248
  160.6 63.9 %all-gather.4.cloned.1.call-done = bf16[64,1,24,2048]{3,2,0,1:T(8,128)(2,1)} async-done(((bf16[64,1,24,512]{3,2,0,1:T(8,128)(2,1)}), bf16[64,1,24,2048]{3,2,0,1:T(8,128)(2,1)}) %all-gather.4.cloned.1.call-update) | async-done | bytes 6291472 | tf_op jit(solution)/shard_map/all_gather | solution.py:255
  224.4 6.1 %fusion.2 = f32[64,24,352]{2,1,0:T(8,128)S(1)} fusion(bf16[64,1,24,2048]{3,2,0,1:T(8,128)(2,1)} %all-gather.4.cloned.1.call-done, bf16[1,2048,352]{1,2,0:T(8,128)(2,1)} %param.27), kind=kOutput, calls=%fused_computation.2 | convolution fusion | flops 2214592512 | bytes 9895936 | tf_op jit(solution)/shard_map/nesd,edf->nesf/dot_general | solution.py:37
  230.6 4.8 %fusion.22 = bf16[64,1,24,352]{3,2,1,0:T(8,128)(2,1)} fusion(bf16[1,2048,352]{1,2,0:T(8,128)(2,1)S(1)} %copy-done.27, bf16[64,1,24,2048]{3,2,0,1:T(8,128)(2,1)S(1)} %copy-done.26, f32[64,24,352]{2,1,0:T(8,128)S(1)} %fusion.2), kind=kOutput, calls=%fused_computation.30 | convolution fusion | flops 2217836544 | bytes 10977280 | tf_op jit(solution)/shard_map/nesd,edf->nesf/dot_general | solution.py:38
  235.5 56.0 %all-gather.6.cloned.1.call-done = bf16[256,1,24,352]{3,2,1,0:T(8,128)(2,1)} async-done(((bf16[64,1,24,352]{3,2,1,0:T(8,128)(2,1)}), bf16[256,1,24,352]{3,2,1,0:T(8,128)(2,1)}) %all-gather.6.cloned.1.call-update) | async-done | bytes 4325392 | tf_op jit(solution)/shard_map/all_gather | solution.py:40
  291.5 2.8 constant_dynamic-slice_fusion
  294.3 2.0 fusion.34
  296.3 1.0 fusion.35
  297.3 1.0 fusion.33
  298.3 1.1 fusion.19
  299.4 2.0 copy.211
  301.4 11.0 %all-to-all-start.1 = ((bf16[64,1,24,512]{3,2,1,0:T(8,128)(2,1)}), bf16[64,1,24,512]{3,2,1,0:T(8,128)(2,1)}, u32[]{:S(2)}, u32[]{:S(2)}) async-start(bf16[64,1,24,512]{3,2,1,0:T(8,128)(2,1)} %copy.211), calls=%async_computation.1 | async-start | bytes 3145728 | tf_op jit(solution)/shard_map/all_to_all | solution.py:82
  312.4 1.5 select_reduce_fusion
  313.9 37.4 %all-to-all-done.1 = bf16[64,1,24,512]{3,2,1,0:T(8,128)(2,1)} async-done(((bf16[64,1,24,512]{3,2,1,0:T(8,128)(2,1)}), bf16[64,1,24,512]{3,2,1,0:T(8,128)(2,1)}, u32[]{:S(2)}, u32[]{:S(2)}) %all-to-all-start.1) | async-done | bytes 1572896 | tf_op jit(solution)/shard_map/all_to_all | solution.py:82
  351.3 3.1 fusion.40
  (141 shorter events, 7.3 us)
Async XLA Ops:
  6.5 12.4 %copy-start = (bf16[2048,768]{1,0:T(8,128)(2,1)S(1)}, bf16[2048,768]{1,0:T(8,128)(2,1)}, u32[]{:S(2)}) copy-start(bf16[2048,768]{1,0:T(8,128)(2,1)} %param.20) | copy-start | bytes 9437188
  6.5 12.4 %copy-start.16 = (f32[2048]{0:T(1024)S(1)}, f32[2048]{0:T(1024)}, u32[]{:S(2)}) copy-start(f32[2048]{0:T(1024)} %param.19) | copy-start | bytes 24580
  6.5 9.9 %copy-start.17 = (s32[4,3,8]{2,0,1:T(4,128)S(1)}, s32[4,3,8]{2,0,1:T(4,128)}, u32[]{:S(2)}) copy-start(s32[4,3,8]{2,0,1:T(4,128)} %param.33) | copy-start | bytes 1156
  6.5 11.5 %copy-start.23 = (s32[4]{0:T(128)S(1)}, s32[4]{0:T(128)}, u32[]{:S(2)}) copy-start(s32[4]{0:T(128)} %param.32) | copy-start | bytes 52
  6.5 217.9 %all-gather.4.cloned.1.call-start = ((), (), s32[]{:S(2)}) async-start(), calls=%async_computation.2 | async-start | bytes 7864320 | tf_op jit(solution)/shard_map/all_gather | solution.py:255
  8.0 10.3 %copy-start.22 = (f32[128]{0:T(128)}, f32[128]{0:T(128)S(1)}, u32[]{:S(2)}) copy-start(f32[128]{0:T(128)S(1)} %add_rsqrt_fusion.1) | copy-start | bytes 1540
  10.3 16.4 %collective-permute-start = (f32[128,144]{0,1:T(8,128)}, f32[128,144]{0,1:T(8,128)}, u32[]{:S(2)}, u32[]{:S(2)}) collective-permute-start(f32[128,144]{0,1:T(8,128)} %fusion.70), channel_id=1, source_target_pairs={{0,3},{1,0},{2,1},{3,2},{4,7},{5,4},{6,5},{7,6},{8,11},{9,8},{10,9... | collective-permute-start | bytes 221192 | tf_op jit(solution)/shard_map/ppermute | solution.py:60
  13.6 14.0 %collective-permute-start.1 = (f32[128,144]{0,1:T(8,128)}, f32[128,144]{0,1:T(8,128)}, u32[]{:S(2)}, u32[]{:S(2)}) collective-permute-start(f32[128,144]{0,1:T(8,128)} %fusion.70), channel_id=1, source_target_pairs={{0,2},{1,3},{2,0},{3,1},{4,6},{5,7},{6,4},{7,5},{8,10},{9,11},{10,... | collective-permute-start | bytes 221192 | tf_op jit(solution)/shard_map/ppermute | solution.py:60
  14.1 14.4 %collective-permute-start.2 = (f32[128,144]{0,1:T(8,128)}, f32[128,144]{0,1:T(8,128)}, u32[]{:S(2)}, u32[]{:S(2)}) collective-permute-start(f32[128,144]{0,1:T(8,128)} %fusion.70), channel_id=1, source_target_pairs={{0,1},{1,2},{2,3},{3,0},{4,5},{5,6},{6,7},{7,4},{8,9},{9,10},{10,1... | collective-permute-start | bytes 221192 | tf_op jit(solution)/shard_map/ppermute | solution.py:60
  21.3 1.7 copy-start.20
  21.3 2.1 copy-start.8
  21.4 5.2 %copy-start.24 = (s32[4]{0:T(128)S(1)}, s32[4]{0:T(128)}, u32[]{:S(2)}) copy-start(s32[4]{0:T(128)} %param.32) | copy-start | bytes 52
  23.1 10.8 %copy-start.19 = (f32[512]{0:T(512)S(1)}, f32[512]{0:T(512)}, u32[]{:S(2)}) copy-start(f32[512]{0:T(512)} %param.22) | copy-start | bytes 6148
  23.4 10.8 %copy-start.21 = (f32[128]{0:T(128)S(1)}, f32[128]{0:T(128)}, u32[]{:S(2)}) copy-start(f32[128]{0:T(128)} %mul.197) | copy-start | bytes 1540
  23.4 10.8 %copy-start.25 = (f32[32]{0:T(128)S(1)}, f32[32]{0:T(128)}, u32[]{:S(2)}) copy-start(f32[32]{0:T(128)} %multiply_power_fusion) | copy-start | bytes 388
  35.8 2.9 copy-start.14
  43.2 2.2 copy-start.3
  45.4 2.3 copy-start.6
  47.6 2.8 copy-start.4
  47.7 7.1 %copy-start.5 = (bf16[512,2048]{1,0:T(8,128)(2,1)S(1)}, bf16[512,2048]{1,0:T(8,128)(2,1)}, u32[]{:S(2)}) copy-start(bf16[512,2048]{1,0:T(8,128)(2,1)} %param.25) | copy-start | bytes 6291460
  48.8 18.0 %collective-permute-start.6 = (bf16[1,352,512]{2,1,0:T(8,128)(2,1)}, bf16[1,352,512]{2,1,0:T(8,128)(2,1)}, u32[]{:S(2)}, u32[]{:S(2)}) collective-permute-start(bf16[1,352,512]{2,1,0:T(8,128)(2,1)} %get-tuple-element.44), channel_id=1, source_target_pairs={{0,1},{1,2},{2,3},{3,0},{4,5},{5,6},{6,7},{7,4},{8,9},{9,10},{10,1... | collective-permute-start | bytes 1081352 | tf_op jit(solution)/shard_map/ppermute | solution.py:74
  50.7 14.5 %copy-start.2 = (bf16[128,2048]{1,0:T(8,128)(2,1)S(1)}, bf16[128,2048]{1,0:T(8,128)(2,1)}, u32[]{:S(2)}) copy-start(bf16[128,2048]{1,0:T(8,128)(2,1)} %param.18) | copy-start | bytes 1572868
  50.7 17.7 %copy-start.15 = (s32[128,6]{0,1:T(8,128)S(1)}, s32[128,6]{0,1:T(8,128)}, u32[]{:S(2)}) copy-start(s32[128,6]{0,1:T(8,128)} %param.34) | copy-start | bytes 9220
  50.7 10.9 %collective-permute-start.3 = (bf16[128,512]{0,1:T(8,128)(2,1)S(1)}, bf16[128,512]{0,1:T(8,128)(2,1)S(1)}, u32[]{:S(2)}, u32[]{:S(2)}) collective-permute-start(bf16[128,512]{0,1:T(8,128)(2,1)S(1)} %bitcast.199), channel_id=1, source_target_pairs={{0,1},{1,2},{2,3},{3,0},{4,5},{5,6},{6,7},{7,4},{8,9},{9,10},{10,1... | collective-permute-start | bytes 393224 | tf_op jit(solution)/shard_map/ppermute | solution.py:60
  50.8 13.8 %collective-permute-start.4 = (bf16[128,512]{0,1:T(8,128)(2,1)S(1)}, bf16[128,512]{0,1:T(8,128)(2,1)S(1)}, u32[]{:S(2)}, u32[]{:S(2)}) collective-permute-start(bf16[128,512]{0,1:T(8,128)(2,1)S(1)} %bitcast.200), channel_id=1, source_target_pairs={{0,2},{1,3},{2,0},{3,1},{4,6},{5,7},{6,4},{7,5},{8,10},{9,11},{10,... | collective-permute-start | bytes 393224 | tf_op jit(solution)/shard_map/ppermute | solution.py:60
  53.1 12.4 %collective-permute-start.5 = (bf16[128,512]{0,1:T(8,128)(2,1)S(1)}, bf16[128,512]{0,1:T(8,128)(2,1)}, u32[]{:S(2)}, u32[]{:S(2)}) collective-permute-start(bf16[128,512]{0,1:T(8,128)(2,1)S(1)} %bitcast.201), channel_id=1, source_target_pairs={{0,3},{1,0},{2,1},{3,2},{4,7},{5,4},{6,5},{7,6},{8,11},{9,8},{10,9... | collective-permute-start | bytes 393224 | tf_op jit(solution)/shard_map/ppermute | solution.py:60
  56.2 41.7 %copy-start.9 = (bf16[512,512]{1,0:T(8,128)(2,1)S(1)}, bf16[512,512]{1,0:T(8,128)(2,1)}, u32[]{:S(2)}) copy-start(bf16[512,512]{1,0:T(8,128)(2,1)} %get-tuple-element.21) | copy-start | bytes 1572868
  56.2 41.7 %collective-permute-start.10 = (bf16[512,512]{1,0:T(8,128)(2,1)}, bf16[512,512]{1,0:T(8,128)(2,1)}, u32[]{:S(2)}, u32[]{:S(2)}) collective-permute-start(bf16[512,512]{1,0:T(8,128)(2,1)} %get-tuple-element.39), channel_id=1, source_target_pairs={{0,2},{1,3},{2,0},{3,1},{4,6},{5,7},{6,4},{7,5},{8,10},{9,11},{10,... | collective-permute-start | bytes 1572872 | tf_op jit(solution)/shard_map/ppermute | solution.py:74
  61.6 3.1 copy-start.12
  61.6 36.3 %collective-permute-start.11 = (bf16[512,512]{1,0:T(8,128)(2,1)}, bf16[512,512]{1,0:T(8,128)(2,1)}, u32[]{:S(2)}, u32[]{:S(2)}) collective-permute-start(bf16[512,512]{1,0:T(8,128)(2,1)} %get-tuple-element.38), channel_id=1, source_target_pairs={{0,3},{1,0},{2,1},{3,2},{4,7},{5,4},{6,5},{7,6},{8,11},{9,8},{10,9... | collective-permute-start | bytes 1572872 | tf_op jit(solution)/shard_map/ppermute | solution.py:74
  64.6 0.7 copy-start.13
  64.6 33.3 %collective-permute-start.9 = (bf16[512,512]{1,0:T(8,128)(2,1)}, bf16[512,512]{1,0:T(8,128)(2,1)}, u32[]{:S(2)}, u32[]{:S(2)}) collective-permute-start(bf16[512,512]{1,0:T(8,128)(2,1)} %get-tuple-element.40), channel_id=1, source_target_pairs={{0,1},{1,2},{2,3},{3,0},{4,5},{5,6},{6,7},{7,4},{8,9},{9,10},{10,1... | collective-permute-start | bytes 1572872 | tf_op jit(solution)/shard_map/ppermute | solution.py:74
  65.5 29.6 %collective-permute-start.7 = (bf16[1,352,512]{2,1,0:T(8,128)(2,1)}, bf16[1,352,512]{2,1,0:T(8,128)(2,1)S(1)}, u32[]{:S(2)}, u32[]{:S(2)}) collective-permute-start(bf16[1,352,512]{2,1,0:T(8,128)(2,1)} %get-tuple-element.43), channel_id=1, source_target_pairs={{0,2},{1,3},{2,0},{3,1},{4,6},{5,7},{6,4},{7,5},{8,10},{9,11},{10,... | collective-permute-start | bytes 1081352 | tf_op jit(solution)/shard_map/ppermute | solution.py:74
  66.8 31.0 %collective-permute-start.8 = (bf16[1,352,512]{2,1,0:T(8,128)(2,1)}, bf16[1,352,512]{2,1,0:T(8,128)(2,1)S(1)}, u32[]{:S(2)}, u32[]{:S(2)}) collective-permute-start(bf16[1,352,512]{2,1,0:T(8,128)(2,1)} %get-tuple-element.42), channel_id=1, source_target_pairs={{0,3},{1,0},{2,1},{3,2},{4,7},{5,4},{6,5},{7,6},{8,11},{9,8},{10,9... | collective-permute-start | bytes 1081352 | tf_op jit(solution)/shard_map/ppermute | solution.py:74
  97.9 2.1 copy-start.10
  99.9 6.0 %collective-permute-start.12 = (f32[128,1]{0,1:T(1,128)S(1)}, f32[128,1]{0,1:T(1,128)S(1)}, u32[]{:S(2)}, u32[]{:S(2)}) collective-permute-start(f32[128,1]{0,1:T(1,128)S(1)} %bitcast.215), channel_id=1, source_target_pairs={{0,1},{1,2},{2,3},{3,0},{4,5},{5,6},{6,7},{7,4},{8,9},{9,10},{10,1... | collective-permute-start | bytes 1544 | tf_op jit(solution)/shard_map/ppermute | solution.py:60
  102.0 3.9 %collective-permute-start.13 = (f32[128,1]{0,1:T(1,128)S(1)}, f32[128,1]{0,1:T(1,128)S(1)}, u32[]{:S(2)}, u32[]{:S(2)}) collective-permute-start(f32[128,1]{0,1:T(1,128)S(1)} %bitcast.216), channel_id=1, source_target_pairs={{0,2},{1,3},{2,0},{3,1},{4,6},{5,7},{6,4},{7,5},{8,10},{9,11},{10,... | collective-permute-start | bytes 1544 | tf_op jit(solution)/shard_map/ppermute | solution.py:60
  104.5 2.4 collective-permute-start.14
  160.3 70.3 %copy-start.27 = (bf16[1,2048,352]{1,2,0:T(8,128)(2,1)S(1)}, bf16[1,2048,352]{1,2,0:T(8,128)(2,1)}, u32[]{:S(2)}) copy-start(bf16[1,2048,352]{1,2,0:T(8,128)(2,1)} %param.28) | copy-start | bytes 4325380
  160.3 131.2 %all-gather.6.cloned.1.call-start = ((), (), s32[]{:S(2)}) async-start(), calls=%async_computation.3 | async-start | bytes 5898240 | tf_op jit(solution)/shard_map/all_gather | solution.py:40
  224.4 6.1 %copy-start.26 = (bf16[64,1,24,2048]{3,2,0,1:T(8,128)(2,1)S(1)}, bf16[64,1,24,2048]{3,2,0,1:T(8,128)(2,1)}, u32[]{:S(2)}) copy-start(bf16[64,1,24,2048]{3,2,0,1:T(8,128)(2,1)} %all-gather.4.cloned.1.call-done) | copy-start | bytes 18874372
  294.3 2.0 copy-start.7
  297.3 1.0 copy-start.11
  301.4 11.0 %copy-start.18 = (f32[128,6]{0,1:T(8,128)S(1)}, f32[128,6]{0,1:T(8,128)}, u32[]{:S(2)}) copy-start(f32[128,6]{0,1:T(8,128)} %param.35) | copy-start | bytes 9220
  301.4 49.9 %all-to-all-start.1 = ((bf16[64,1,24,512]{3,2,1,0:T(8,128)(2,1)}), bf16[64,1,24,512]{3,2,1,0:T(8,128)(2,1)}, u32[]{:S(2)}, u32[]{:S(2)}) async-start(bf16[64,1,24,512]{3,2,1,0:T(8,128)(2,1)} %copy.211), calls=%async_computation.1 | async-start | bytes 3145728 | tf_op jit(solution)/shard_map/all_to_all | solution.py:82
  312.4 42.0 %copy-start.1 = (bf16[2048,768]{1,0:T(8,128)(2,1)S(1)}, bf16[2048,768]{1,0:T(8,128)(2,1)}, u32[]{:S(2)}) copy-start(bf16[2048,768]{1,0:T(8,128)(2,1)} %param.20) | copy-start | bytes 9437188
Sparse Core Ops, SparseCore 0:
  160.4 64.0 all-gather.3
  235.5 55.8 all-gather.5

commit v11 on v10

--- a/solution.py
+++ b/solution.py
@@ -62,20 +62,28 @@
     return pieces
 
 
-def by_columns(weight):
+def by_columns(down_w, out_w):
     tp_count = lax.axis_size("tp")
     tp_index = lax.axis_index("tp")
-    col_share = weight.shape[-1] // tp_count
-    pieces = [None] * tp_count
+    col_share = out_w.shape[-1] // tp_count
+    down_rows = down_w.shape[1]
+    down_pieces, out_pieces = [], []
     for shift in range(tp_count):
-        target = (tp_index + shift) % tp_count
-        piece = lax.dynamic_slice_in_dim(weight, target * col_share, col_share, weight.ndim - 1)
+        start = ((tp_index + shift) % tp_count) * col_share
+        piece = jnp.concatenate(
+            [
+                lax.dynamic_slice_in_dim(down_w[0], start, col_share, 1),
+                lax.dynamic_slice_in_dim(out_w, start, col_share, 1),
+            ],
+            axis=0,
+        )
         if shift:
             piece = lax.ppermute(
                 piece, "tp", [(s, (s + shift) % tp_count) for s in range(tp_count)]
             )
-        pieces[shift] = piece
-    return pieces
+        down_pieces.append(piece[None, :down_rows])
+        out_pieces.append(piece[down_rows:])
+    return down_pieces, out_pieces
 
 
 def send_home(shares):
@@ -112,6 +120,7 @@
     max_len = PAGES * PAGE
     hidden_f = hidden_in.astype(jnp.float32)
     normed = (hidden_f * rms_scale(hidden_f) * attn_gain).astype(jnp.bfloat16)
+    normed, down_late, out_late = lax.optimization_barrier((normed, w_down, w_out))
     positions = (
         cache_len.astype(jnp.float32)[:, None, None]
         + jnp.arange(STEPS, dtype=jnp.float32)[None, :, None]
@@ -136,7 +145,6 @@
         tp_count * kv_part.shape[1],
         1,
     )
-    kv_all, down_late, out_late = lax.optimization_barrier((kv_all, w_down, w_out))
     new_lat = kv_all[:, :LATENT] * rms_scale(kv_all[:, :LATENT]) * kv_gain
     new_rope = rotate(kv_all[:, LATENT:], cos_val, sin_val)
     new_keys = jnp.concatenate([new_lat, new_rope], axis=1).astype(jnp.bfloat16)
@@ -231,7 +239,7 @@
     col_start = tp_index * col_share
     head_shift = jnp.concatenate(tp_shifted(head_out), axis=1)
     head_shift, down_pieces, out_pieces = lax.optimization_barrier(
-        (head_shift, by_columns(down_late), by_columns(out_late))
+        (head_shift,) + by_columns(down_late, out_late)
     )
     attn_cols = jnp.dot(
         head_shift, jnp.concatenate(out_pieces, axis=0), preferred_element_type=jnp.float32

time: 365 us -> 342 us (0.937)
  waiting for transfers between devices: 193 us -> 168 us
  starting transfers between devices: 31.1 us -> 24.3 us
  local copies, waits for them, and re-layouts: 24.6 us -> 31.4 us
    ppermute x6 -> x3, waiting for transfers between devices: 28.4 us -> 0.01 us  [by_columns(): lax.ppermute(piece, 'tp', [(s, (s + shift) % tp_count) for s in range(tp_...]
    ppermute x9, starting transfers between devices: 13.3 us -> 8.87 us  [tp_shifted(): lax.ppermute(values, 'tp', [(s, (s + shift) % tp_count) for s in range(tp...]
    ppermute x9, waiting for transfers between devices: 7.25 us -> 11.5 us  [tp_shifted(): lax.ppermute(values, 'tp', [(s, (s + shift) % tp_count) for s in range(tp...]
    broadcast_in_dim x0 -> x3, local copies, waits for them, and re-layouts: none -> 3.81 us  [by_columns(): down_pieces.append(piece[None, :down_rows])]
    unnamed x66 -> x58, local copies, waits for them, and re-layouts: 7.92 us -> 7.49 us
  transfers between devices with their start and end apart: 18 -> 15, of which waited for: 8 -> 8; matrix products, arithmetic and copies ran while one was open for 5% -> 13% of each run, Pallas kernels for 0% -> 0%
where the time goes in v11:
time: 342 us; the launch traced here: 340 us
  waiting for transfers between devices  168 us (49%)
  blocking collectives  55.9 us (16%)
  matrix products  34 us (10%)
  local copies, waits for them, and re-layouts  31.4 us (9%)
  starting transfers between devices  24.3 us (7%)
  between operations  14.2 us (4%)
  other arithmetic  13 us (4%)
    all_gather x1, waiting for transfers between devices, local(): arrived = lax.all_gather(arrived_cols, 'tp', axis=3, tiled=True)  62.8 us
    all_gather x1, waiting for transfers between devices, expert_math(): active_all = lax.all_gather(active, 'tp', axis=0)  56 us
    all_to_all x1, blocking collectives, local(): lax.all_to_all(placed.reshape(req_count, EXP_DEV, capacity, col_share), '...  55.9 us
    all_to_all x1, waiting for transfers between devices, send_home(): lax.all_to_all(shares, 'req', split_axis=0, concat_axis=0, tiled=True)  37.4 us
    ppermute x9, waiting for transfers between devices, tp_shifted(): lax.ppermute(values, 'tp', [(s, (s + shift) % tp_count) for s in range(tp...  11.5 us
    all_to_all x1, starting transfers between devices, send_home(): lax.all_to_all(shares, 'req', split_axis=0, concat_axis=0, tiled=True)  11 us
    ppermute x9, starting transfers between devices, tp_shifted(): lax.ppermute(values, 'tp', [(s, (s + shift) % tp_count) for s in range(tp...  8.87 us
    unnamed x58, local copies, waits for them, and re-layouts  7.49 us
  transfers between devices with their start and end apart: 15, of which 8 were waited for; matrix products, arithmetic and copies ran while one was open for 13% of the time, Pallas kernels for 0%

profile of v11, /device:TPU:1, one launch (start us, length us, event | category | flops | bytes accessed | tf_op | source)
XLA Modules:
  0.0 340.5 jit_solution(7288955099298715798)
XLA Ops:
  6.5 1.4 multiply_reduce_fusion
  7.9 1.3 multiply_convert_fusion
  9.2 0.8 copy-done.3
  10.0 2.0 fusion.81
  12.0 3.3 collective-permute-start
  16.4 2.8 constant_dynamic-slice_fusion.4
  19.2 1.0 dynamic-slice_bitcast_fusion
  20.2 1.0 pad_maximum_fusion
  21.2 1.5 collective-permute-start.6
  22.7 1.0 pad_maximum_fusion.1
  23.7 1.7 collective-permute-start.7
  25.7 2.4 fusion.80
  28.4 1.5 fusion.32
  31.3 1.0 copy.218
  32.6 1.8 reduce-window.6
  34.5 1.0 pad_maximum_fusion.2
  35.5 0.9 collective-permute-start.8
  36.4 0.9 constant_dynamic-update-slice_fusion.7
  37.3 0.9 constant_dynamic-update-slice_fusion.6
  38.2 0.9 constant_dynamic-update-slice_fusion.5
  39.1 0.9 constant_dynamic-update-slice_fusion.4
  40.0 0.9 constant_dynamic-update-slice_fusion.3
  40.9 0.9 constant_dynamic-update-slice_fusion.2
  41.7 0.9 constant_dynamic-update-slice_fusion.1
  42.6 0.9 constant_dynamic-update-slice_fusion
  45.0 2.8 fusion.78
  48.0 1.1 multiply_convert_fusion.2
  49.9 0.8 slice.91
  50.7 1.0 fusion.79
  52.2 1.3 reshape.312
  54.2 1.9 fusion.49
  56.1 2.2 fusion.30
  58.6 0.9 collective-permute-start.3
  60.4 1.3 collective-permute-start.4
  61.7 4.2 %collective-permute-done.3 = bf16[128,512]{0,1:T(8,128)(2,1)S(1)} collective-permute-done((bf16[128,512]{0,1:T(8,128)(2,1)S(1)}, bf16[128,512]{0,1:T(8,128)(2,1)S(1)}, u32[]{:S(2)}, u32[]{:S(2)}) %collective-permute-start.3) | collective-permute-done | bytes 131104 | tf_op jit(solution)/shard_map/ppermute | solution.py:60
  65.9 1.5 collective-permute-done.4
  67.4 3.7 %collective-permute-done.5 = bf16[128,512]{0,1:T(8,128)(2,1)S(1)} collective-permute-done((bf16[128,512]{0,1:T(8,128)(2,1)S(1)}, bf16[128,512]{0,1:T(8,128)(2,1)S(1)}, u32[]{:S(2)}, u32[]{:S(2)}) %collective-permute-start.5) | collective-permute-done | bytes 131104 | tf_op jit(solution)/shard_map/ppermute | solution.py:60
  71.1 1.1 slice.96
  72.2 1.1 slice.97
  73.3 1.0 slice_bitcast_fusion.6
  74.4 1.0 slice_bitcast_fusion.7
  75.4 1.1 slice.95
  76.5 1.8 slice_bitcast_fusion.8
  78.3 0.9 multiply_reduce_fusion.1
  79.2 0.8 collective-permute-start.10
  80.0 1.4 collective-permute-start.11
  82.1 0.8 dynamic_slice.65
  83.1 1.8 collective-permute-done.9
  85.0 0.6 convolution_convert_fusion
  85.6 55.9 %all_to_all.10 = bf16[64,1,24,512]{3,2,1,0:T(8,128)(2,1)} all-to-all(bf16[64,1,24,512]{3,2,1,0:T(8,128)(2,1)S(1)} %bitcast.204), channel_id=1, replica_groups=mesh['req'=64,'tp'=4] {'req'}, dimensions={0} | all-to-all | bytes 3145728 | tf_op jit(solution)/shard_map/all_to_all | solution.py:256
  141.8 62.8 %all-gather.4.cloned.1.call-done = bf16[64,1,24,2048]{3,2,0,1:T(8,128)(2,1)} async-done(((bf16[64,1,24,512]{3,2,0,1:T(8,128)(2,1)}), bf16[64,1,24,2048]{3,2,0,1:T(8,128)(2,1)}) %all-gather.4.cloned.1.call-update) | async-done | bytes 6291472 | tf_op jit(solution)/shard_map/all_gather | solution.py:263
  204.6 6.1 %fusion.2 = f32[64,24,352]{2,1,0:T(8,128)S(1)} fusion(bf16[64,1,24,2048]{3,2,0,1:T(8,128)(2,1)} %all-gather.4.cloned.1.call-done, bf16[1,2048,352]{1,2,0:T(8,128)(2,1)} %param.27), kind=kOutput, calls=%fused_computation.2 | convolution fusion | flops 2214592512 | bytes 9895936 | tf_op jit(solution)/shard_map/nesd,edf->nesf/dot_general | solution.py:37
  210.8 4.8 %fusion.22 = bf16[64,1,24,352]{3,2,1,0:T(8,128)(2,1)} fusion(bf16[1,2048,352]{1,2,0:T(8,128)(2,1)S(1)} %copy-done.23, bf16[64,1,24,2048]{3,2,0,1:T(8,128)(2,1)S(1)} %copy-done.22, f32[64,24,352]{2,1,0:T(8,128)S(1)} %fusion.2), kind=kOutput, calls=%fused_computation.30 | convolution fusion | flops 2217836544 | bytes 10977280 | tf_op jit(solution)/shard_map/nesd,edf->nesf/dot_general | solution.py:38
  215.7 56.0 %all-gather.6.cloned.1.call-done = bf16[256,1,24,352]{3,2,1,0:T(8,128)(2,1)} async-done(((bf16[64,1,24,352]{3,2,1,0:T(8,128)(2,1)}), bf16[256,1,24,352]{3,2,1,0:T(8,128)(2,1)}) %all-gather.6.cloned.1.call-update) | async-done | bytes 4325392 | tf_op jit(solution)/shard_map/all_gather | solution.py:40
  271.6 2.9 constant_dynamic-slice_fusion
  274.5 1.0 fusion.34
  275.5 1.0 fusion.35
  276.5 1.0 fusion.33
  277.5 1.1 fusion.19
  278.6 2.0 copy.211
  280.6 11.0 %all-to-all-start.1 = ((bf16[64,1,24,512]{3,2,1,0:T(8,128)(2,1)}), bf16[64,1,24,512]{3,2,1,0:T(8,128)(2,1)}, u32[]{:S(2)}, u32[]{:S(2)}) async-start(bf16[64,1,24,512]{3,2,1,0:T(8,128)(2,1)} %copy.211), calls=%async_computation.1 | async-start | bytes 3145728 | tf_op jit(solution)/shard_map/all_to_all | solution.py:90
  291.6 1.5 select_reduce_fusion
  293.1 37.4 %all-to-all-done.1 = bf16[64,1,24,512]{3,2,1,0:T(8,128)(2,1)} async-done(((bf16[64,1,24,512]{3,2,1,0:T(8,128)(2,1)}), bf16[64,1,24,512]{3,2,1,0:T(8,128)(2,1)}, u32[]{:S(2)}, u32[]{:S(2)}) %all-to-all-start.1) | async-done | bytes 1572896 | tf_op jit(solution)/shard_map/all_to_all | solution.py:90
  330.5 3.1 fusion.40
  (136 shorter events, 9.4 us)
Async XLA Ops:
  6.5 19.2 %copy-start = (bf16[2048,768]{1,0:T(8,128)(2,1)S(1)}, bf16[2048,768]{1,0:T(8,128)(2,1)}, u32[]{:S(2)}) copy-start(bf16[2048,768]{1,0:T(8,128)(2,1)} %param.20) | copy-start | bytes 9437188
  6.5 198.1 %all-gather.4.cloned.1.call-start = ((), (), s32[]{:S(2)}) async-start(), calls=%async_computation.2 | async-start | bytes 7864320 | tf_op jit(solution)/shard_map/all_gather | solution.py:263
  9.2 0.8 copy-start.3
  12.0 23.5 %collective-permute-start = (f32[128,144]{0,1:T(8,128)}, f32[128,144]{0,1:T(8,128)}, u32[]{:S(2)}, u32[]{:S(2)}) collective-permute-start(f32[128,144]{0,1:T(8,128)} %fusion.81), channel_id=1, source_target_pairs={{0,3},{1,0},{2,1},{3,2},{4,7},{5,4},{6,5},{7,6},{8,11},{9,8},{10,9... | collective-permute-start | bytes 221192 | tf_op jit(solution)/shard_map/ppermute | solution.py:60
  15.3 22.0 %collective-permute-start.1 = (f32[128,144]{0,1:T(8,128)}, f32[128,144]{0,1:T(8,128)}, u32[]{:S(2)}, u32[]{:S(2)}) collective-permute-start(f32[128,144]{0,1:T(8,128)} %fusion.81), channel_id=1, source_target_pairs={{0,2},{1,3},{2,0},{3,1},{4,6},{5,7},{6,4},{7,5},{8,10},{9,11},{10,... | collective-permute-start | bytes 221192 | tf_op jit(solution)/shard_map/ppermute | solution.py:60
  15.8 22.4 %collective-permute-start.2 = (f32[128,144]{0,1:T(8,128)}, f32[128,144]{0,1:T(8,128)}, u32[]{:S(2)}, u32[]{:S(2)}) collective-permute-start(f32[128,144]{0,1:T(8,128)} %fusion.81), channel_id=1, source_target_pairs={{0,1},{1,2},{2,3},{3,0},{4,5},{5,6},{6,7},{7,4},{8,9},{9,10},{10,1... | collective-permute-start | bytes 221192 | tf_op jit(solution)/shard_map/ppermute | solution.py:60
  16.4 2.8 copy-start.8
  20.2 5.2 %copy-start.21 = (s32[4]{0:T(128)S(1)}, s32[4]{0:T(128)}, u32[]{:S(2)}) copy-start(s32[4]{0:T(128)} %param.32) | copy-start | bytes 52
  21.2 54.2 %collective-permute-start.6 = (bf16[864,512]{1,0:T(8,128)(2,1)}, bf16[864,512]{1,0:T(8,128)(2,1)}, u32[]{:S(2)}, u32[]{:S(2)}) collective-permute-start(bf16[864,512]{1,0:T(8,128)(2,1)} %pad_maximum_fusion), channel_id=1, source_target_pairs={{0,1},{1,2},{2,3},{3,0},{4,5},{5,6},{6,7},{7,4},{8,9},{9,10},{10,1... | collective-permute-start | bytes 2654216 | tf_op jit(solution)/shard_map/ppermute | solution.py:81
  23.7 47.4 %collective-permute-start.7 = (bf16[864,512]{1,0:T(8,128)(2,1)}, bf16[864,512]{1,0:T(8,128)(2,1)}, u32[]{:S(2)}, u32[]{:S(2)}) collective-permute-start(bf16[864,512]{1,0:T(8,128)(2,1)} %pad_maximum_fusion.1), channel_id=1, source_target_pairs={{0,2},{1,3},{2,0},{3,1},{4,6},{5,7},{6,4},{7,5},{8,10},{9,11},{10,... | collective-permute-start | bytes 2654216 | tf_op jit(solution)/shard_map/ppermute | solution.py:81
  28.1 1.9 copy-start.20
  28.1 2.2 copy-start.17
  28.1 3.2 copy-start.14
  28.1 4.2 %copy-start.16 = (s32[128,6]{0,1:T(8,128)S(1)}, s32[128,6]{0,1:T(8,128)}, u32[]{:S(2)}) copy-start(s32[128,6]{0,1:T(8,128)} %param.34) | copy-start | bytes 9220
  28.2 6.3 %copy-start.6 = (bf16[512,512]{1,0:T(8,128)(2,1)S(1)}, bf16[512,512]{1,0:T(8,128)(2,1)}, u32[]{:S(2)}) copy-start(bf16[512,512]{1,0:T(8,128)(2,1)} %get-tuple-element.39) | copy-start | bytes 1572868
  28.2 6.3 %copy-start.7 = (bf16[352,512]{1,0:T(8,128)(2,1)S(1)}, bf16[352,512]{1,0:T(8,128)(2,1)}, u32[]{:S(2)}) copy-start(bf16[352,512]{1,0:T(8,128)(2,1)} %get-tuple-element.42) | copy-start | bytes 1081348
  35.5 36.7 %collective-permute-start.8 = (bf16[864,512]{1,0:T(8,128)(2,1)}, bf16[864,512]{1,0:T(8,128)(2,1)}, u32[]{:S(2)}, u32[]{:S(2)}) collective-permute-start(bf16[864,512]{1,0:T(8,128)(2,1)} %pad_maximum_fusion.2), channel_id=1, source_target_pairs={{0,3},{1,0},{2,1},{3,2},{4,7},{5,4},{6,5},{7,6},{8,11},{9,8},{10,9... | collective-permute-start | bytes 2654216 | tf_op jit(solution)/shard_map/ppermute | solution.py:81
  43.5 1.5 copy-start.13
  45.0 3.0 copy-start.19
  53.9 2.2 copy-start.4
  56.0 2.3 copy-start.5
  58.2 1.5 copy-start.2
  58.6 7.3 %collective-permute-start.3 = (bf16[128,512]{0,1:T(8,128)(2,1)S(1)}, bf16[128,512]{0,1:T(8,128)(2,1)S(1)}, u32[]{:S(2)}, u32[]{:S(2)}) collective-permute-start(bf16[128,512]{0,1:T(8,128)(2,1)S(1)} %bitcast.213), channel_id=1, source_target_pairs={{0,1},{1,2},{2,3},{3,0},{4,5},{5,6},{6,7},{7,4},{8,9},{9,10},{10,1... | collective-permute-start | bytes 393224 | tf_op jit(solution)/shard_map/ppermute | solution.py:60
  60.4 7.0 %collective-permute-start.4 = (bf16[128,512]{0,1:T(8,128)(2,1)S(1)}, bf16[128,512]{0,1:T(8,128)(2,1)S(1)}, u32[]{:S(2)}, u32[]{:S(2)}) collective-permute-start(bf16[128,512]{0,1:T(8,128)(2,1)S(1)} %bitcast.214), channel_id=1, source_target_pairs={{0,2},{1,3},{2,0},{3,1},{4,6},{5,7},{6,4},{7,5},{8,10},{9,11},{10,... | collective-permute-start | bytes 393224 | tf_op jit(solution)/shard_map/ppermute | solution.py:60
  65.9 5.2 %collective-permute-start.5 = (bf16[128,512]{0,1:T(8,128)(2,1)S(1)}, bf16[128,512]{0,1:T(8,128)(2,1)S(1)}, u32[]{:S(2)}, u32[]{:S(2)}) collective-permute-start(bf16[128,512]{0,1:T(8,128)(2,1)S(1)} %bitcast.215), channel_id=1, source_target_pairs={{0,3},{1,0},{2,1},{3,2},{4,7},{5,4},{6,5},{7,6},{8,11},{9,8},{10,9... | collective-permute-start | bytes 393224 | tf_op jit(solution)/shard_map/ppermute | solution.py:60
  72.2 6.1 %copy-start.15 = (bf16[512,512]{1,0:T(8,128)(2,1)S(1)}, bf16[512,512]{1,0:T(8,128)(2,1)}, u32[]{:S(2)}) copy-start(bf16[512,512]{1,0:T(8,128)(2,1)} %get-tuple-element.21) | copy-start | bytes 1572868
  79.1 62.3 %copy-start.11 = (f32[128,512]{1,0:T(8,128)}, f32[128,512]{1,0:T(8,128)S(1)}, u32[]{:S(2)}) copy-start(f32[128,512]{1,0:T(8,128)S(1)} %get-tuple-element.66) | copy-start | bytes 786436
  79.2 4.0 %collective-permute-start.10 = (f32[128,1]{0,1:T(1,128)S(1)}, f32[128,1]{0,1:T(1,128)S(1)}, u32[]{:S(2)}, u32[]{:S(2)}) collective-permute-start(f32[128,1]{0,1:T(1,128)S(1)} %bitcast.229), channel_id=1, source_target_pairs={{0,2},{1,3},{2,0},{3,1},{4,6},{5,7},{6,4},{7,5},{8,10},{9,11},{10,... | collective-permute-start | bytes 1544 | tf_op jit(solution)/shard_map/ppermute | solution.py:60
  80.0 3.2 collective-permute-start.11
  81.4 3.6 %collective-permute-start.9 = (f32[128,1]{0,1:T(1,128)S(1)}, f32[128,1]{0,1:T(1,128)S(1)}, u32[]{:S(2)}, u32[]{:S(2)}) collective-permute-start(f32[128,1]{0,1:T(1,128)S(1)} %bitcast.231), channel_id=1, source_target_pairs={{0,1},{1,2},{2,3},{3,0},{4,5},{5,6},{6,7},{7,4},{8,9},{9,10},{10,1... | collective-permute-start | bytes 1544 | tf_op jit(solution)/shard_map/ppermute | solution.py:60
  141.5 69.2 %copy-start.23 = (bf16[1,2048,352]{1,2,0:T(8,128)(2,1)S(1)}, bf16[1,2048,352]{1,2,0:T(8,128)(2,1)}, u32[]{:S(2)}) copy-start(bf16[1,2048,352]{1,2,0:T(8,128)(2,1)} %param.28) | copy-start | bytes 4325380
  141.5 130.1 %all-gather.6.cloned.1.call-start = ((), (), s32[]{:S(2)}) async-start(), calls=%async_computation.3 | async-start | bytes 5898240 | tf_op jit(solution)/shard_map/all_gather | solution.py:40
  204.6 6.1 %copy-start.22 = (bf16[64,1,24,2048]{3,2,0,1:T(8,128)(2,1)S(1)}, bf16[64,1,24,2048]{3,2,0,1:T(8,128)(2,1)}, u32[]{:S(2)}) copy-start(bf16[64,1,24,2048]{3,2,0,1:T(8,128)(2,1)} %all-gather.4.cloned.1.call-done) | copy-start | bytes 18874372
  271.6 2.9 copy-start.10
  274.5 1.0 copy-start.9
  280.6 11.0 %copy-start.18 = (f32[128,6]{0,1:T(8,128)S(1)}, f32[128,6]{0,1:T(8,128)}, u32[]{:S(2)}) copy-start(f32[128,6]{0,1:T(8,128)} %param.35) | copy-start | bytes 9220
  280.6 49.9 %copy-start.12 = (f32[128,512]{1,0:T(8,128)S(1)}, f32[128,512]{1,0:T(8,128)}, u32[]{:S(2)}) copy-start(f32[128,512]{1,0:T(8,128)} %copy-done.11) | copy-start | bytes 786436
  280.6 49.9 %all-to-all-start.1 = ((bf16[64,1,24,512]{3,2,1,0:T(8,128)(2,1)}), bf16[64,1,24,512]{3,2,1,0:T(8,128)(2,1)}, u32[]{:S(2)}, u32[]{:S(2)}) async-start(bf16[64,1,24,512]{3,2,1,0:T(8,128)(2,1)} %copy.211), calls=%async_computation.1 | async-start | bytes 3145728 | tf_op jit(solution)/shard_map/all_to_all | solution.py:90
  291.6 42.0 %copy-start.1 = (bf16[2048,768]{1,0:T(8,128)(2,1)S(1)}, bf16[2048,768]{1,0:T(8,128)(2,1)}, u32[]{:S(2)}) copy-start(bf16[2048,768]{1,0:T(8,128)(2,1)} %param.20) | copy-start | bytes 9437188
Sparse Core Ops, SparseCore 0:
  141.6 62.9 all-gather.3
  215.7 55.8 all-gather.5

commit v12 on v11

--- a/solution.py
+++ b/solution.py
@@ -37,14 +37,8 @@
     gate_val = jnp.einsum("nesd,edf->nesf", arrived, gate_w, preferred_element_type=jnp.float32)
     up_val = jnp.einsum("nesd,edf->nesf", arrived, up_w, preferred_element_type=jnp.float32)
     active = (jax.nn.silu(gate_val) * up_val).astype(jnp.bfloat16)
-    active_all = lax.all_gather(active, "tp", axis=0)
-    tp_count = lax.axis_size("tp")
-    tp_index = lax.axis_index("tp")
     total = None
-    for shift in range(tp_count):
-        source = lax.dynamic_index_in_dim(
-            active_all, (tp_index - shift) % tp_count, 0, keepdims=False
-        )
+    for shift, source in enumerate(tp_shifted(active)):
         term = jnp.einsum(
             "nesf,efd->nesd", source, down_pieces[shift], preferred_element_type=jnp.float32
         )

time: 342 us -> 335 us (0.980)
  waiting for transfers between devices: 168 us -> 159 us
  starting transfers between devices: 24.3 us -> 30.6 us
    all_gather x1 -> x0, waiting for transfers between devices: 56 us -> none  [expert_math(): active_all = lax.all_gather(active, 'tp', axis=0)]
    ppermute x9 -> x12, waiting for transfers between devices: 11.5 us -> 58.3 us  [tp_shifted(): lax.ppermute(values, 'tp', [(s, (s + shift) % tp_count) for s in range(tp...]
    ppermute x9 -> x12, starting transfers between devices: 8.87 us -> 13.2 us  [tp_shifted(): lax.ppermute(values, 'tp', [(s, (s + shift) % tp_count) for s in range(tp...]
  transfers between devices with their start and end apart: 15 -> 17, of which waited for: 8 -> 10; matrix products, arithmetic and copies ran while one was open for 13% -> 15% of each run, Pallas kernels for 0% -> 0%
where the time goes in v12:
time: 335 us; the launch traced here: 334 us
  waiting for transfers between devices  159 us (47%)
  blocking collectives  55.9 us (17%)
  matrix products  32.9 us (10%)
  starting transfers between devices  30.6 us (9%)
  local copies, waits for them, and re-layouts  28.5 us (9%)
  between operations  14.1 us (4%)
  other arithmetic  13 us (4%)
    all_gather x1, waiting for transfers between devices, local(): arrived = lax.all_gather(arrived_cols, 'tp', axis=3, tiled=True)  63.1 us
    ppermute x12, waiting for transfers between devices, tp_shifted(): lax.ppermute(values, 'tp', [(s, (s + shift) % tp_count) for s in range(tp...  58.3 us
    all_to_all x1, blocking collectives, local(): lax.all_to_all(placed.reshape(req_count, EXP_DEV, capacity, col_share), '...  55.9 us
    all_to_all x1, waiting for transfers between devices, send_home(): lax.all_to_all(shares, 'req', split_axis=0, concat_axis=0, tiled=True)  37.4 us
    all_to_all x1, starting transfers between devices, send_home(): lax.all_to_all(shares, 'req', split_axis=0, concat_axis=0, tiled=True)  13.2 us
    ppermute x12, starting transfers between devices, tp_shifted(): lax.ppermute(values, 'tp', [(s, (s + shift) % tp_count) for s in range(tp...  13.2 us
    unnamed x58, local copies, waits for them, and re-layouts  7.49 us
  transfers between devices with their start and end apart: 17, of which 10 were waited for; matrix products, arithmetic and copies ran while one was open for 15% of the time, Pallas kernels for 0%

profile of v12, /device:TPU:1, one launch (start us, length us, event | category | flops | bytes accessed | tf_op | source)
XLA Modules:
  0.0 333.8 jit_solution(815698064198867251)
XLA Ops:
  6.5 1.4 multiply_reduce_fusion
  7.9 1.3 multiply_convert_fusion
  10.0 2.0 fusion.83
  12.0 3.3 collective-permute-start
  16.4 2.8 constant_dynamic-slice_fusion
  19.2 1.0 dynamic-slice_bitcast_fusion
  20.2 1.0 pad_maximum_fusion
  21.2 1.5 collective-permute-start.6
  22.7 1.0 pad_maximum_fusion.1
  23.7 1.7 collective-permute-start.7
  25.7 2.4 fusion.82
  28.4 1.5 fusion.27
  31.3 1.0 copy.215
  32.6 1.8 reduce-window.6
  34.5 1.0 pad_maximum_fusion.2
  35.5 0.9 collective-permute-start.8
  36.4 0.9 constant_dynamic-update-slice_fusion.7
  37.3 0.9 constant_dynamic-update-slice_fusion.6
  38.2 0.9 constant_dynamic-update-slice_fusion.5
  39.1 0.9 constant_dynamic-update-slice_fusion.4
  40.0 0.9 constant_dynamic-update-slice_fusion.3
  40.9 0.9 constant_dynamic-update-slice_fusion.2
  41.7 0.9 constant_dynamic-update-slice_fusion.1
  42.6 0.9 constant_dynamic-update-slice_fusion
  45.0 2.8 fusion.80
  48.0 1.1 multiply_convert_fusion.2
  49.9 0.8 slice.91
  50.7 1.0 fusion.81
  52.2 1.3 reshape.308
  54.2 1.9 fusion.51
  56.1 2.2 fusion.25
  58.6 0.9 collective-permute-start.3
  60.4 1.3 collective-permute-start.4
  61.7 4.2 %collective-permute-done.3 = bf16[128,512]{0,1:T(8,128)(2,1)S(1)} collective-permute-done((bf16[128,512]{0,1:T(8,128)(2,1)S(1)}, bf16[128,512]{0,1:T(8,128)(2,1)S(1)}, u32[]{:S(2)}, u32[]{:S(2)}) %collective-permute-start.3) | collective-permute-done | bytes 131104 | tf_op jit(solution)/shard_map/ppermute | solution.py:54
  65.9 1.5 collective-permute-done.4
  67.4 3.7 %collective-permute-done.5 = bf16[128,512]{0,1:T(8,128)(2,1)S(1)} collective-permute-done((bf16[128,512]{0,1:T(8,128)(2,1)S(1)}, bf16[128,512]{0,1:T(8,128)(2,1)S(1)}, u32[]{:S(2)}, u32[]{:S(2)}) %collective-permute-start.5) | collective-permute-done | bytes 131104 | tf_op jit(solution)/shard_map/ppermute | solution.py:54
  71.1 1.1 slice.96
  72.2 1.1 slice.97
  73.3 1.0 slice_bitcast_fusion.6
  74.4 1.0 slice_bitcast_fusion.7
  75.4 1.1 slice.95
  76.5 1.8 slice_bitcast_fusion.8
  78.3 0.9 multiply_reduce_fusion.1
  79.2 0.8 collective-permute-start.10
  80.0 1.4 collective-permute-start.11
  83.1 1.8 collective-permute-done.9
  85.6 55.9 %all_to_all.10 = bf16[64,1,24,512]{3,2,1,0:T(8,128)(2,1)} all-to-all(bf16[64,1,24,512]{3,2,1,0:T(8,128)(2,1)S(1)} %bitcast.185), channel_id=1, replica_groups=mesh['req'=64,'tp'=4] {'req'}, dimensions={0} | all-to-all | bytes 3145728 | tf_op jit(solution)/shard_map/all_to_all | solution.py:250
  141.5 63.1 %all-gather.2.cloned.1.call-done = bf16[64,1,24,2048]{3,2,0,1:T(8,128)(2,1)} async-done(((bf16[64,1,24,512]{3,2,0,1:T(8,128)(2,1)}), bf16[64,1,24,2048]{3,2,0,1:T(8,128)(2,1)}) %all-gather.2.cloned.1.call-update) | async-done | bytes 6291472 | tf_op jit(solution)/shard_map/all_gather | solution.py:257
  204.6 6.1 %fusion.2 = f32[64,24,352]{2,1,0:T(8,128)S(1)} fusion(bf16[64,1,24,2048]{3,2,0,1:T(8,128)(2,1)} %all-gather.2.cloned.1.call-done, bf16[1,2048,352]{1,2,0:T(8,128)(2,1)} %param.27), kind=kOutput, calls=%fused_computation.2 | convolution fusion | flops 2214592512 | bytes 9895936 | tf_op jit(solution)/shard_map/nesd,edf->nesf/dot_general | solution.py:37
  210.8 3.8 %fusion.4 = bf16[64,1,24,352]{3,2,0,1:T(8,128)(2,1)S(1)} fusion(f32[64,24,352]{2,1,0:T(8,128)S(1)} %fusion.2, bf16[64,1,24,2048]{3,2,0,1:T(8,128)(2,1)S(1)} %copy-done.22, bf16[1,2048,352]{1,2,0:T(8,128)(2,1)S(1)} %copy-done.23), kind=kOutput, calls=%fused_computation.10 | convolution fusion | flops 2217836544 | bytes 10977280 | tf_op jit(solution)/shard_map/nesd,edf->nesf/dot_general | solution.py:38
  214.5 1.0 collective-permute-start.12
  215.5 1.3 collective-permute-start.13
  216.9 2.0 collective-permute-start.14
  218.8 1.0 fusion.36
  219.8 23.4 %collective-permute-done.12 = bf16[64,1,24,352]{3,2,0,1:T(8,128)(2,1)S(1)} collective-permute-done((bf16[64,1,24,352]{3,2,0,1:T(8,128)(2,1)S(1)}, bf16[64,1,24,352]{3,2,0,1:T(8,128)(2,1)S(1)}, u32[]{:S(2)}, u32[]{:S(2)}) %collective-permute-start.12) | collective-permute-done | bytes 1081376 | tf_op jit(solution)/shard_map/ppermute | solution.py:54
  243.2 1.0 fusion.34
  244.2 23.3 %collective-permute-done.13 = bf16[64,1,24,352]{3,2,0,1:T(8,128)(2,1)S(1)} collective-permute-done((bf16[64,1,24,352]{3,2,0,1:T(8,128)(2,1)S(1)}, bf16[64,1,24,352]{3,2,0,1:T(8,128)(2,1)S(1)}, u32[]{:S(2)}, u32[]{:S(2)}) %collective-permute-start.13) | collective-permute-done | bytes 1081376 | tf_op jit(solution)/shard_map/ppermute | solution.py:54
  267.4 1.0 fusion.32
  268.6 1.1 fusion.19
  269.7 2.0 copy.208
  271.7 13.2 %all-to-all-start.1 = ((bf16[64,1,24,512]{3,2,1,0:T(8,128)(2,1)}), bf16[64,1,24,512]{3,2,1,0:T(8,128)(2,1)}, u32[]{:S(2)}, u32[]{:S(2)}) async-start(bf16[64,1,24,512]{3,2,1,0:T(8,128)(2,1)} %copy.208), calls=%async_computation.1 | async-start | bytes 3145728 | tf_op jit(solution)/shard_map/all_to_all | solution.py:84
  284.9 1.5 select_reduce_fusion
  286.5 37.4 %all-to-all-done.1 = bf16[64,1,24,512]{3,2,1,0:T(8,128)(2,1)} async-done(((bf16[64,1,24,512]{3,2,1,0:T(8,128)(2,1)}), bf16[64,1,24,512]{3,2,1,0:T(8,128)(2,1)}, u32[]{:S(2)}, u32[]{:S(2)}) %all-to-all-start.1) | async-done | bytes 1572896 | tf_op jit(solution)/shard_map/all_to_all | solution.py:84
  323.9 3.1 fusion.42
  (138 shorter events, 11.4 us)
Async XLA Ops:
  6.5 19.2 %copy-start = (bf16[2048,768]{1,0:T(8,128)(2,1)S(1)}, bf16[2048,768]{1,0:T(8,128)(2,1)}, u32[]{:S(2)}) copy-start(bf16[2048,768]{1,0:T(8,128)(2,1)} %param.20) | copy-start | bytes 9437188
  6.5 198.1 %all-gather.2.cloned.1.call-start = ((), (), s32[]{:S(2)}) async-start(), calls=%async_computation.2 | async-start | bytes 7864320 | tf_op jit(solution)/shard_map/all_gather | solution.py:257
  9.2 0.8 copy-start.3
  12.0 23.5 %collective-permute-start = (f32[128,144]{0,1:T(8,128)}, f32[128,144]{0,1:T(8,128)}, u32[]{:S(2)}, u32[]{:S(2)}) collective-permute-start(f32[128,144]{0,1:T(8,128)} %fusion.83), channel_id=1, source_target_pairs={{0,3},{1,0},{2,1},{3,2},{4,7},{5,4},{6,5},{7,6},{8,11},{9,8},{10,9... | collective-permute-start | bytes 221192 | tf_op jit(solution)/shard_map/ppermute | solution.py:54
  15.3 22.0 %collective-permute-start.1 = (f32[128,144]{0,1:T(8,128)}, f32[128,144]{0,1:T(8,128)}, u32[]{:S(2)}, u32[]{:S(2)}) collective-permute-start(f32[128,144]{0,1:T(8,128)} %fusion.83), channel_id=1, source_target_pairs={{0,2},{1,3},{2,0},{3,1},{4,6},{5,7},{6,4},{7,5},{8,10},{9,11},{10,... | collective-permute-start | bytes 221192 | tf_op jit(solution)/shard_map/ppermute | solution.py:54
  15.8 22.4 %collective-permute-start.2 = (f32[128,144]{0,1:T(8,128)}, f32[128,144]{0,1:T(8,128)}, u32[]{:S(2)}, u32[]{:S(2)}) collective-permute-start(f32[128,144]{0,1:T(8,128)} %fusion.83), channel_id=1, source_target_pairs={{0,1},{1,2},{2,3},{3,0},{4,5},{5,6},{6,7},{7,4},{8,9},{9,10},{10,1... | collective-permute-start | bytes 221192 | tf_op jit(solution)/shard_map/ppermute | solution.py:54
  16.4 2.8 copy-start.8
  20.2 5.2 %copy-start.21 = (s32[4]{0:T(128)S(1)}, s32[4]{0:T(128)}, u32[]{:S(2)}) copy-start(s32[4]{0:T(128)} %param.32) | copy-start | bytes 52
  21.2 54.2 %collective-permute-start.6 = (bf16[864,512]{1,0:T(8,128)(2,1)}, bf16[864,512]{1,0:T(8,128)(2,1)}, u32[]{:S(2)}, u32[]{:S(2)}) collective-permute-start(bf16[864,512]{1,0:T(8,128)(2,1)} %pad_maximum_fusion), channel_id=1, source_target_pairs={{0,1},{1,2},{2,3},{3,0},{4,5},{5,6},{6,7},{7,4},{8,9},{9,10},{10,1... | collective-permute-start | bytes 2654216 | tf_op jit(solution)/shard_map/ppermute | solution.py:75
  23.7 47.4 %collective-permute-start.7 = (bf16[864,512]{1,0:T(8,128)(2,1)}, bf16[864,512]{1,0:T(8,128)(2,1)}, u32[]{:S(2)}, u32[]{:S(2)}) collective-permute-start(bf16[864,512]{1,0:T(8,128)(2,1)} %pad_maximum_fusion.1), channel_id=1, source_target_pairs={{0,2},{1,3},{2,0},{3,1},{4,6},{5,7},{6,4},{7,5},{8,10},{9,11},{10,... | collective-permute-start | bytes 2654216 | tf_op jit(solution)/shard_map/ppermute | solution.py:75
  28.1 1.9 copy-start.20
  28.1 2.2 copy-start.17
  28.1 3.2 copy-start.14
  28.1 4.2 %copy-start.16 = (s32[128,6]{0,1:T(8,128)S(1)}, s32[128,6]{0,1:T(8,128)}, u32[]{:S(2)}) copy-start(s32[128,6]{0,1:T(8,128)} %param.34) | copy-start | bytes 9220
  28.2 6.3 %copy-start.6 = (bf16[512,512]{1,0:T(8,128)(2,1)S(1)}, bf16[512,512]{1,0:T(8,128)(2,1)}, u32[]{:S(2)}) copy-start(bf16[512,512]{1,0:T(8,128)(2,1)} %get-tuple-element.35) | copy-start | bytes 1572868
  28.2 6.3 %copy-start.7 = (bf16[352,512]{1,0:T(8,128)(2,1)S(1)}, bf16[352,512]{1,0:T(8,128)(2,1)}, u32[]{:S(2)}) copy-start(bf16[352,512]{1,0:T(8,128)(2,1)} %get-tuple-element.38) | copy-start | bytes 1081348
  35.5 36.7 %collective-permute-start.8 = (bf16[864,512]{1,0:T(8,128)(2,1)}, bf16[864,512]{1,0:T(8,128)(2,1)}, u32[]{:S(2)}, u32[]{:S(2)}) collective-permute-start(bf16[864,512]{1,0:T(8,128)(2,1)} %pad_maximum_fusion.2), channel_id=1, source_target_pairs={{0,3},{1,0},{2,1},{3,2},{4,7},{5,4},{6,5},{7,6},{8,11},{9,8},{10,9... | collective-permute-start | bytes 2654216 | tf_op jit(solution)/shard_map/ppermute | solution.py:75
  43.5 1.5 copy-start.13
  45.0 3.0 copy-start.19
  53.9 2.2 copy-start.4
  56.0 2.3 copy-start.5
  58.2 1.5 copy-start.2
  58.6 7.3 %collective-permute-start.3 = (bf16[128,512]{0,1:T(8,128)(2,1)S(1)}, bf16[128,512]{0,1:T(8,128)(2,1)S(1)}, u32[]{:S(2)}, u32[]{:S(2)}) collective-permute-start(bf16[128,512]{0,1:T(8,128)(2,1)S(1)} %bitcast.197), channel_id=1, source_target_pairs={{0,1},{1,2},{2,3},{3,0},{4,5},{5,6},{6,7},{7,4},{8,9},{9,10},{10,1... | collective-permute-start | bytes 393224 | tf_op jit(solution)/shard_map/ppermute | solution.py:54
  60.4 7.0 %collective-permute-start.4 = (bf16[128,512]{0,1:T(8,128)(2,1)S(1)}, bf16[128,512]{0,1:T(8,128)(2,1)S(1)}, u32[]{:S(2)}, u32[]{:S(2)}) collective-permute-start(bf16[128,512]{0,1:T(8,128)(2,1)S(1)} %bitcast.198), channel_id=1, source_target_pairs={{0,2},{1,3},{2,0},{3,1},{4,6},{5,7},{6,4},{7,5},{8,10},{9,11},{10,... | collective-permute-start | bytes 393224 | tf_op jit(solution)/shard_map/ppermute | solution.py:54
  65.9 5.2 %collective-permute-start.5 = (bf16[128,512]{0,1:T(8,128)(2,1)S(1)}, bf16[128,512]{0,1:T(8,128)(2,1)S(1)}, u32[]{:S(2)}, u32[]{:S(2)}) collective-permute-start(bf16[128,512]{0,1:T(8,128)(2,1)S(1)} %bitcast.199), channel_id=1, source_target_pairs={{0,3},{1,0},{2,1},{3,2},{4,7},{5,4},{6,5},{7,6},{8,11},{9,8},{10,9... | collective-permute-start | bytes 393224 | tf_op jit(solution)/shard_map/ppermute | solution.py:54
  72.2 6.1 %copy-start.15 = (bf16[512,512]{1,0:T(8,128)(2,1)S(1)}, bf16[512,512]{1,0:T(8,128)(2,1)}, u32[]{:S(2)}) copy-start(bf16[512,512]{1,0:T(8,128)(2,1)} %get-tuple-element.21) | copy-start | bytes 1572868
  79.1 62.3 %copy-start.11 = (f32[128,512]{1,0:T(8,128)}, f32[128,512]{1,0:T(8,128)S(1)}, u32[]{:S(2)}) copy-start(f32[128,512]{1,0:T(8,128)S(1)} %get-tuple-element.62) | copy-start | bytes 786436
  79.2 4.0 %collective-permute-start.10 = (f32[128,1]{0,1:T(1,128)S(1)}, f32[128,1]{0,1:T(1,128)S(1)}, u32[]{:S(2)}, u32[]{:S(2)}) collective-permute-start(f32[128,1]{0,1:T(1,128)S(1)} %bitcast.213), channel_id=1, source_target_pairs={{0,2},{1,3},{2,0},{3,1},{4,6},{5,7},{6,4},{7,5},{8,10},{9,11},{10,... | collective-permute-start | bytes 1544 | tf_op jit(solution)/shard_map/ppermute | solution.py:54
  80.0 3.2 collective-permute-start.11
  81.4 3.6 %collective-permute-start.9 = (f32[128,1]{0,1:T(1,128)S(1)}, f32[128,1]{0,1:T(1,128)S(1)}, u32[]{:S(2)}, u32[]{:S(2)}) collective-permute-start(f32[128,1]{0,1:T(1,128)S(1)} %bitcast.215), channel_id=1, source_target_pairs={{0,1},{1,2},{2,3},{3,0},{4,5},{5,6},{6,7},{7,4},{8,9},{9,10},{10,1... | collective-permute-start | bytes 1544 | tf_op jit(solution)/shard_map/ppermute | solution.py:54
  204.6 6.1 %copy-start.22 = (bf16[64,1,24,2048]{3,2,0,1:T(8,128)(2,1)S(1)}, bf16[64,1,24,2048]{3,2,0,1:T(8,128)(2,1)}, u32[]{:S(2)}) copy-start(bf16[64,1,24,2048]{3,2,0,1:T(8,128)(2,1)} %all-gather.2.cloned.1.call-done) | copy-start | bytes 18874372
  204.6 6.1 %copy-start.23 = (bf16[1,2048,352]{1,2,0:T(8,128)(2,1)S(1)}, bf16[1,2048,352]{1,2,0:T(8,128)(2,1)}, u32[]{:S(2)}) copy-start(bf16[1,2048,352]{1,2,0:T(8,128)(2,1)} %param.28) | copy-start | bytes 4325380
  210.8 8.1 %copy-start.9 = (bf16[1,352,512]{2,1,0:T(8,128)(2,1)S(1)}, bf16[1,352,512]{2,1,0:T(8,128)(2,1)}, u32[]{:S(2)}) copy-start(bf16[1,352,512]{2,1,0:T(8,128)(2,1)} %get-tuple-element.25) | copy-start | bytes 1081348
  214.5 28.7 %collective-permute-start.12 = (bf16[64,1,24,352]{3,2,0,1:T(8,128)(2,1)S(1)}, bf16[64,1,24,352]{3,2,0,1:T(8,128)(2,1)S(1)}, u32[]{:S(2)}, u32[]{:S(2)}) collective-permute-start(bf16[64,1,24,352]{3,2,0,1:T(8,128)(2,1)S(1)} %fusion.4), channel_id=1, source_target_pairs={{0,1},{1,2},{2,3},{3,0},{4,5},{5,6},{6,7},{7,4},{8,9},{9,10},{10,1... | collective-permute-start | bytes 3244040 | tf_op jit(solution)/shard_map/ppermute | solution.py:54
  215.5 51.9 %collective-permute-start.13 = (bf16[64,1,24,352]{3,2,0,1:T(8,128)(2,1)S(1)}, bf16[64,1,24,352]{3,2,0,1:T(8,128)(2,1)S(1)}, u32[]{:S(2)}, u32[]{:S(2)}) collective-permute-start(bf16[64,1,24,352]{3,2,0,1:T(8,128)(2,1)S(1)} %fusion.4), channel_id=1, source_target_pairs={{0,2},{1,3},{2,0},{3,1},{4,6},{5,7},{6,4},{7,5},{8,10},{9,11},{10,... | collective-permute-start | bytes 3244040 | tf_op jit(solution)/shard_map/ppermute | solution.py:54
  216.9 51.7 %collective-permute-start.14 = (bf16[64,1,24,352]{3,2,0,1:T(8,128)(2,1)S(1)}, bf16[64,1,24,352]{3,2,0,1:T(8,128)(2,1)S(1)}, u32[]{:S(2)}, u32[]{:S(2)}) collective-permute-start(bf16[64,1,24,352]{3,2,0,1:T(8,128)(2,1)S(1)} %fusion.4), channel_id=1, source_target_pairs={{0,3},{1,0},{2,1},{3,2},{4,7},{5,4},{6,5},{7,6},{8,11},{9,8},{10,9... | collective-permute-start | bytes 3244040 | tf_op jit(solution)/shard_map/ppermute | solution.py:54
  218.8 24.4 %copy-start.10 = (bf16[1,352,512]{2,1,0:T(8,128)(2,1)S(1)}, bf16[1,352,512]{2,1,0:T(8,128)(2,1)}, u32[]{:S(2)}) copy-start(bf16[1,352,512]{2,1,0:T(8,128)(2,1)} %slice_bitcast_fusion.8) | copy-start | bytes 1081348
  271.7 13.2 %copy-start.18 = (f32[128,6]{0,1:T(8,128)S(1)}, f32[128,6]{0,1:T(8,128)}, u32[]{:S(2)}) copy-start(f32[128,6]{0,1:T(8,128)} %param.35) | copy-start | bytes 9220
  271.7 52.2 %copy-start.12 = (f32[128,512]{1,0:T(8,128)S(1)}, f32[128,512]{1,0:T(8,128)}, u32[]{:S(2)}) copy-start(f32[128,512]{1,0:T(8,128)} %copy-done.11) | copy-start | bytes 786436
  271.7 52.2 %all-to-all-start.1 = ((bf16[64,1,24,512]{3,2,1,0:T(8,128)(2,1)}), bf16[64,1,24,512]{3,2,1,0:T(8,128)(2,1)}, u32[]{:S(2)}, u32[]{:S(2)}) async-start(bf16[64,1,24,512]{3,2,1,0:T(8,128)(2,1)} %copy.208), calls=%async_computation.1 | async-start | bytes 3145728 | tf_op jit(solution)/shard_map/all_to_all | solution.py:84
  284.9 42.0 %copy-start.1 = (bf16[2048,768]{1,0:T(8,128)(2,1)S(1)}, bf16[2048,768]{1,0:T(8,128)(2,1)}, u32[]{:S(2)}) copy-start(bf16[2048,768]{1,0:T(8,128)(2,1)} %param.20) | copy-start | bytes 9437188
Sparse Core Ops, SparseCore 0:
  141.6 62.9 all-gather.1
